TPU v7x, 512 devices: a whole 4x8x8 slice. The times are simulated.
512 devices in a mesh: nodes: 128 (over z, y, core), rep: 4 (over x).
Axes of the slice: x: 4, y: 8, z: 8, core: 2. Of those that a mesh axis runs over, the one named last changes fastest.
Arguments:
- memory: float32 [65536, 512], P('nodes'), may hold values from -16 to 16
- last_tick: int32 [65536], P('nodes'), may hold values from 0 to 499
- src_local: int32 [65536], P(('nodes', 'rep')), may hold values from 0 to 511
- dst_owner: int32 [65536, 1], P(('nodes', 'rep')), may hold values from 0 to 127; in each aligned block of 128 rows (0 to 127, 128 to 255, ...) at most 2 rows name the same one
- dst_local: int32 [65536], P(('nodes', 'rep')), may hold values from 0 to 511
- event_tick: int32 [65536], P(('nodes', 'rep')), may hold values from 500 to 999
- nbr_owner: int32 [65536, 16, 1], P(('nodes', 'rep')), may hold values from 0 to 127; in each aligned block of 2048 rows (0 to 2047, 2048 to 4095, ..., all dimensions but the last counted through in order) at most 32 rows name the same one
- nbr_local: int32 [65536, 16], P(('nodes', 'rep')), may hold values from 0 to 511
- nbr_tick: int32 [65536, 16], P(('nodes', 'rep')), may hold values from 0 to 499
- freq: float32 [128], replicated, may hold values from 0.002 to 0.5
- phase: float32 [128], replicated, may hold values from -3.140625 to 3.140625
- w_message: bfloat16 [1152, 512], replicated, may hold values from -0.1875 to 0.1875
- gru_input: float32 [3, 512, 512], P(None, None, 'rep'), may hold values from -0.5 to 0.5
- gru_hidden: float32 [3, 512, 512], P(None, None, 'rep'), may hold values from -0.25 to 0.25
- gru_bias: float32 [4, 512], P(None, 'rep'), may hold values from -3 to 3
- w_query: bfloat16 [512, 512], replicated, may hold values from -1 to 1
- w_keyval_mem: bfloat16 [512, 1024], replicated, may hold values from -0.25 to 0.25
- w_keyval_time: bfloat16 [128, 1024], replicated, may hold values from -0.5 to 0.5
Outputs:
- new_memory: float32 [65536, 512], P('nodes', 'rep')
- embed: bfloat16 [65536, 512], P(('nodes', 'rep'))
Inputs may be any that keep to these rules, and one draw needn't show every extreme that they name: `dst_owner`: on one device no owner is named by more than 2 events. `nbr_owner`: on one device no owner is named by more than 32 neighbour entries.
All inputs are finite; a program needn't handle non-finite values.
Results may differ from a plain program's by a relative error of at most 0.012.
The roundings to bfloat16 on the way count: a program that leaves them out, or rounds other values in their place, can miss the bound.
Values may be sent and summed in bfloat16 or wider, within the bound.
No kernel may reach another device: no remote copies, remote signals or barrier semaphores. Data moves between devices by JAX's collectives and lax.ppermute only.
A program may use at most 128 MiB of HBM per device.

v0:
```python
import math

import jax
import jax.numpy as jnp
from jax import lax
from jax.sharding import PartitionSpec as P

HEADS = 8
HEAD_DIM = 64


def encode(gaps, freq, phase):
    return jnp.cos(gaps[..., None] * freq + phase)


def place(owner, groups, capacity):
    onehot = (owner[:, None] == jnp.arange(groups, dtype=jnp.int32)[None, :]).astype(jnp.int32)
    before = jnp.cumsum(onehot, axis=0) - onehot
    return owner * capacity + jnp.sum(before * onehot, axis=1)


def message_pair(src_rows, dst_rows, src_time, dst_time, w_message):
    count = src_rows.shape[0]
    stacked = jnp.concatenate(
        [
            jnp.concatenate([src_rows, dst_rows, src_time], axis=1),
            jnp.concatenate([dst_rows, src_rows, dst_time], axis=1),
        ],
        axis=0,
    )
    messages = jax.nn.silu(jnp.dot(stacked, w_message, preferred_element_type=jnp.float32)).astype(
        jnp.bfloat16
    )
    return (messages[:count], messages[count:])


def on_device(
    memory,
    last_tick,
    src_local,
    dst_owner,
    dst_local,
    event_tick,
    nbr_owner,
    nbr_local,
    nbr_tick,
    freq,
    phase,
    w_message,
    gru_input,
    gru_hidden,
    gru_bias,
    w_query,
    w_keyval_mem,
    w_keyval_time,
):
    groups = lax.axis_size("nodes")
    events = src_local.shape[0]
    rows_here = memory.shape[0]
    width_m = memory.shape[1]
    neighbours = nbr_local.shape[1]
    msg_width = w_message.shape[1]
    dst_cap = max(2, 2 * events // groups)
    nbr_cap = 2 * events * neighbours // groups
    dst_slot = place(dst_owner[:, 0], groups, dst_cap)
    nbr_slot = place(nbr_owner.reshape(-1), groups, nbr_cap)
    dst_ids = (
        jnp.full((groups * dst_cap,), -1, jnp.int32)
        .at[dst_slot]
        .set(dst_local)
        .reshape(groups, dst_cap)
    )
    nbr_ids = (
        jnp.full((groups * nbr_cap,), -1, jnp.int32)
        .at[nbr_slot]
        .set(nbr_local.reshape(-1))
        .reshape(groups, nbr_cap)
    )
    mem_half = memory.astype(jnp.bfloat16)
    near_rows = mem_half[src_local]
    near_ticks = last_tick[src_local]
    ticks = event_tick.astype(jnp.float32)
    got_dst, got_nbr = (
        lax.all_to_all(dst_ids, "nodes", split_axis=0, concat_axis=0, tiled=True),
        lax.all_to_all(nbr_ids, "nodes", split_axis=0, concat_axis=0, tiled=True),
    )
    safe_dst = jnp.maximum(got_dst, 0)
    reply_rows, reply_ticks = (
        lax.all_to_all(mem_half[safe_dst], "nodes", split_axis=0, concat_axis=0, tiled=True),
        lax.all_to_all(last_tick[safe_dst], "nodes", split_axis=0, concat_axis=0, tiled=True),
    )
    far_rows = reply_rows.reshape(-1, width_m)[dst_slot]
    far_ticks = reply_ticks.reshape(-1)[dst_slot]
    src_time = encode(ticks - near_ticks.astype(jnp.float32), freq, phase).astype(jnp.bfloat16)
    dst_time = encode(ticks - far_ticks.astype(jnp.float32), freq, phase).astype(jnp.bfloat16)
    msg_src, msg_dst = message_pair(near_rows, far_rows, src_time, dst_time, w_message)
    outgoing = (
        jnp.zeros((groups * dst_cap, msg_width), jnp.bfloat16)
        .at[dst_slot]
        .set(msg_dst)
        .reshape(groups, dst_cap, msg_width)
    )
    incoming = lax.all_to_all(outgoing, "nodes", split_axis=0, concat_axis=0, tiled=True)
    far_msgs = incoming.reshape(-1, msg_width)
    row_ids = jnp.arange(rows_here, dtype=jnp.int32)[:, None]
    hit_far = (row_ids == got_dst.reshape(1, -1)).astype(jnp.bfloat16)
    hit_near = (row_ids == src_local[None, :]).astype(jnp.bfloat16)
    sums = jnp.dot(hit_near, msg_src, preferred_element_type=jnp.float32) + jnp.dot(
        hit_far, far_msgs, preferred_element_type=jnp.float32
    )
    counts = jnp.sum(hit_near.astype(jnp.float32), axis=1) + jnp.sum(
        hit_far.astype(jnp.float32), axis=1
    )
    sums, counts = lax.psum((sums, counts), "rep")
    unit_width = gru_bias.shape[1]
    start = lax.axis_index("rep") * unit_width
    state_part = lax.dynamic_slice_in_dim(memory, start, unit_width, 1)
    mean = sums / jnp.maximum(counts, 1.0)[:, None]
    highest = lax.Precision.HIGHEST
    a_parts = jnp.einsum("rk,gku->gru", mean, gru_input, precision=highest)
    b_parts = jnp.einsum("rk,gku->gru", memory, gru_hidden, precision=highest)
    update = jax.nn.sigmoid(a_parts[0] + b_parts[0] + gru_bias[0])
    reset = jax.nn.sigmoid(a_parts[1] + b_parts[1] + gru_bias[1])
    cand = jnp.tanh(a_parts[2] + gru_bias[2] + reset * (b_parts[2] + gru_bias[3]))
    fresh = (1.0 - update) * cand + update * state_part
    new_part = jnp.where((counts > 0.0)[:, None], fresh, state_part)
    updated = lax.all_gather(new_part.astype(jnp.bfloat16), "rep", axis=1, tiled=True)
    served = updated[jnp.maximum(got_nbr, 0)]
    returned = lax.all_to_all(served, "nodes", split_axis=0, concat_axis=0, tiled=True)
    fetched = returned.reshape(-1, updated.shape[1])[nbr_slot]
    kv_mem = jnp.dot(fetched, w_keyval_mem, preferred_element_type=jnp.float32).astype(jnp.bfloat16)
    kv_mem = lax.optimization_barrier(kv_mem).astype(jnp.float32)
    gaps = ticks[:, None] - nbr_tick.astype(jnp.float32)
    time_enc = encode(gaps, freq, phase).reshape(-1, freq.shape[0]).astype(jnp.bfloat16)
    kv_time = jnp.dot(time_enc, w_keyval_time, preferred_element_type=jnp.float32)
    keyval = (kv_mem + kv_time).reshape(events, neighbours, 2, HEADS, HEAD_DIM)
    query = jnp.dot(updated[src_local], w_query, preferred_element_type=jnp.float32).astype(
        jnp.bfloat16
    )
    query = lax.optimization_barrier(query).astype(jnp.float32).reshape(events, HEADS, HEAD_DIM)
    scores = jnp.einsum("ehd,ejhd->ehj", query, keyval[:, :, 0]) / math.sqrt(HEAD_DIM)
    weights = jax.nn.softmax(scores, axis=-1)
    mixed = jnp.einsum("ehj,ejhd->ehd", weights, keyval[:, :, 1])
    embed = mixed.reshape(events, HEADS * HEAD_DIM).astype(jnp.bfloat16)
    return (new_part, embed)


def solution(mesh):
    placed = (
        P("nodes", None),
        P("nodes"),
        P(("nodes", "rep")),
        P(("nodes", "rep"), None),
        P(("nodes", "rep")),
        P(("nodes", "rep")),
        P(("nodes", "rep"), None, None),
        P(("nodes", "rep"), None),
        P(("nodes", "rep"), None),
        P(),
        P(),
        P(),
        P(None, None, "rep"),
        P(None, None, "rep"),
        P(None, "rep"),
        P(),
        P(),
        P(),
    )
    return jax.shard_map(
        on_device,
        mesh=mesh,
        in_specs=placed,
        out_specs=(P("nodes", "rep"), P(("nodes", "rep"), None)),
        check_vma=False,
    )
```

profile of v0, /device:TPU:41, one launch (start us, length us, event | category | flops | bytes accessed | tf_op | source)
XLA Modules:
  0.0 390.3 jit_solution(18406961669935850036)
XLA Ops:
  7.2 0.8 fusion.62
  8.2 0.8 select_reduce_fusion
  9.7 1.1 scatter_custom_fusion
  10.8 0.8 all_to_all.27
  11.6 17.2 %all-to-all-start = ((s32[128,1,2]{2,1,0:T(1,128)}), s32[128,1,2]{2,1,0:T(1,128)S(1)}, u32[]{:S(2)}, u32[]{:S(2)}) async-start(s32[128,1,2]{2,1,0:T(1,128)} %bitcast.5), calls=%async_computation | async-start | bytes 131072 | tf_op jit(solution)/shard_map/all_to_all | solution.py:84
  28.8 0.7 broadcast_multiply_fusion
  29.5 0.8 copy.53
  32.7 4.2 %all-to-all-done = s32[128,1,2]{2,1,0:T(1,128)S(1)} async-done(((s32[128,1,2]{2,1,0:T(1,128)}), s32[128,1,2]{2,1,0:T(1,128)S(1)}, u32[]{:S(2)}, u32[]{:S(2)}) %all-to-all-start) | async-done | bytes 1056 | tf_op jit(solution)/shard_map/all_to_all | solution.py:84
  37.4 1.5 fusion.72
  39.1 1.9 gather_fusion.4
  41.0 0.8 all_to_all.30
  41.8 9.6 %all-to-all-start.2 = ((s32[128,1,2]{2,1,0:T(1,128)}), s32[128,1,2]{2,1,0:T(1,128)S(1)}, u32[]{:S(2)}, u32[]{:S(2)}) async-start(s32[128,1,2]{2,1,0:T(1,128)} %bitcast.6), calls=%async_computation.2 | async-start | bytes 131072 | tf_op jit(solution)/shard_map/all_to_all | solution.py:90
  51.4 1.3 gather_fusion.3
  53.2 0.8 gather_fusion
  54.0 1.2 gather_fusion.1
  55.2 0.8 reshape.151
  56.0 3.5 all-to-all-done.2
  59.5 10.2 %all-to-all-start.1 = ((bf16[128,2,512]{2,1,0:T(2,128)(2,1)}), bf16[128,2,512]{2,1,0:T(2,128)(2,1)S(1)}, u32[]{:S(2)}, u32[]{:S(2)}) async-start(bf16[128,2,512]{2,1,0:T(2,128)(2,1)} %reshape.151), calls=%async_computation.1 | async-start | bytes 524288 | tf_op jit(solution)/shard_map/all_to_all | solution.py:89
  69.7 0.8 reduce.18
  70.7 1.3 gather_fusion.5
  72.5 9.4 %all-to-all-done.1 = bf16[128,2,512]{2,1,0:T(2,128)(2,1)S(1)} async-done(((bf16[128,2,512]{2,1,0:T(2,128)(2,1)}), bf16[128,2,512]{2,1,0:T(2,128)(2,1)S(1)}, u32[]{:S(2)}, u32[]{:S(2)}) %all-to-all-start.1) | async-done | bytes 262176 | tf_op jit(solution)/shard_map/all_to_all | solution.py:89
  82.0 0.8 gather_fusion.2
  83.4 1.1 scatter_custom_fusion.1
  84.6 0.8 reshape.135
  85.4 8.8 %all-to-all-start.3 = ((bf16[128,2,512]{2,1,0:T(2,128)(2,1)}), bf16[128,2,512]{2,1,0:T(2,128)(2,1)S(1)}, u32[]{:S(2)}, u32[]{:S(2)}) async-start(bf16[128,2,512]{2,1,0:T(2,128)(2,1)} %reshape.135), calls=%async_computation.3 | async-start | bytes 524288 | tf_op jit(solution)/shard_map/all_to_all | solution.py:103
  94.3 8.1 %scatter_custom_fusion.2 = s32[4096]{0:T(1024)S(1)} fusion(s32[2048]{0:T(1024)S(1)} %bitcast.137, s32[2048]{0:T(1024)S(1)} %reshape.234, s32[]{:T(128)} %constant.15.clone.1), kind=kCustom, calls=%fused_computation.109 | custom fusion | bytes 16388 | tf_op jit(solution)/shard_map/scatter | solution.py:76
  103.0 3.0 convolution_bitcast_fusion
  106.0 1.0 eq.76
  107.0 14.2 %all-to-all-start.4 = ((s32[128,1,32]{2,1,0:T(1,128)}), s32[128,1,32]{2,1,0:T(1,128)}, u32[]{:S(2)}, u32[]{:S(2)}) async-start(s32[128,1,32]{2,1,0:T(1,128)} %bitcast.135), calls=%async_computation.4 | async-start | bytes 131072 | tf_op jit(solution)/shard_map/all_to_all | solution.py:85
  121.7 2.2 convolution_add_fusion
  124.3 8.7 %psum.14 = f32[512]{0:T(512)S(1)} all-reduce(f32[512]{0:T(512)S(1)} %add.150), channel_id=1, replica_groups=mesh['nodes'=128,'rep'=4] {'rep'}, use_global_device_ids=true, to_apply=%region_5.6 | all-reduce | flops 512 | bytes 4096 | tf_op jit(solution)/shard_map/psum | solution.py:114
  133.0 1.0 maximum_reduce_fusion
  134.1 46.1 %all-reduce.2.cloned.1.call-done = f32[512,512]{1,0:T(8,128)} async-done(((f32[512,512]{1,0:T(8,128)}), f32[512,512]{1,0:T(8,128)}) %all-reduce.2.cloned.1.call-update) | async-done | bytes 1048592 | tf_op jit(solution)/shard_map/psum | solution.py:114
  180.2 3.3 convolution_bitcast_fusion.1
  183.5 0.9 fusion.73
  184.4 11.5 %all_gather.3 = bf16[512,512]{1,0:T(8,128)(2,1)S(1)} all-gather(bf16[512,128]{1,0:T(8,128)(2,1)S(1)} %get-tuple-element.10), channel_id=1, replica_groups=mesh['nodes'=128,'rep'=4] {'rep'}, dimensions={1}, use_global_device_ids=true | all-gather | bytes 655360 | tf_op jit(solution)/shard_map/all_gather | solution.py:127
  196.0 17.3 %gather_fusion.7 = bf16[4096,512]{1,0:T(8,128)(2,1)} fusion(bf16[512,512]{1,0:T(8,128)(2,1)S(1)} %all_gather.3, s32[4096]{0:T(1024)S(1)} %broadcast_clamp_fusion), kind=kCustom, calls=%fused_computation.7 | custom fusion | bytes 8404992 | tf_op jit(solution)/shard_map/gather | solution.py:128
  213.3 19.2 %all-to-all-start.5 = ((bf16[128,32,512]{2,1,0:T(8,128)(2,1)}), bf16[128,32,512]{2,1,0:T(8,128)(2,1)}, u32[]{:S(2)}, u32[]{:S(2)}) async-start(bf16[128,32,512]{2,1,0:T(8,128)(2,1)} %bitcast.132), calls=%async_computation.5 | async-start | bytes 8388608 | tf_op jit(solution)/shard_map/all_to_all | solution.py:129
  232.8 1.0 gather_fusion.6
  234.1 1.0 copy.77
  235.1 101.1 %all-to-all-done.5 = bf16[128,32,512]{2,1,0:T(8,128)(2,1)} async-done(((bf16[128,32,512]{2,1,0:T(8,128)(2,1)}), bf16[128,32,512]{2,1,0:T(8,128)(2,1)}, u32[]{:S(2)}, u32[]{:S(2)}) %all-to-all-start.5) | async-done | bytes 4194336 | tf_op jit(solution)/shard_map/all_to_all | solution.py:129
  336.2 10.3 %gather_fusion.8 = bf16[2048,512]{1,0:T(8,128)(2,1)S(1)} fusion(bf16[4096,512]{1,0:T(8,128)(2,1)} %bitcast.27, s32[2048]{0:T(1024)S(1)} %broadcast_clamp_fusion.1), kind=kCustom, calls=%fused_computation.8 | custom fusion | bytes 4202496 | tf_op jit(solution)/shard_map/gather | solution.py:130
  346.6 3.6 convolution_convert_fusion
  350.2 6.6 %convert_add_fusion = f32[2048,1024]{1,0:T(8,128)} fusion(bf16[2048,1024]{1,0:T(8,128)(2,1)S(1)} %convolution_convert_fusion, bf16[128,1024]{1,0:T(8,128)(2,1)S(1)} %copy-done.5, f32[128]{0:T(128)S(1)} %copy-done.13, f32[128]{0:T(128)S(1)} %copy-done.15, f32[2048]{0:T(1024)S(1)} %mul.102), kind=kOutput, calls=%fused_computation.19 | convolution fusion | flops 541851648 | bytes 12854272 | tf_op jit(solution)/shard_map/dot_general | solution.py:135
  356.9 13.4 %reshape.141 = f32[128,16,2,8,64]{4,3,2,1,0:T(8,128)} reshape(f32[2048,1024]{1,0:T(8,128)} %convert_add_fusion) | data formatting | bytes 16777216 | tf_op jit(solution)/shard_map/reshape | solution.py:136
  370.3 5.7 %fusion.4 = f32[128,8,16]{1,2,0:T(8,128)S(1)} fusion(f32[128,16,2,8,64]{4,3,2,1,0:T(8,128)} %reshape.141, f32[128,8,64]{2,1,0:T(8,128)S(1)} %copy-done.3), kind=kLoop, calls=%fused_computation.18 | loop fusion | flops 2080768 | bytes 4521984
  377.2 5.3 %fusion.2 = bf16[128,8,64]{2,1,0:T(8,128)(2,1)S(1)} fusion(f32[128,16,2,8,64]{4,3,2,1,0:T(8,128)} %reshape.141, f32[128,8,16]{1,2,0:T(8,128)S(1)} %copy.78), kind=kLoop, calls=%fused_computation.15 | loop fusion | flops 2031616 | bytes 4390912
  382.6 0.8 copy.60
  (96 shorter events, 9.2 us)
Async XLA Ops:
  7.2 75.6 %copy-start = (bf16[1152,512]{1,0:T(8,128)(2,1)S(1)}, bf16[1152,512]{1,0:T(8,128)(2,1)}, u32[]{:S(2)}) copy-start(bf16[1152,512]{1,0:T(8,128)(2,1)} %param.29) | copy-start | bytes 3538948
  7.2 31.8 %copy-start.1 = (s32[512]{0:T(512)S(1)}, s32[512]{0:T(512)}, u32[]{:S(2)}) copy-start(s32[512]{0:T(512)} %param.19) | copy-start | bytes 6148
  11.6 25.2 %all-to-all-start = ((s32[128,1,2]{2,1,0:T(1,128)}), s32[128,1,2]{2,1,0:T(1,128)S(1)}, u32[]{:S(2)}, u32[]{:S(2)}) async-start(s32[128,1,2]{2,1,0:T(1,128)} %bitcast.5), calls=%async_computation | async-start | bytes 131072 | tf_op jit(solution)/shard_map/all_to_all | solution.py:84
  39.0 13.9 %copy-start.9 = (s32[128,16]{0,1:T(8,128)S(1)}, s32[128,16]{0,1:T(8,128)}, u32[]{:S(2)}) copy-start(s32[128,16]{0,1:T(8,128)} %param.25) | copy-start | bytes 24580
  39.0 14.0 %copy-start.2 = (f32[512,512]{1,0:T(8,128)S(1)}, f32[512,512]{1,0:T(8,128)}, u32[]{:S(2)}) copy-start(f32[512,512]{1,0:T(8,128)} %param.18) | copy-start | bytes 3145732
  41.0 30.9 %copy-start.18 = (s32[128]{0:T(128)S(1)}, s32[128]{0:T(128)}, u32[]{:S(2)}) copy-start(s32[128]{0:T(128)} %param.23) | copy-start | bytes 1540
  41.0 30.9 %copy-start.12 = (f32[128]{0:T(128)S(1)}, f32[128]{0:T(128)}, u32[]{:S(2)}) copy-start(f32[128]{0:T(128)} %param.28) | copy-start | bytes 1540
  41.0 30.9 %copy-start.14 = (f32[128]{0:T(128)S(1)}, f32[128]{0:T(128)}, u32[]{:S(2)}) copy-start(f32[128]{0:T(128)} %param.27) | copy-start | bytes 1540
  41.8 17.7 %all-to-all-start.2 = ((s32[128,1,2]{2,1,0:T(1,128)}), s32[128,1,2]{2,1,0:T(1,128)S(1)}, u32[]{:S(2)}, u32[]{:S(2)}) async-start(s32[128,1,2]{2,1,0:T(1,128)} %bitcast.6), calls=%async_computation.2 | async-start | bytes 131072 | tf_op jit(solution)/shard_map/all_to_all | solution.py:90
  51.4 1.8 copy-start.11
  59.5 22.4 %all-to-all-start.1 = ((bf16[128,2,512]{2,1,0:T(2,128)(2,1)}), bf16[128,2,512]{2,1,0:T(2,128)(2,1)S(1)}, u32[]{:S(2)}, u32[]{:S(2)}) async-start(bf16[128,2,512]{2,1,0:T(2,128)(2,1)} %reshape.151), calls=%async_computation.1 | async-start | bytes 524288 | tf_op jit(solution)/shard_map/all_to_all | solution.py:89
  83.4 37.8 %copy-start.6 = (bf16[256,512]{1,0:T(8,128)(2,1)}, bf16[256,512]{1,0:T(8,128)(2,1)S(1)}, u32[]{:S(2)}) copy-start(bf16[256,512]{1,0:T(8,128)(2,1)S(1)} %multiply_convert_fusion) | copy-start | bytes 786436
  83.4 38.3 %copy-start.16 = (s32[128]{0:T(128)S(1)}, s32[128]{0:T(128)}, u32[]{:S(2)}) copy-start(s32[128]{0:T(128)} %param.20) | copy-start | bytes 1540
  85.4 38.6 %copy-start.17 = (f32[4,128]{1,0:T(4,128)S(1)}, f32[4,128]{1,0:T(4,128)}, u32[]{:S(2)}) copy-start(f32[4,128]{1,0:T(4,128)} %param.32) | copy-start | bytes 6148
  85.4 21.6 %all-to-all-start.3 = ((bf16[128,2,512]{2,1,0:T(2,128)(2,1)}), bf16[128,2,512]{2,1,0:T(2,128)(2,1)S(1)}, u32[]{:S(2)}, u32[]{:S(2)}) async-start(bf16[128,2,512]{2,1,0:T(2,128)(2,1)} %reshape.135), calls=%async_computation.3 | async-start | bytes 524288 | tf_op jit(solution)/shard_map/all_to_all | solution.py:103
  94.3 8.1 %copy-start.7 = (s32[2048,1]{0,1:T(1,128)}, s32[2048,1]{0,1:T(1,128)S(1)}, u32[]{:S(2)}) copy-start(s32[2048,1]{0,1:T(1,128)S(1)} %compare_select_fusion) | copy-start | bytes 24580
  107.0 26.0 %all-to-all-start.4 = ((s32[128,1,32]{2,1,0:T(1,128)}), s32[128,1,32]{2,1,0:T(1,128)}, u32[]{:S(2)}, u32[]{:S(2)}) async-start(s32[128,1,32]{2,1,0:T(1,128)} %bitcast.135), calls=%async_computation.4 | async-start | bytes 131072 | tf_op jit(solution)/shard_map/all_to_all | solution.py:85
  121.3 58.9 %all-reduce.2.cloned.1.call-start = ((), (), s32[]{:S(2)}) async-start(), calls=%async_computation.6 | async-start | bytes 2097152 | tf_op jit(solution)/shard_map/psum | solution.py:114
  213.3 19.2 %copy-start.19 = (s32[128]{0:T(128)S(1)}, s32[128]{0:T(128)}, u32[]{:S(2)}) copy-start(s32[128]{0:T(128)} %param.23) | copy-start | bytes 1540
  213.3 19.2 %copy-start.10 = (s32[128,16]{0,1:T(8,128)S(1)}, s32[128,16]{0,1:T(8,128)}, u32[]{:S(2)}) copy-start(s32[128,16]{0,1:T(8,128)} %param.26) | copy-start | bytes 24580
  213.3 19.5 %copy-start.8 = (s32[2048,1]{0,1:T(1,128)S(1)}, s32[2048,1]{0,1:T(1,128)}, u32[]{:S(2)}) copy-start(s32[2048,1]{0,1:T(1,128)} %copy-done.7) | copy-start | bytes 24580
  213.3 20.4 %copy-start.4 = (bf16[512,512]{1,0:T(8,128)(2,1)S(1)}, bf16[512,512]{1,0:T(8,128)(2,1)}, u32[]{:S(2)}) copy-start(bf16[512,512]{1,0:T(8,128)(2,1)} %param.33) | copy-start | bytes 1572868
  213.3 122.9 %all-to-all-start.5 = ((bf16[128,32,512]{2,1,0:T(8,128)(2,1)}), bf16[128,32,512]{2,1,0:T(8,128)(2,1)}, u32[]{:S(2)}, u32[]{:S(2)}) async-start(bf16[128,32,512]{2,1,0:T(8,128)(2,1)} %bitcast.132), calls=%async_computation.5 | async-start | bytes 8388608 | tf_op jit(solution)/shard_map/all_to_all | solution.py:129
  346.6 3.6 copy-start.5
  346.6 3.6 copy-start.13
  346.6 3.6 copy-start.15
  356.8 13.4 %copy-start.3 = (f32[128,8,64]{2,1,0:T(8,128)S(1)}, f32[128,8,64]{2,1,0:T(8,128)}, u32[]{:S(2)}) copy-start(f32[128,8,64]{2,1,0:T(8,128)} %copy.77) | copy-start | bytes 786436
Sparse Core Ops, SparseCore 0:
  124.4 55.7 all-reduce.1
where the time goes:
time: 392 us; the launch traced here: 390 us
  waiting for transfers between devices  164 us (42%)
  starting transfers between devices  79.3 us (20%)
  local copies, waits for them, and re-layouts  70.6 us (18%)
  other arithmetic  21.3 us (5%)
  blocking collectives  20.3 us (5%)
  matrix products  19.8 us (5%)
  between operations  14.7 us (4%)
    all_to_all x1, waiting for transfers between devices, on_device(): lax.all_to_all(served, 'nodes', split_axis=0, concat_axis=0, tiled=True)  101 us
    psum x1, waiting for transfers between devices, on_device(): sums, counts = lax.psum((sums, counts), 'rep')  46.1 us
    all_to_all x1, starting transfers between devices, on_device(): lax.all_to_all(served, 'nodes', split_axis=0, concat_axis=0, tiled=True)  19.2 us
    gather x1, local copies, waits for them, and re-layouts, on_device(): served = updated[jnp.maximum(got_nbr, 0)]  17.3 us
    all_to_all x1, starting transfers between devices, on_device(): lax.all_to_all(dst_ids, 'nodes', split_axis=0, concat_axis=0, tiled=True)  17.2 us
    all_to_all x1, starting transfers between devices, on_device(): lax.all_to_all(nbr_ids, 'nodes', split_axis=0, concat_axis=0, tiled=True)  14.2 us
    reshape x1, local copies, waits for them, and re-layouts, on_device(): keyval = (kv_mem + kv_time).reshape(events, neighbours, 2, HEADS, HEAD_DIM)  13.4 us
    all_gather x1, blocking collectives, on_device(): lax.all_gather(new_part.astype(jnp.bfloat16), 'rep', axis=1, tiled=True)  11.5 us
  transfers between devices with their start and end apart: 7, of which 5 were waited for; matrix products, arithmetic and copies ran while one was open for 8% of the time, Pallas kernels for 0%

commit v1 on v0

--- a/solution.py
+++ b/solution.py
@@ -19,19 +19,9 @@
     return owner * capacity + jnp.sum(before * onehot, axis=1)
 
 
-def message_pair(src_rows, dst_rows, src_time, dst_time, w_message):
-    count = src_rows.shape[0]
-    stacked = jnp.concatenate(
-        [
-            jnp.concatenate([src_rows, dst_rows, src_time], axis=1),
-            jnp.concatenate([dst_rows, src_rows, dst_time], axis=1),
-        ],
-        axis=0,
-    )
-    messages = jax.nn.silu(jnp.dot(stacked, w_message, preferred_element_type=jnp.float32)).astype(
-        jnp.bfloat16
-    )
-    return (messages[:count], messages[count:])
+def select_rows(ids, table):
+    hits = (ids[:, None] == jnp.arange(table.shape[0], dtype=jnp.int32)[None, :]).astype(table.dtype)
+    return jnp.dot(hits, table, preferred_element_type=jnp.float32).astype(table.dtype)
 
 
 def on_device(
@@ -55,20 +45,26 @@
     w_keyval_time,
 ):
     groups = lax.axis_size("nodes")
+    reps = lax.axis_size("rep")
     events = src_local.shape[0]
     rows_here = memory.shape[0]
     width_m = memory.shape[1]
     neighbours = nbr_local.shape[1]
-    msg_width = w_message.shape[1]
     dst_cap = max(2, 2 * events // groups)
     nbr_cap = 2 * events * neighbours // groups
     dst_slot = place(dst_owner[:, 0], groups, dst_cap)
     nbr_slot = place(nbr_owner.reshape(-1), groups, nbr_cap)
-    dst_ids = (
-        jnp.full((groups * dst_cap,), -1, jnp.int32)
+    mem_half = memory.astype(jnp.bfloat16)
+    near_rows = mem_half[src_local]
+    near_ticks = last_tick[src_local]
+    ticks = event_tick.astype(jnp.float32)
+
+    req = jnp.stack([dst_local, event_tick, near_ticks], axis=1)
+    req_ints = (
+        jnp.full((groups * dst_cap, 3), -1, jnp.int32)
         .at[dst_slot]
-        .set(dst_local)
-        .reshape(groups, dst_cap)
+        .set(req)
+        .reshape(groups, dst_cap * 3)
     )
     nbr_ids = (
         jnp.full((groups * nbr_cap,), -1, jnp.int32)
@@ -76,42 +72,60 @@
         .set(nbr_local.reshape(-1))
         .reshape(groups, nbr_cap)
     )
-    mem_half = memory.astype(jnp.bfloat16)
-    near_rows = mem_half[src_local]
-    near_ticks = last_tick[src_local]
-    ticks = event_tick.astype(jnp.float32)
-    got_dst, got_nbr = (
-        lax.all_to_all(dst_ids, "nodes", split_axis=0, concat_axis=0, tiled=True),
-        lax.all_to_all(nbr_ids, "nodes", split_axis=0, concat_axis=0, tiled=True),
+    req_rows = (
+        jnp.zeros((groups * dst_cap, width_m), jnp.bfloat16)
+        .at[dst_slot]
+        .set(near_rows)
+        .reshape(groups, dst_cap, width_m)
     )
+    ints_out = jnp.concatenate([req_ints, nbr_ids], axis=1)
+    ints_in = lax.all_to_all(ints_out, "nodes", split_axis=0, concat_axis=0, tiled=True)
+    rows_in = lax.all_to_all(req_rows, "nodes", split_axis=0, concat_axis=0, tiled=True)
+    got = ints_in[:, : dst_cap * 3].reshape(groups * dst_cap, 3)
+    got_nbr = ints_in[:, dst_cap * 3 :]
+    got_dst = got[:, 0]
+    got_tick = got[:, 1].astype(jnp.float32)
+    got_src_tick = got[:, 2].astype(jnp.float32)
     safe_dst = jnp.maximum(got_dst, 0)
-    reply_rows, reply_ticks = (
-        lax.all_to_all(mem_half[safe_dst], "nodes", split_axis=0, concat_axis=0, tiled=True),
-        lax.all_to_all(last_tick[safe_dst], "nodes", split_axis=0, concat_axis=0, tiled=True),
+    far_src = rows_in.reshape(-1, width_m)
+    own_dst = mem_half[safe_dst]
+    own_dst_tick = last_tick[safe_dst].astype(jnp.float32)
+
+    src_time = encode(got_tick - got_src_tick, freq, phase).astype(jnp.bfloat16)
+    dst_time = encode(got_tick - own_dst_tick, freq, phase).astype(jnp.bfloat16)
+    slots = far_src.shape[0]
+    stacked = jnp.concatenate(
+        [
+            jnp.concatenate([far_src, own_dst, src_time], axis=1),
+            jnp.concatenate([own_dst, far_src, dst_time], axis=1),
+        ],
+        axis=0,
     )
-    far_rows = reply_rows.reshape(-1, width_m)[dst_slot]
-    far_ticks = reply_ticks.reshape(-1)[dst_slot]
-    src_time = encode(ticks - near_ticks.astype(jnp.float32), freq, phase).astype(jnp.bfloat16)
-    dst_time = encode(ticks - far_ticks.astype(jnp.float32), freq, phase).astype(jnp.bfloat16)
-    msg_src, msg_dst = message_pair(near_rows, far_rows, src_time, dst_time, w_message)
-    outgoing = (
-        jnp.zeros((groups * dst_cap, msg_width), jnp.bfloat16)
-        .at[dst_slot]
-        .set(msg_dst)
-        .reshape(groups, dst_cap, msg_width)
+    messages = jax.nn.silu(jnp.dot(stacked, w_message, preferred_element_type=jnp.float32)).astype(
+        jnp.bfloat16
     )
-    incoming = lax.all_to_all(outgoing, "nodes", split_axis=0, concat_axis=0, tiled=True)
-    far_msgs = incoming.reshape(-1, msg_width)
+    msg_src_slots = messages[:slots]
+    msg_dst = messages[slots:]
+    back = lax.all_to_all(
+        msg_src_slots.reshape(groups, dst_cap, -1), "nodes", split_axis=0, concat_axis=0, tiled=True
+    )
+    msg_src = back.reshape(-1, back.shape[2])[dst_slot]
+
+    local_msgs = jnp.concatenate([msg_src, msg_dst], axis=0)
+    local_ids = jnp.concatenate([src_local, got_dst], axis=0)
+    all_msgs = [local_msgs]
+    all_ids = [local_ids]
+    for shift in range(1, reps):
+        pairs = [(i, (i + shift) % reps) for i in range(reps)]
+        all_msgs.append(lax.ppermute(local_msgs, "rep", pairs))
+        all_ids.append(lax.ppermute(local_ids, "rep", pairs))
+    all_msgs = jnp.concatenate(all_msgs, axis=0)
+    all_ids = jnp.concatenate(all_ids, axis=0)
     row_ids = jnp.arange(rows_here, dtype=jnp.int32)[:, None]
-    hit_far = (row_ids == got_dst.reshape(1, -1)).astype(jnp.bfloat16)
-    hit_near = (row_ids == src_local[None, :]).astype(jnp.bfloat16)
-    sums = jnp.dot(hit_near, msg_src, preferred_element_type=jnp.float32) + jnp.dot(
-        hit_far, far_msgs, preferred_element_type=jnp.float32
-    )
-    counts = jnp.sum(hit_near.astype(jnp.float32), axis=1) + jnp.sum(
-        hit_far.astype(jnp.float32), axis=1
-    )
-    sums, counts = lax.psum((sums, counts), "rep")
+    hits = row_ids == all_ids[None, :]
+    sums = jnp.dot(hits.astype(jnp.bfloat16), all_msgs, preferred_element_type=jnp.float32)
+    counts = jnp.sum(hits.astype(jnp.float32), axis=1)
+
     unit_width = gru_bias.shape[1]
     start = lax.axis_index("rep") * unit_width
     state_part = lax.dynamic_slice_in_dim(memory, start, unit_width, 1)
@@ -125,7 +139,7 @@
     fresh = (1.0 - update) * cand + update * state_part
     new_part = jnp.where((counts > 0.0)[:, None], fresh, state_part)
     updated = lax.all_gather(new_part.astype(jnp.bfloat16), "rep", axis=1, tiled=True)
-    served = updated[jnp.maximum(got_nbr, 0)]
+    served = select_rows(got_nbr.reshape(-1), updated).reshape(groups, nbr_cap, -1)
     returned = lax.all_to_all(served, "nodes", split_axis=0, concat_axis=0, tiled=True)
     fetched = returned.reshape(-1, updated.shape[1])[nbr_slot]
     kv_mem = jnp.dot(fetched, w_keyval_mem, preferred_element_type=jnp.float32).astype(jnp.bfloat16)

time: 392 us -> 326 us (0.83)
  the two profiles are of different devices: /device:TPU:41 before, /device:TPU:33 now
where the time goes in v1:
time: 326 us; the launch traced here: 324 us
  waiting for transfers between devices  118 us (36%)
  starting transfers between devices  79.6 us (24%)
  local copies, waits for them, and re-layouts  64.4 us (20%)
  other arithmetic  26.1 us (8%)
  matrix products  22.8 us (7%)
  blocking collectives  11.4 us (3%)
    all_to_all x1, waiting for transfers between devices, on_device(): lax.all_to_all(served, 'nodes', split_axis=0, concat_axis=0, tiled=True)  102 us
    all_to_all x1, starting transfers between devices, on_device(): lax.all_to_all(ints_out, 'nodes', split_axis=0, concat_axis=0, tiled=True)  17.8 us
    all_to_all x1, starting transfers between devices, on_device(): lax.all_to_all(msg_src_slots.reshape(groups, dst_cap, -1), 'nodes', split...  14.6 us
    all_to_all x1, starting transfers between devices, on_device(): lax.all_to_all(req_rows, 'nodes', split_axis=0, concat_axis=0, tiled=True)  14.2 us
    all_to_all x1, starting transfers between devices, on_device(): lax.all_to_all(served, 'nodes', split_axis=0, concat_axis=0, tiled=True)  13.6 us
    reshape x1, local copies, waits for them, and re-layouts, on_device(): keyval = (kv_mem + kv_time).reshape(events, neighbours, 2, HEADS, HEAD_DIM)  13.4 us
    ppermute x3, waiting for transfers between devices, on_device(): all_msgs.append(lax.ppermute(local_msgs, 'rep', pairs))  12.8 us
    unnamed x4, other arithmetic  12.2 us
  transfers between devices with their start and end apart: 10, of which 3 were waited for; matrix products, arithmetic and copies ran while one was open for 10% of the time, Pallas kernels for 0%

profile of v1, /device:TPU:33, one launch (start us, length us, event | category | flops | bytes accessed | tf_op | source)
XLA Modules:
  0.0 323.8 jit_solution(6872314112118746933)
XLA Ops:
  2.4 1.3 constant_dynamic-update-slice_fusion
  3.9 1.6 gather_fusion
  9.8 0.9 scatter_custom_fusion
  12.3 8.1 %scatter_custom_fusion.1 = s32[4096]{0:T(1024)S(1)} fusion(s32[2048]{0:T(1024)S(1)} %bitcast.143, s32[2048]{0:T(1024)S(1)} %reshape.201, s32[]{:T(128)} %constant.14.clone.1), kind=kCustom, calls=%fused_computation.117 | custom fusion | bytes 16388 | tf_op jit(solution)/shard_map/scatter | solution.py:72
  21.2 17.8 %all-to-all-start = ((s32[128,1,38]{2,1,0:T(1,128)}), s32[128,1,38]{2,1,0:T(1,128)}, u32[]{:S(2)}, u32[]{:S(2)}) async-start(s32[128,1,38]{2,1,0:T(1,128)} %bitcast.14), calls=%async_computation | async-start | bytes 131072 | tf_op jit(solution)/shard_map/all_to_all | solution.py:82
  39.5 3.0 convolution_bitcast_fusion
  43.2 2.4 scatter_custom_fusion.2
  45.6 1.7 reshape.125
  47.4 14.2 %all-to-all-start.1 = ((bf16[128,2,512]{2,1,0:T(2,128)(2,1)}), bf16[128,2,512]{2,1,0:T(2,128)(2,1)}, u32[]{:S(2)}, u32[]{:S(2)}) async-start(bf16[128,2,512]{2,1,0:T(2,128)(2,1)} %reshape.125), calls=%async_computation.1 | async-start | bytes 524288 | tf_op jit(solution)/shard_map/all_to_all | solution.py:83
  61.6 1.6 reshape.124
  63.1 1.0 slice_reduce_fusion
  64.8 2.0 gather_fusion.1
  66.8 2.1 gather_fusion.2
  69.5 4.6 %collective-permute-start.2 = (s32[384]{0:T(512)S(1)}, s32[384]{0:T(512)}, u32[]{:S(2)}, u32[]{:S(2)}) collective-permute-start(s32[384]{0:T(512)S(1)} %pad_add_fusion.2), channel_id=1, source_target_pairs={{0,3},{1,0},{2,1},{3,2},{4,7},{5,4},{6,5},{7,6},{8,11},{9,8},{10,9... | collective-permute-start | bytes 4616 | tf_op jit(solution)/shard_map/ppermute | solution.py:121
  74.1 2.4 collective-permute-start.1
  76.5 2.5 collective-permute-start
  79.2 1.2 fusion.58
  80.4 1.6 cosine_convert_fusion.3
  82.1 1.1 reshape.126
  83.1 2.0 multiply_convert_fusion
  86.8 14.6 %all-to-all-start.2 = ((bf16[128,2,512]{2,1,0:T(2,128)(2,1)}), bf16[128,2,512]{2,1,0:T(2,128)(2,1)S(1)}, u32[]{:S(2)}, u32[]{:S(2)}) async-start(bf16[128,2,512]{2,1,0:T(2,128)(2,1)} %reshape.127), calls=%async_computation.2 | async-start | bytes 524288 | tf_op jit(solution)/shard_map/all_to_all | solution.py:109
  101.3 1.3 constant_dynamic-update-slice_fusion.9
  102.6 0.9 slice.112
  104.3 1.3 constant_dynamic-update-slice_fusion.8
  105.6 1.3 constant_dynamic-update-slice_fusion.7
  106.9 1.3 constant_dynamic-update-slice_fusion.6
  108.1 1.1 convert_reduce_fusion
  109.2 3.5 %all-to-all-done.2 = bf16[128,2,512]{2,1,0:T(2,128)(2,1)S(1)} async-done(((bf16[128,2,512]{2,1,0:T(2,128)(2,1)}), bf16[128,2,512]{2,1,0:T(2,128)(2,1)S(1)}, u32[]{:S(2)}, u32[]{:S(2)}) %all-to-all-start.2) | async-done | bytes 262176 | tf_op jit(solution)/shard_map/all_to_all | solution.py:109
  112.8 1.0 gather_fusion.3
  113.8 1.0 fusion.74
  114.8 3.5 %collective-permute-start.4 = (bf16[384,512]{1,0:T(8,128)(2,1)S(1)}, bf16[384,512]{1,0:T(8,128)(2,1)S(1)}, u32[]{:S(2)}, u32[]{:S(2)}) collective-permute-start(bf16[384,512]{1,0:T(8,128)(2,1)S(1)} %pad_maximum_fusion), channel_id=1, source_target_pairs={{0,2},{1,3},{2,0},{3,1},{4,6},{5,7},{6,4},{7,5},{8,10},{9,11},{10,... | collective-permute-start | bytes 1179656 | tf_op jit(solution)/shard_map/ppermute | solution.py:120
  118.3 3.0 collective-permute-start.3
  121.3 3.5 %collective-permute-start.5 = (bf16[384,512]{1,0:T(8,128)(2,1)S(1)}, bf16[384,512]{1,0:T(8,128)(2,1)S(1)}, u32[]{:S(2)}, u32[]{:S(2)}) collective-permute-start(bf16[384,512]{1,0:T(8,128)(2,1)S(1)} %pad_maximum_fusion), channel_id=1, source_target_pairs={{0,3},{1,0},{2,1},{3,2},{4,7},{5,4},{6,5},{7,6},{8,11},{9,8},{10,9... | collective-permute-start | bytes 1179656 | tf_op jit(solution)/shard_map/ppermute | solution.py:120
  124.8 12.8 %collective-permute-done.3 = bf16[384,512]{1,0:T(8,128)(2,1)S(1)} collective-permute-done((bf16[384,512]{1,0:T(8,128)(2,1)S(1)}, bf16[384,512]{1,0:T(8,128)(2,1)S(1)}, u32[]{:S(2)}, u32[]{:S(2)}) %collective-permute-start.3) | collective-permute-done | bytes 393248 | tf_op jit(solution)/shard_map/ppermute | solution.py:120
  137.8 1.0 fusion.11
  139.0 1.8 convolution_bitcast_fusion.1
  140.8 1.0 fusion.72
  141.8 11.4 %all_gather.3 = bf16[512,512]{1,0:T(8,128)(2,1)S(1)} all-gather(bf16[512,128]{1,0:T(8,128)(2,1)S(1)} %get-tuple-element.12), channel_id=1, replica_groups=mesh['nodes'=128,'rep'=4] {'rep'}, dimensions={1}, use_global_device_ids=true | all-gather | bytes 655360 | tf_op jit(solution)/shard_map/all_gather | solution.py:141
  153.1 3.9 %fusion.6 = bf16[4096,512]{1,0:T(8,128)(2,1)} fusion(bf16[512,512]{1,0:T(8,128)(2,1)S(1)} %all_gather.3, s32[4096]{0:T(1024)S(1)} %copy-done.7), kind=kOutput, calls=%fused_computation.20 | convolution fusion | flops 2151677952 | bytes 4734976 | tf_op jit(solution)/shard_map/dot_general | solution.py:24
  157.1 13.6 %all-to-all-start.3 = ((bf16[128,32,512]{2,1,0:T(8,128)(2,1)}), bf16[128,32,512]{2,1,0:T(8,128)(2,1)}, u32[]{:S(2)}, u32[]{:S(2)}) async-start(bf16[128,32,512]{2,1,0:T(8,128)(2,1)} %bitcast.139), calls=%async_computation.3 | async-start | bytes 8388608 | tf_op jit(solution)/shard_map/all_to_all | solution.py:143
  171.0 1.0 gather_fusion.4
  172.5 101.9 %all-to-all-done.3 = bf16[128,32,512]{2,1,0:T(8,128)(2,1)} async-done(((bf16[128,32,512]{2,1,0:T(8,128)(2,1)}), bf16[128,32,512]{2,1,0:T(8,128)(2,1)}, u32[]{:S(2)}, u32[]{:S(2)}) %all-to-all-start.3) | async-done | bytes 4194336 | tf_op jit(solution)/shard_map/all_to_all | solution.py:143
  274.5 12.0 %gather_fusion.5 = bf16[2048,512]{1,0:T(8,128)(2,1)} fusion(bf16[4096,512]{1,0:T(8,128)(2,1)} %bitcast.31, s32[2048]{0:T(1024)S(1)} %broadcast_clamp_fusion), kind=kCustom, calls=%fused_computation.6 | custom fusion | bytes 4202496 | tf_op jit(solution)/shard_map/gather | solution.py:144
  286.4 4.2 %convolution_convert_fusion = bf16[2048,1024]{1,0:T(8,128)(2,1)S(1)} fusion(bf16[2048,512]{1,0:T(8,128)(2,1)} %gather_fusion.5, bf16[512,1024]{1,0:T(8,128)(2,1)} %param.34), kind=kOutput, calls=%fused_computation.22 | convolution fusion | flops 2149580800 | bytes 7340032 | tf_op jit(solution)/shard_map/dot_general | solution.py:145
  290.7 6.6 %convert_add_fusion = f32[2048,1024]{1,0:T(8,128)} fusion(bf16[2048,1024]{1,0:T(8,128)(2,1)S(1)} %convolution_convert_fusion, bf16[128,1024]{1,0:T(8,128)(2,1)S(1)} %copy-done.6, f32[128]{0:T(128)S(1)} %copy-done.11, f32[128]{0:T(128)S(1)} %copy-done.12, f32[2048]{0:T(1024)S(1)} %mul.108), kind=kOutput, calls=%fused_computation.17 | convolution fusion | flops 541851648 | bytes 12854272 | tf_op jit(solution)/shard_map/dot_general | solution.py:149
  297.3 13.4 %reshape.132 = f32[128,16,2,8,64]{4,3,2,1,0:T(8,128)} reshape(f32[2048,1024]{1,0:T(8,128)} %convert_add_fusion) | data formatting | bytes 16777216 | tf_op jit(solution)/shard_map/reshape | solution.py:150
  310.7 5.7 %fusion.4 = f32[128,8,16]{1,2,0:T(8,128)S(1)} fusion(f32[128,16,2,8,64]{4,3,2,1,0:T(8,128)} %reshape.132, f32[128,8,64]{2,1,0:T(8,128)S(1)} %copy.81), kind=kLoop, calls=%fused_computation.16 | loop fusion | flops 2080768 | bytes 4521984
  317.6 5.3 %fusion.2 = bf16[128,8,64]{2,1,0:T(8,128)(2,1)S(1)} fusion(f32[128,16,2,8,64]{4,3,2,1,0:T(8,128)} %reshape.132, f32[128,8,16]{1,2,0:T(8,128)S(1)} %copy.82), kind=kLoop, calls=%fused_computation.13 | loop fusion | flops 2031616 | bytes 4390912
  (109 shorter events, 16.7 us)
Async XLA Ops:
  0.6 82.5 %copy-start = (bf16[1152,512]{1,0:T(8,128)(2,1)S(1)}, bf16[1152,512]{1,0:T(8,128)(2,1)}, u32[]{:S(2)}) copy-start(bf16[1152,512]{1,0:T(8,128)(2,1)} %param.29) | copy-start | bytes 3538948
  3.7 39.5 %copy-start.10 = (s32[1024]{0:T(1024)}, s32[1024]{0:T(1024)S(1)}, u32[]{:S(2)}) copy-start(s32[1024]{0:T(1024)S(1)} %pad_clamp_fusion.2) | copy-start | bytes 12292
  9.8 1.4 copy-start.19
  11.2 27.8 %copy-start.17 = (f32[4,128]{1,0:T(4,128)S(1)}, f32[4,128]{1,0:T(4,128)}, u32[]{:S(2)}) copy-start(f32[4,128]{1,0:T(4,128)} %param.32) | copy-start | bytes 6148
  11.2 28.3 %copy-start.2 = (f32[512,512]{1,0:T(8,128)S(1)}, f32[512,512]{1,0:T(8,128)}, u32[]{:S(2)}) copy-start(f32[512,512]{1,0:T(8,128)} %param.18) | copy-start | bytes 3145732
  11.6 30.9 %copy-start.20 = (s32[128]{0:T(128)S(1)}, s32[128]{0:T(128)}, u32[]{:S(2)}) copy-start(s32[128]{0:T(128)} %copy-done.19) | copy-start | bytes 1540
  21.2 26.2 %all-to-all-start = ((s32[128,1,38]{2,1,0:T(1,128)}), s32[128,1,38]{2,1,0:T(1,128)}, u32[]{:S(2)}, u32[]{:S(2)}) async-start(s32[128,1,38]{2,1,0:T(1,128)} %bitcast.14), calls=%async_computation | async-start | bytes 131072 | tf_op jit(solution)/shard_map/all_to_all | solution.py:82
  43.2 23.6 %copy-start.1 = (s32[512]{0:T(512)S(1)}, s32[512]{0:T(512)}, u32[]{:S(2)}) copy-start(s32[512]{0:T(512)} %param.19) | copy-start | bytes 6148
  47.4 34.7 %all-to-all-start.1 = ((bf16[128,2,512]{2,1,0:T(2,128)(2,1)}), bf16[128,2,512]{2,1,0:T(2,128)(2,1)}, u32[]{:S(2)}, u32[]{:S(2)}) async-start(bf16[128,2,512]{2,1,0:T(2,128)(2,1)} %reshape.125), calls=%async_computation.1 | async-start | bytes 524288 | tf_op jit(solution)/shard_map/all_to_all | solution.py:83
  69.5 37.3 %collective-permute-start.2 = (s32[384]{0:T(512)S(1)}, s32[384]{0:T(512)}, u32[]{:S(2)}, u32[]{:S(2)}) collective-permute-start(s32[384]{0:T(512)S(1)} %pad_add_fusion.2), channel_id=1, source_target_pairs={{0,3},{1,0},{2,1},{3,2},{4,7},{5,4},{6,5},{7,6},{8,11},{9,8},{10,9... | collective-permute-start | bytes 4616 | tf_op jit(solution)/shard_map/ppermute | solution.py:121
  74.1 31.5 %collective-permute-start.1 = (s32[384]{0:T(512)S(1)}, s32[384]{0:T(512)}, u32[]{:S(2)}, u32[]{:S(2)}) collective-permute-start(s32[384]{0:T(512)S(1)} %pad_add_fusion.2), channel_id=1, source_target_pairs={{0,2},{1,3},{2,0},{3,1},{4,6},{5,7},{6,4},{7,5},{8,10},{9,11},{10,... | collective-permute-start | bytes 4616 | tf_op jit(solution)/shard_map/ppermute | solution.py:121
  76.5 27.7 %collective-permute-start = (s32[384]{0:T(512)S(1)}, s32[384]{0:T(512)}, u32[]{:S(2)}, u32[]{:S(2)}) collective-permute-start(s32[384]{0:T(512)S(1)} %pad_add_fusion.2), channel_id=1, source_target_pairs={{0,1},{1,2},{2,3},{3,0},{4,5},{5,6},{6,7},{7,4},{8,9},{9,10},{10,1... | collective-permute-start | bytes 4616 | tf_op jit(solution)/shard_map/ppermute | solution.py:121
  85.2 0.8 copy-start.4
  86.8 25.9 %all-to-all-start.2 = ((bf16[128,2,512]{2,1,0:T(2,128)(2,1)}), bf16[128,2,512]{2,1,0:T(2,128)(2,1)S(1)}, u32[]{:S(2)}, u32[]{:S(2)}) async-start(bf16[128,2,512]{2,1,0:T(2,128)(2,1)} %reshape.127), calls=%async_computation.2 | async-start | bytes 524288 | tf_op jit(solution)/shard_map/all_to_all | solution.py:109
  113.8 24.0 %copy-start.8 = (s32[1536]{0:T(1024)S(1)}, s32[1536]{0:T(1024)}, u32[]{:S(2)}) copy-start(s32[1536]{0:T(1024)} %constant_dynamic-update-slice_fusion.6) | copy-start | bytes 18436
  114.8 22.9 %collective-permute-start.4 = (bf16[384,512]{1,0:T(8,128)(2,1)S(1)}, bf16[384,512]{1,0:T(8,128)(2,1)S(1)}, u32[]{:S(2)}, u32[]{:S(2)}) collective-permute-start(bf16[384,512]{1,0:T(8,128)(2,1)S(1)} %pad_maximum_fusion), channel_id=1, source_target_pairs={{0,2},{1,3},{2,0},{3,1},{4,6},{5,7},{6,4},{7,5},{8,10},{9,11},{10,... | collective-permute-start | bytes 1179656 | tf_op jit(solution)/shard_map/ppermute | solution.py:120
  118.3 19.4 %collective-permute-start.3 = (bf16[384,512]{1,0:T(8,128)(2,1)S(1)}, bf16[384,512]{1,0:T(8,128)(2,1)S(1)}, u32[]{:S(2)}, u32[]{:S(2)}) collective-permute-start(bf16[384,512]{1,0:T(8,128)(2,1)S(1)} %pad_maximum_fusion), channel_id=1, source_target_pairs={{0,1},{1,2},{2,3},{3,0},{4,5},{5,6},{6,7},{7,4},{8,9},{9,10},{10,1... | collective-permute-start | bytes 1179656 | tf_op jit(solution)/shard_map/ppermute | solution.py:120
  121.3 16.5 %collective-permute-start.5 = (bf16[384,512]{1,0:T(8,128)(2,1)S(1)}, bf16[384,512]{1,0:T(8,128)(2,1)S(1)}, u32[]{:S(2)}, u32[]{:S(2)}) collective-permute-start(bf16[384,512]{1,0:T(8,128)(2,1)S(1)} %pad_maximum_fusion), channel_id=1, source_target_pairs={{0,3},{1,0},{2,1},{3,2},{4,7},{5,4},{6,5},{7,6},{8,11},{9,8},{10,9... | collective-permute-start | bytes 1179656 | tf_op jit(solution)/shard_map/ppermute | solution.py:120
  137.8 1.1 copy-start.3
  138.9 1.8 copy-start.13
  138.9 1.9 copy-start.14
  138.9 1.9 copy-start.15
  138.9 1.9 copy-start.16
  138.9 14.2 %copy-start.7 = (s32[4096]{0:T(1024)S(1)}, s32[4096]{0:T(1024)}, u32[]{:S(2)}) copy-start(s32[4096]{0:T(1024)} %eq.83) | copy-start | bytes 49156
  157.1 13.7 %copy-start.18 = (s32[128]{0:T(128)S(1)}, s32[128]{0:T(128)}, u32[]{:S(2)}) copy-start(s32[128]{0:T(128)} %param.23) | copy-start | bytes 1540
  157.1 13.7 %copy-start.9 = (s32[128,16]{0,1:T(8,128)S(1)}, s32[128,16]{0,1:T(8,128)}, u32[]{:S(2)}) copy-start(s32[128,16]{0,1:T(8,128)} %param.26) | copy-start | bytes 24580
  157.1 14.9 %copy-start.5 = (bf16[512,512]{1,0:T(8,128)(2,1)S(1)}, bf16[512,512]{1,0:T(8,128)(2,1)}, u32[]{:S(2)}) copy-start(bf16[512,512]{1,0:T(8,128)(2,1)} %param.33) | copy-start | bytes 1572868
  157.1 117.4 %all-to-all-start.3 = ((bf16[128,32,512]{2,1,0:T(8,128)(2,1)}), bf16[128,32,512]{2,1,0:T(8,128)(2,1)}, u32[]{:S(2)}, u32[]{:S(2)}) async-start(bf16[128,32,512]{2,1,0:T(8,128)(2,1)} %bitcast.139), calls=%async_computation.3 | async-start | bytes 8388608 | tf_op jit(solution)/shard_map/all_to_all | solution.py:143
  286.4 4.3 %copy-start.6 = (bf16[128,1024]{1,0:T(8,128)(2,1)S(1)}, bf16[128,1024]{1,0:T(8,128)(2,1)}, u32[]{:S(2)}) copy-start(bf16[128,1024]{1,0:T(8,128)(2,1)} %param.35) | copy-start | bytes 786436
  286.4 4.3 %copy-start.11 = (f32[128]{0:T(128)S(1)}, f32[128]{0:T(128)}, u32[]{:S(2)}) copy-start(f32[128]{0:T(128)} %param.28) | copy-start | bytes 1540
  286.4 4.3 %copy-start.12 = (f32[128]{0:T(128)S(1)}, f32[128]{0:T(128)}, u32[]{:S(2)}) copy-start(f32[128]{0:T(128)} %param.27) | copy-start | bytes 1540

commit v2 on v1

--- a/solution.py
+++ b/solution.py
@@ -3,6 +3,8 @@
 import jax
 import jax.numpy as jnp
 from jax import lax
+from jax.experimental import pallas as pl
+from jax.experimental.pallas import tpu as pltpu
 from jax.sharding import PartitionSpec as P
 
 HEADS = 8
@@ -22,6 +24,55 @@
 def select_rows(ids, table):
     hits = (ids[:, None] == jnp.arange(table.shape[0], dtype=jnp.int32)[None, :]).astype(table.dtype)
     return jnp.dot(hits, table, preferred_element_type=jnp.float32).astype(table.dtype)
+
+
+def attend_kernel(fetched_ref, tenc_ref, q_ref, wm_ref, wt_ref, out_ref):
+    f32, bf16 = jnp.float32, jnp.bfloat16
+    block = q_ref.shape[0]
+    rows = fetched_ref.shape[0]
+    nbrs = rows // block
+    width = q_ref.shape[1]
+    kv_mem = jnp.dot(fetched_ref[...], wm_ref[...], preferred_element_type=f32).astype(bf16)
+    kv_time = jnp.dot(tenc_ref[...], wt_ref[...], preferred_element_type=f32)
+    keyval = kv_mem.astype(f32) + kv_time
+    keys = keyval[:, :width]
+    values = keyval[:, width:]
+    query = q_ref[...].astype(f32)
+    prod = (keys.reshape(block, nbrs, width) * query[:, None, :]).reshape(rows, width)
+    lane = lax.broadcasted_iota(jnp.int32, (width, 128), 0)
+    col = lax.broadcasted_iota(jnp.int32, (width, 128), 1)
+    head_of = (lane // HEAD_DIM == col).astype(f32)
+    highest = lax.Precision.HIGHEST
+    scores = jnp.dot(prod, head_of, preferred_element_type=f32, precision=highest)
+    scores = (scores / math.sqrt(HEAD_DIM)).reshape(block, nbrs, 128)
+    top = jnp.max(scores, axis=1, keepdims=True)
+    ex = jnp.exp(scores - top)
+    weights = (ex / jnp.sum(ex, axis=1, keepdims=True)).reshape(rows, 128)
+    row = lax.broadcasted_iota(jnp.int32, (128, width), 0)
+    lane2 = lax.broadcasted_iota(jnp.int32, (128, width), 1)
+    head_to = (lane2 // HEAD_DIM == row).astype(f32)
+    spread = jnp.dot(weights, head_to, preferred_element_type=f32, precision=highest)
+    mixed = jnp.sum((spread * values).reshape(block, nbrs, width), axis=1)
+    out_ref[...] = mixed.astype(out_ref.dtype)
+
+
+def attend(fetched, time_enc, query, w_keyval_mem, w_keyval_time, block=16):
+    events, width = query.shape
+    nbrs = fetched.shape[0] // events
+    rows = block * nbrs
+    return pl.pallas_call(
+        attend_kernel,
+        grid=(events // block,),
+        in_specs=[
+            pl.BlockSpec((rows, fetched.shape[1]), lambda i: (i, 0)),
+            pl.BlockSpec((rows, time_enc.shape[1]), lambda i: (i, 0)),
+            pl.BlockSpec((block, width), lambda i: (i, 0)),
+            pl.BlockSpec(w_keyval_mem.shape, lambda i: (0, 0)),
+            pl.BlockSpec(w_keyval_time.shape, lambda i: (0, 0)),
+        ],
+        out_specs=pl.BlockSpec((block, width), lambda i: (i, 0)),
+        out_shape=jax.ShapeDtypeStruct((events, width), jnp.bfloat16),
+    )(fetched, time_enc, query, w_keyval_mem, w_keyval_time)
 
 
 def on_device(
@@ -142,20 +193,12 @@
     served = select_rows(got_nbr.reshape(-1), updated).reshape(groups, nbr_cap, -1)
     returned = lax.all_to_all(served, "nodes", split_axis=0, concat_axis=0, tiled=True)
     fetched = returned.reshape(-1, updated.shape[1])[nbr_slot]
-    kv_mem = jnp.dot(fetched, w_keyval_mem, preferred_element_type=jnp.float32).astype(jnp.bfloat16)
-    kv_mem = lax.optimization_barrier(kv_mem).astype(jnp.float32)
     gaps = ticks[:, None] - nbr_tick.astype(jnp.float32)
     time_enc = encode(gaps, freq, phase).reshape(-1, freq.shape[0]).astype(jnp.bfloat16)
-    kv_time = jnp.dot(time_enc, w_keyval_time, preferred_element_type=jnp.float32)
-    keyval = (kv_mem + kv_time).reshape(events, neighbours, 2, HEADS, HEAD_DIM)
     query = jnp.dot(updated[src_local], w_query, preferred_element_type=jnp.float32).astype(
         jnp.bfloat16
     )
-    query = lax.optimization_barrier(query).astype(jnp.float32).reshape(events, HEADS, HEAD_DIM)
-    scores = jnp.einsum("ehd,ejhd->ehj", query, keyval[:, :, 0]) / math.sqrt(HEAD_DIM)
-    weights = jax.nn.softmax(scores, axis=-1)
-    mixed = jnp.einsum("ehj,ejhd->ehd", weights, keyval[:, :, 1])
-    embed = mixed.reshape(events, HEADS * HEAD_DIM).astype(jnp.bfloat16)
+    embed = attend(fetched, time_enc, query, w_keyval_mem, w_keyval_time)
     return (new_part, embed)
 
 

time: 326 us -> 308 us (0.945)
  the two profiles are of different devices: /device:TPU:33 before, /device:TPU:32 now
where the time goes in v2:
time: 308 us; the launch traced here: 307 us
  waiting for transfers between devices  115 us (37%)
  starting transfers between devices  76.8 us (25%)
  local copies, waits for them, and re-layouts  48.8 us (16%)
  Pallas kernels  20.8 us (7%)
  other arithmetic  16.9 us (5%)
  blocking collectives  14.3 us (5%)
  matrix products  12.6 us (4%)
    all_to_all x1, waiting for transfers between devices, on_device(): lax.all_to_all(served, 'nodes', split_axis=0, concat_axis=0, tiled=True)  95.6 us
    pallas_call x1, Pallas kernels, attend(): pl.pallas_call(attend_kernel, grid=(events // block,), in_specs=[pl.Block...  20.8 us
    all_to_all x1, starting transfers between devices, on_device(): lax.all_to_all(ints_out, 'nodes', split_axis=0, concat_axis=0, tiled=True)  17.5 us
    ppermute x3, waiting for transfers between devices, on_device(): all_msgs.append(lax.ppermute(local_msgs, 'rep', pairs))  16 us
    all_gather x1, blocking collectives, on_device(): lax.all_gather(new_part.astype(jnp.bfloat16), 'rep', axis=1, tiled=True)  14.3 us
    all_to_all x1, starting transfers between devices, on_device(): lax.all_to_all(req_rows, 'nodes', split_axis=0, concat_axis=0, tiled=True)  14.2 us
    all_to_all x1, starting transfers between devices, on_device(): lax.all_to_all(msg_src_slots.reshape(groups, dst_cap, -1), 'nodes', split...  13.7 us
    gather x1, local copies, waits for them, and re-layouts, on_device(): fetched = returned.reshape(-1, updated.shape[1])[nbr_slot]  12 us
  transfers between devices with their start and end apart: 10, of which 4 were waited for; matrix products, arithmetic and copies ran while one was open for 13% of the time, Pallas kernels for 0%

profile of v2, /device:TPU:32, one launch (start us, length us, event | category | flops | bytes accessed | tf_op | source)
XLA Modules:
  0.0 306.8 jit_solution(8735251324412147551)
XLA Ops:
  4.7 8.1 %scatter_custom_fusion.1 = s32[4096]{0:T(1024)S(1)} fusion(s32[2048]{0:T(1024)S(1)} %bitcast.117, s32[2048]{0:T(1024)S(1)} %reshape.189, s32[]{:T(128)} %constant.12.clone.1), kind=kCustom, calls=%fused_computation.99 | custom fusion | bytes 16388 | tf_op jit(solution)/shard_map/scatter | solution.py:123
  13.4 1.3 constant_dynamic-update-slice_fusion
  14.7 1.3 gather_fusion
  16.1 0.9 scatter_custom_fusion
  17.8 17.5 %all-to-all-start = ((s32[128,1,38]{2,1,0:T(1,128)}), s32[128,1,38]{2,1,0:T(1,128)}, u32[]{:S(2)}, u32[]{:S(2)}) async-start(s32[128,1,38]{2,1,0:T(1,128)} %bitcast.12), calls=%async_computation | async-start | bytes 131072 | tf_op jit(solution)/shard_map/all_to_all | solution.py:133
  35.9 3.0 convolution_bitcast_fusion
  39.6 2.4 scatter_custom_fusion.2
  42.0 1.8 reshape.115
  43.8 14.2 %all-to-all-start.1 = ((bf16[128,2,512]{2,1,0:T(2,128)(2,1)}), bf16[128,2,512]{2,1,0:T(2,128)(2,1)}, u32[]{:S(2)}, u32[]{:S(2)}) async-start(bf16[128,2,512]{2,1,0:T(2,128)(2,1)} %reshape.115), calls=%async_computation.1 | async-start | bytes 524288 | tf_op jit(solution)/shard_map/all_to_all | solution.py:134
  58.0 1.6 reshape.114
  59.6 1.0 slice_reduce_fusion
  61.2 2.6 gather_fusion.2
  63.8 2.1 gather_fusion.1
  66.6 3.4 %collective-permute-start = (s32[384]{0:T(512)S(1)}, s32[384]{0:T(512)}, u32[]{:S(2)}, u32[]{:S(2)}) collective-permute-start(s32[384]{0:T(512)S(1)} %pad_add_fusion.2), channel_id=1, source_target_pairs={{0,1},{1,2},{2,3},{3,0},{4,5},{5,6},{6,7},{7,4},{8,9},{9,10},{10,1... | collective-permute-start | bytes 4616 | tf_op jit(solution)/shard_map/ppermute | solution.py:172
  70.0 4.6 %collective-permute-start.1 = (s32[384]{0:T(512)S(1)}, s32[384]{0:T(512)}, u32[]{:S(2)}, u32[]{:S(2)}) collective-permute-start(s32[384]{0:T(512)S(1)} %pad_add_fusion.2), channel_id=1, source_target_pairs={{0,2},{1,3},{2,0},{3,1},{4,6},{5,7},{6,4},{7,5},{8,10},{9,11},{10,... | collective-permute-start | bytes 4616 | tf_op jit(solution)/shard_map/ppermute | solution.py:172
  74.7 3.3 %collective-permute-start.2 = (s32[384]{0:T(512)S(1)}, s32[384]{0:T(512)}, u32[]{:S(2)}, u32[]{:S(2)}) collective-permute-start(s32[384]{0:T(512)S(1)} %pad_add_fusion.2), channel_id=1, source_target_pairs={{0,3},{1,0},{2,1},{3,2},{4,7},{5,4},{6,5},{7,6},{8,11},{9,8},{10,9... | collective-permute-start | bytes 4616 | tf_op jit(solution)/shard_map/ppermute | solution.py:172
  78.2 1.2 fusion.48
  79.4 1.6 cosine_convert_fusion.2
  81.0 1.1 reshape.116
  82.1 2.0 multiply_convert_fusion
  84.9 0.8 reshape.117
  85.7 13.7 %all-to-all-start.2 = ((bf16[128,2,512]{2,1,0:T(2,128)(2,1)}), bf16[128,2,512]{2,1,0:T(2,128)(2,1)S(1)}, u32[]{:S(2)}, u32[]{:S(2)}) async-start(bf16[128,2,512]{2,1,0:T(2,128)(2,1)} %reshape.117), calls=%async_computation.2 | async-start | bytes 524288 | tf_op jit(solution)/shard_map/all_to_all | solution.py:160
  99.5 1.3 constant_dynamic-update-slice_fusion.9
  100.8 0.9 slice.104
  102.4 1.3 constant_dynamic-update-slice_fusion.8
  103.7 1.3 constant_dynamic-update-slice_fusion.7
  105.0 1.3 constant_dynamic-update-slice_fusion.6
  106.3 1.1 convert_reduce_fusion
  107.4 3.5 %all-to-all-done.2 = bf16[128,2,512]{2,1,0:T(2,128)(2,1)S(1)} async-done(((bf16[128,2,512]{2,1,0:T(2,128)(2,1)}), bf16[128,2,512]{2,1,0:T(2,128)(2,1)S(1)}, u32[]{:S(2)}, u32[]{:S(2)}) %all-to-all-start.2) | async-done | bytes 262176 | tf_op jit(solution)/shard_map/all_to_all | solution.py:160
  110.9 1.0 gather_fusion.3
  111.9 1.0 fusion.61
  113.0 2.5 collective-permute-start.3
  115.5 2.8 collective-permute-start.4
  118.3 3.7 %collective-permute-start.5 = (bf16[384,512]{1,0:T(8,128)(2,1)S(1)}, bf16[384,512]{1,0:T(8,128)(2,1)S(1)}, u32[]{:S(2)}, u32[]{:S(2)}) collective-permute-start(bf16[384,512]{1,0:T(8,128)(2,1)S(1)} %pad_maximum_fusion), channel_id=1, source_target_pairs={{0,3},{1,0},{2,1},{3,2},{4,7},{5,4},{6,5},{7,6},{8,11},{9,8},{10,9... | collective-permute-start | bytes 1179656 | tf_op jit(solution)/shard_map/ppermute | solution.py:171
  122.0 13.6 %collective-permute-done.3 = bf16[384,512]{1,0:T(8,128)(2,1)S(1)} collective-permute-done((bf16[384,512]{1,0:T(8,128)(2,1)S(1)}, bf16[384,512]{1,0:T(8,128)(2,1)S(1)}, u32[]{:S(2)}, u32[]{:S(2)}) %collective-permute-start.3) | collective-permute-done | bytes 393248 | tf_op jit(solution)/shard_map/ppermute | solution.py:171
  135.7 2.5 collective-permute-done.5
  138.2 1.0 fusion.6
  139.3 1.8 convolution_bitcast_fusion.1
  141.2 1.0 fusion.59
  142.1 14.3 %all_gather.3 = bf16[512,512]{1,0:T(8,128)(2,1)S(1)} all-gather(bf16[512,128]{1,0:T(8,128)(2,1)S(1)} %get-tuple-element.6), channel_id=1, replica_groups=mesh['nodes'=128,'rep'=4] {'rep'}, dimensions={1}, use_global_device_ids=true | all-gather | bytes 655360 | tf_op jit(solution)/shard_map/all_gather | solution.py:192
  156.5 3.9 %fusion.1 = bf16[4096,512]{1,0:T(8,128)(2,1)} fusion(bf16[512,512]{1,0:T(8,128)(2,1)S(1)} %all_gather.3, s32[4096]{0:T(1024)S(1)} %copy-done.6), kind=kOutput, calls=%fused_computation.12 | convolution fusion | flops 2151677952 | bytes 4734976 | tf_op jit(solution)/shard_map/dot_general | solution.py:26
  160.4 11.0 %all-to-all-start.3 = ((bf16[128,32,512]{2,1,0:T(8,128)(2,1)}), bf16[128,32,512]{2,1,0:T(8,128)(2,1)}, u32[]{:S(2)}, u32[]{:S(2)}) async-start(bf16[128,32,512]{2,1,0:T(8,128)(2,1)} %bitcast.115), calls=%async_computation.3 | async-start | bytes 8388608 | tf_op jit(solution)/shard_map/all_to_all | solution.py:194
  171.8 4.7 %cosine_convert_fusion.tenc_ref = bf16[2048,128]{1,0:T(8,128)(2,1)} fusion(f32[128]{0:T(128)S(1)} %copy-done.18, f32[128]{0:T(128)S(1)} %copy-done.19, f32[2048]{0:T(1024)S(1)} %mul.108), kind=kLoop, calls=%fused_computation.39 | loop fusion | flops 786432 | bytes 533504 | tf_op jit(solution)/shard_map/convert_element_type | solution.py:197
  176.4 1.0 gather_fusion.5
  177.4 0.9 convolution_convert_fusion.q_ref
  178.3 95.6 %all-to-all-done.3 = bf16[128,32,512]{2,1,0:T(8,128)(2,1)} async-done(((bf16[128,32,512]{2,1,0:T(8,128)(2,1)}), bf16[128,32,512]{2,1,0:T(8,128)(2,1)}, u32[]{:S(2)}, u32[]{:S(2)}) %all-to-all-start.3) | async-done | bytes 4194336 | tf_op jit(solution)/shard_map/all_to_all | solution.py:194
  273.9 12.0 %gather_fusion.4 = bf16[2048,512]{1,0:T(8,128)(2,1)} fusion(bf16[4096,512]{1,0:T(8,128)(2,1)} %bitcast.28, s32[2048]{0:T(1024)S(1)} %broadcast_clamp_fusion), kind=kCustom, calls=%fused_computation.5 | custom fusion | bytes 4202496 | tf_op jit(solution)/shard_map/gather | solution.py:195
  285.9 20.8 %shard_map.185 = bf16[128,512]{1,0:T(8,128)(2,1)} custom-call(bf16[2048,512]{1,0:T(8,128)(2,1)} %gather_fusion.4, bf16[2048,128]{1,0:T(8,128)(2,1)} %cosine_convert_fusion.tenc_ref, bf16[128,512]{1,0:T(8,128)(2,1)} %convolution_convert_fusion.q_ref, bf16[512,1024]{1,0:T(8,128)(2,1)} %wm_ref.1, bf16[128,1024]{1,0:T(8,128)(2,1)} %wt_ref.1), custom_call_target="tpu_custom_call" | custom-call | tf_op jit(solution)/shard_map/pallas_call | solution.py:63
  (106 shorter events, 10.3 us)
Async XLA Ops:
  0.6 81.5 %copy-start = (bf16[1152,512]{1,0:T(8,128)(2,1)S(1)}, bf16[1152,512]{1,0:T(8,128)(2,1)}, u32[]{:S(2)}) copy-start(bf16[1152,512]{1,0:T(8,128)(2,1)} %param.29) | copy-start | bytes 3538948
  3.2 0.7 copy-start.7
  3.2 9.7 %copy-start.12 = (s32[128,1]{0,1:T(1,128)S(1)}, s32[128,1]{0,1:T(1,128)}, u32[]{:S(2)}) copy-start(s32[128,1]{0,1:T(1,128)} %param.21) | copy-start | bytes 1540
  3.2 10.1 %copy-start.21 = (s32[128]{0:T(128)S(1)}, s32[128]{0:T(128)}, u32[]{:S(2)}) copy-start(s32[128]{0:T(128)} %param.20) | copy-start | bytes 1540
  3.2 11.5 %copy-start.1 = (s32[512]{0:T(512)S(1)}, s32[512]{0:T(512)}, u32[]{:S(2)}) copy-start(s32[512]{0:T(512)} %param.19) | copy-start | bytes 6148
  3.9 12.1 %copy-start.20 = (s32[128]{0:T(128)S(1)}, s32[128]{0:T(128)}, u32[]{:S(2)}) copy-start(s32[128]{0:T(128)} %param.22) | copy-start | bytes 1540
  3.9 12.1 %copy-start.22 = (s32[128]{0:T(128)S(1)}, s32[128]{0:T(128)}, u32[]{:S(2)}) copy-start(s32[128]{0:T(128)} %param.23) | copy-start | bytes 1540
  3.9 31.4 %copy-start.17 = (f32[4,128]{1,0:T(4,128)S(1)}, f32[4,128]{1,0:T(4,128)}, u32[]{:S(2)}) copy-start(f32[4,128]{1,0:T(4,128)} %param.32) | copy-start | bytes 6148
  3.9 32.0 %copy-start.2 = (f32[512,512]{1,0:T(8,128)S(1)}, f32[512,512]{1,0:T(8,128)}, u32[]{:S(2)}) copy-start(f32[512,512]{1,0:T(8,128)} %param.18) | copy-start | bytes 3145732
  13.4 25.5 %copy-start.24 = (s32[128]{0:T(128)}, s32[128]{0:T(128)S(1)}, u32[]{:S(2)}) copy-start(s32[128]{0:T(128)S(1)} %fusion.57) | copy-start | bytes 1540
  14.7 24.9 %copy-start.10 = (s32[1024]{0:T(1024)}, s32[1024]{0:T(1024)S(1)}, u32[]{:S(2)}) copy-start(s32[1024]{0:T(1024)S(1)} %pad_clamp_fusion.2) | copy-start | bytes 12292
  17.8 25.9 %all-to-all-start = ((s32[128,1,38]{2,1,0:T(1,128)}), s32[128,1,38]{2,1,0:T(1,128)}, u32[]{:S(2)}, u32[]{:S(2)}) async-start(s32[128,1,38]{2,1,0:T(1,128)} %bitcast.12), calls=%async_computation | async-start | bytes 131072 | tf_op jit(solution)/shard_map/all_to_all | solution.py:133
  43.8 37.2 %all-to-all-start.1 = ((bf16[128,2,512]{2,1,0:T(2,128)(2,1)}), bf16[128,2,512]{2,1,0:T(2,128)(2,1)}, u32[]{:S(2)}, u32[]{:S(2)}) async-start(bf16[128,2,512]{2,1,0:T(2,128)(2,1)} %reshape.115), calls=%async_computation.1 | async-start | bytes 524288 | tf_op jit(solution)/shard_map/all_to_all | solution.py:134
  63.8 14.2 %copy-start.11 = (s32[256]{0:T(256)S(1)}, s32[256]{0:T(256)}, u32[]{:S(2)}) copy-start(s32[256]{0:T(256)} %gather_fusion.2) | copy-start | bytes 3076
  66.6 35.8 %collective-permute-start = (s32[384]{0:T(512)S(1)}, s32[384]{0:T(512)}, u32[]{:S(2)}, u32[]{:S(2)}) collective-permute-start(s32[384]{0:T(512)S(1)} %pad_add_fusion.2), channel_id=1, source_target_pairs={{0,1},{1,2},{2,3},{3,0},{4,5},{5,6},{6,7},{7,4},{8,9},{9,10},{10,1... | collective-permute-start | bytes 4616 | tf_op jit(solution)/shard_map/ppermute | solution.py:172
  70.0 33.7 %collective-permute-start.1 = (s32[384]{0:T(512)S(1)}, s32[384]{0:T(512)}, u32[]{:S(2)}, u32[]{:S(2)}) collective-permute-start(s32[384]{0:T(512)S(1)} %pad_add_fusion.2), channel_id=1, source_target_pairs={{0,2},{1,3},{2,0},{3,1},{4,6},{5,7},{6,4},{7,5},{8,10},{9,11},{10,... | collective-permute-start | bytes 4616 | tf_op jit(solution)/shard_map/ppermute | solution.py:172
  74.7 30.3 %collective-permute-start.2 = (s32[384]{0:T(512)S(1)}, s32[384]{0:T(512)}, u32[]{:S(2)}, u32[]{:S(2)}) collective-permute-start(s32[384]{0:T(512)S(1)} %pad_add_fusion.2), channel_id=1, source_target_pairs={{0,3},{1,0},{2,1},{3,2},{4,7},{5,4},{6,5},{7,6},{8,11},{9,8},{10,9... | collective-permute-start | bytes 4616 | tf_op jit(solution)/shard_map/ppermute | solution.py:172
  84.1 0.8 copy-start.4
  85.7 25.1 %all-to-all-start.2 = ((bf16[128,2,512]{2,1,0:T(2,128)(2,1)}), bf16[128,2,512]{2,1,0:T(2,128)(2,1)S(1)}, u32[]{:S(2)}, u32[]{:S(2)}) async-start(bf16[128,2,512]{2,1,0:T(2,128)(2,1)} %reshape.117), calls=%async_computation.2 | async-start | bytes 524288 | tf_op jit(solution)/shard_map/all_to_all | solution.py:160
  112.9 25.2 %copy-start.8 = (s32[1536]{0:T(1024)S(1)}, s32[1536]{0:T(1024)}, u32[]{:S(2)}) copy-start(s32[1536]{0:T(1024)} %constant_dynamic-update-slice_fusion.6) | copy-start | bytes 18436
  113.0 22.6 %collective-permute-start.3 = (bf16[384,512]{1,0:T(8,128)(2,1)S(1)}, bf16[384,512]{1,0:T(8,128)(2,1)S(1)}, u32[]{:S(2)}, u32[]{:S(2)}) collective-permute-start(bf16[384,512]{1,0:T(8,128)(2,1)S(1)} %pad_maximum_fusion), channel_id=1, source_target_pairs={{0,1},{1,2},{2,3},{3,0},{4,5},{5,6},{6,7},{7,4},{8,9},{9,10},{10,1... | collective-permute-start | bytes 1179656 | tf_op jit(solution)/shard_map/ppermute | solution.py:171
  115.5 20.1 %collective-permute-start.4 = (bf16[384,512]{1,0:T(8,128)(2,1)S(1)}, bf16[384,512]{1,0:T(8,128)(2,1)S(1)}, u32[]{:S(2)}, u32[]{:S(2)}) collective-permute-start(bf16[384,512]{1,0:T(8,128)(2,1)S(1)} %pad_maximum_fusion), channel_id=1, source_target_pairs={{0,2},{1,3},{2,0},{3,1},{4,6},{5,7},{6,4},{7,5},{8,10},{9,11},{10,... | collective-permute-start | bytes 1179656 | tf_op jit(solution)/shard_map/ppermute | solution.py:171
  118.3 19.8 %collective-permute-start.5 = (bf16[384,512]{1,0:T(8,128)(2,1)S(1)}, bf16[384,512]{1,0:T(8,128)(2,1)S(1)}, u32[]{:S(2)}, u32[]{:S(2)}) collective-permute-start(bf16[384,512]{1,0:T(8,128)(2,1)S(1)} %pad_maximum_fusion), channel_id=1, source_target_pairs={{0,3},{1,0},{2,1},{3,2},{4,7},{5,4},{6,5},{7,6},{8,11},{9,8},{10,9... | collective-permute-start | bytes 1179656 | tf_op jit(solution)/shard_map/ppermute | solution.py:171
  138.2 1.1 copy-start.3
  139.3 1.8 copy-start.13
  139.3 1.9 copy-start.14
  139.3 1.9 copy-start.15
  139.3 1.9 copy-start.16
  141.1 15.3 %copy-start.6 = (s32[4096]{0:T(1024)S(1)}, s32[4096]{0:T(1024)}, u32[]{:S(2)}) copy-start(s32[4096]{0:T(1024)} %eq.83) | copy-start | bytes 49156
  160.4 11.1 %copy-start.23 = (s32[128]{0:T(128)S(1)}, s32[128]{0:T(128)}, u32[]{:S(2)}) copy-start(s32[128]{0:T(128)} %param.23) | copy-start | bytes 1540
  160.4 11.1 %copy-start.9 = (s32[128,16]{0,1:T(8,128)S(1)}, s32[128,16]{0,1:T(8,128)}, u32[]{:S(2)}) copy-start(s32[128,16]{0,1:T(8,128)} %param.26) | copy-start | bytes 24580
  160.4 11.3 %copy-start.18 = (f32[128]{0:T(128)S(1)}, f32[128]{0:T(128)}, u32[]{:S(2)}) copy-start(f32[128]{0:T(128)} %param.28) | copy-start | bytes 1540
  160.4 11.3 %copy-start.19 = (f32[128]{0:T(128)S(1)}, f32[128]{0:T(128)}, u32[]{:S(2)}) copy-start(f32[128]{0:T(128)} %param.27) | copy-start | bytes 1540
  160.4 113.5 %all-to-all-start.3 = ((bf16[128,32,512]{2,1,0:T(8,128)(2,1)}), bf16[128,32,512]{2,1,0:T(8,128)(2,1)}, u32[]{:S(2)}, u32[]{:S(2)}) async-start(bf16[128,32,512]{2,1,0:T(8,128)(2,1)} %bitcast.115), calls=%async_computation.3 | async-start | bytes 8388608 | tf_op jit(solution)/shard_map/all_to_all | solution.py:194
  171.5 5.9 %copy-start.5 = (bf16[512,512]{1,0:T(8,128)(2,1)S(1)}, bf16[512,512]{1,0:T(8,128)(2,1)}, u32[]{:S(2)}) copy-start(bf16[512,512]{1,0:T(8,128)(2,1)} %param.33) | copy-start | bytes 1572868

commit v3 on v2

--- a/solution.py
+++ b/solution.py
@@ -18,7 +18,23 @@
 def place(owner, groups, capacity):
     onehot = (owner[:, None] == jnp.arange(groups, dtype=jnp.int32)[None, :]).astype(jnp.int32)
     before = jnp.cumsum(onehot, axis=0) - onehot
-    return owner * capacity + jnp.sum(before * onehot, axis=1)
+    rank = jnp.sum(before * onehot, axis=1)
+    return owner * capacity + rank, onehot, rank
+
+
+def split_pairs(v):
+    return (v // 32).astype(jnp.bfloat16), (v % 32).astype(jnp.bfloat16)
+
+
+def scatter_ids(onehot, rank, values, capacity):
+    hi, lo = split_pairs(values + 1)
+    at_rank = rank[:, None] == jnp.arange(capacity, dtype=jnp.int32)[None, :]
+    cols = jnp.concatenate(
+        [jnp.where(at_rank, hi[:, None], 0.0), jnp.where(at_rank, lo[:, None], 0.0)], axis=1
+    ).astype(jnp.bfloat16)
+    table = jnp.dot(onehot.T.astype(jnp.bfloat16), cols, preferred_element_type=jnp.float32)
+    table = table.astype(jnp.int32)
+    return table[:, :capacity] * 32 + table[:, capacity:] - 1
 
 
 def select_rows(ids, table):
@@ -103,8 +119,8 @@
     neighbours = nbr_local.shape[1]
     dst_cap = max(2, 2 * events // groups)
     nbr_cap = 2 * events * neighbours // groups
-    dst_slot = place(dst_owner[:, 0], groups, dst_cap)
-    nbr_slot = place(nbr_owner.reshape(-1), groups, nbr_cap)
+    dst_slot, _, _ = place(dst_owner[:, 0], groups, dst_cap)
+    nbr_slot, nbr_hot, nbr_rank = place(nbr_owner.reshape(-1), groups, nbr_cap)
     mem_half = memory.astype(jnp.bfloat16)
     near_rows = mem_half[src_local]
     near_ticks = last_tick[src_local]
@@ -117,12 +133,7 @@
         .set(req)
         .reshape(groups, dst_cap * 3)
     )
-    nbr_ids = (
-        jnp.full((groups * nbr_cap,), -1, jnp.int32)
-        .at[nbr_slot]
-        .set(nbr_local.reshape(-1))
-        .reshape(groups, nbr_cap)
-    )
+    nbr_ids = scatter_ids(nbr_hot, nbr_rank, nbr_local.reshape(-1), nbr_cap)
     req_rows = (
         jnp.zeros((groups * dst_cap, width_m), jnp.bfloat16)
         .at[dst_slot]
@@ -164,14 +175,21 @@
 
     local_msgs = jnp.concatenate([msg_src, msg_dst], axis=0)
     local_ids = jnp.concatenate([src_local, got_dst], axis=0)
-    all_msgs = [local_msgs]
-    all_ids = [local_ids]
+    id_hi, id_lo = split_pairs(local_ids + 1)
+    id_rows = -(-2 * local_ids.shape[0] // width_m)
+    id_rows = -(-id_rows // 16) * 16
+    id_block = jnp.concatenate(
+        [id_hi, id_lo, jnp.zeros((id_rows * width_m - 2 * local_ids.shape[0],), jnp.bfloat16)]
+    ).reshape(id_rows, width_m)
+    payload = jnp.concatenate([local_msgs, id_block], axis=0)
+    parts = [payload]
     for shift in range(1, reps):
         pairs = [(i, (i + shift) % reps) for i in range(reps)]
-        all_msgs.append(lax.ppermute(local_msgs, "rep", pairs))
-        all_ids.append(lax.ppermute(local_ids, "rep", pairs))
-    all_msgs = jnp.concatenate(all_msgs, axis=0)
-    all_ids = jnp.concatenate(all_ids, axis=0)
+        parts.append(lax.ppermute(payload, "rep", pairs))
+    count = local_msgs.shape[0]
+    all_msgs = jnp.concatenate([p[:count] for p in parts], axis=0)
+    coded = jnp.stack([p[count:].reshape(-1)[: 2 * count] for p in parts]).astype(jnp.int32)
+    all_ids = (coded[:, :count] * 32 + coded[:, count:] - 1).reshape(-1)
     row_ids = jnp.arange(rows_here, dtype=jnp.int32)[:, None]
     hits = row_ids == all_ids[None, :]
     sums = jnp.dot(hits.astype(jnp.bfloat16), all_msgs, preferred_element_type=jnp.float32)

time: 308 us -> 287 us (0.932)
  the two profiles are of different devices: /device:TPU:32 before, /device:TPU:34 now
where the time goes in v3:
time: 287 us; the launch traced here: 286 us
  waiting for transfers between devices  131 us (46%)
  starting transfers between devices  57.6 us (20%)
  local copies, waits for them, and re-layouts  33.6 us (12%)
  Pallas kernels  20.8 us (7%)
  blocking collectives  15.8 us (6%)
  matrix products  13.4 us (5%)
  other arithmetic  12.9 us (4%)
    all_to_all x1, waiting for transfers between devices, on_device(): lax.all_to_all(served, 'nodes', split_axis=0, concat_axis=0, tiled=True)  95.5 us
    pallas_call x1, Pallas kernels, attend(): pl.pallas_call(attend_kernel, grid=(events // block,), in_specs=[pl.Block...  20.8 us
    all_to_all x1, starting transfers between devices, on_device(): lax.all_to_all(ints_out, 'nodes', split_axis=0, concat_axis=0, tiled=True)  17 us
    all_gather x1, blocking collectives, on_device(): lax.all_gather(new_part.astype(jnp.bfloat16), 'rep', axis=1, tiled=True)  15.8 us
    ppermute x3, waiting for transfers between devices, on_device(): parts.append(lax.ppermute(payload, 'rep', pairs))  13.9 us
    gather x1, local copies, waits for them, and re-layouts, on_device(): fetched = returned.reshape(-1, updated.shape[1])[nbr_slot]  12 us
    all_to_all x1, waiting for transfers between devices, on_device(): lax.all_to_all(msg_src_slots.reshape(groups, dst_cap, -1), 'nodes', split...  11.3 us
    all_to_all x1, starting transfers between devices, on_device(): lax.all_to_all(served, 'nodes', split_axis=0, concat_axis=0, tiled=True)  10.8 us
  transfers between devices with their start and end apart: 7, of which 7 were waited for; matrix products, arithmetic and copies ran while one was open for 7% of the time, Pallas kernels for 0%

profile of v3, /device:TPU:34, one launch (start us, length us, event | category | flops | bytes accessed | tf_op | source)
XLA Modules:
  0.0 286.3 jit_solution(68259541223645683)
XLA Ops:
  0.6 0.9 copy.50
  3.2 0.6 fusion.20
  3.9 1.6 fusion.23
  6.7 1.3 gather_fusion
  8.1 0.9 scatter_custom_fusion
  9.2 0.8 copy.56
  9.9 17.0 %all-to-all-start = ((s32[128,1,38]{2,1,0:T(1,128)}), s32[128,1,38]{2,1,0:T(1,128)S(1)}, u32[]{:S(2)}, u32[]{:S(2)}) async-start(s32[128,1,38]{2,1,0:T(1,128)} %copy.56), calls=%async_computation | async-start | bytes 131072 | tf_op jit(solution)/shard_map/all_to_all | solution.py:144
  27.1 1.7 scatter_custom_fusion.1
  28.8 0.8 reshape.159
  29.6 4.8 %all-to-all-done = s32[128,1,38]{2,1,0:T(1,128)S(1)} async-done(((s32[128,1,38]{2,1,0:T(1,128)}), s32[128,1,38]{2,1,0:T(1,128)S(1)}, u32[]{:S(2)}, u32[]{:S(2)}) %all-to-all-start) | async-done | bytes 19488 | tf_op jit(solution)/shard_map/all_to_all | solution.py:144
  34.3 9.8 %all-to-all-start.1 = ((bf16[128,2,512]{2,1,0:T(2,128)(2,1)}), bf16[128,2,512]{2,1,0:T(2,128)(2,1)S(1)}, u32[]{:S(2)}, u32[]{:S(2)}) async-start(bf16[128,2,512]{2,1,0:T(2,128)(2,1)} %reshape.159), calls=%async_computation.1 | async-start | bytes 524288 | tf_op jit(solution)/shard_map/all_to_all | solution.py:145
  44.3 0.7 slice_reduce_fusion
  45.0 1.9 gather_fusion.2
  46.9 1.2 gather_fusion.1
  48.5 1.8 cosine_convert_fusion.2
  50.3 5.3 %all-to-all-done.1 = bf16[128,2,512]{2,1,0:T(2,128)(2,1)S(1)} async-done(((bf16[128,2,512]{2,1,0:T(2,128)(2,1)}), bf16[128,2,512]{2,1,0:T(2,128)(2,1)S(1)}, u32[]{:S(2)}, u32[]{:S(2)}) %all-to-all-start.1) | async-done | bytes 262176 | tf_op jit(solution)/shard_map/all_to_all | solution.py:145
  55.7 1.8 multiply_convert_fusion
  57.6 0.8 reshape.161
  58.4 9.5 %all-to-all-start.2 = ((bf16[128,2,512]{2,1,0:T(2,128)(2,1)}), bf16[128,2,512]{2,1,0:T(2,128)(2,1)S(1)}, u32[]{:S(2)}, u32[]{:S(2)}) async-start(bf16[128,2,512]{2,1,0:T(2,128)(2,1)} %reshape.161), calls=%async_computation.2 | async-start | bytes 524288 | tf_op jit(solution)/shard_map/all_to_all | solution.py:171
  68.0 11.3 %all-to-all-done.2 = bf16[128,2,512]{2,1,0:T(2,128)(2,1)S(1)} async-done(((bf16[128,2,512]{2,1,0:T(2,128)(2,1)}), bf16[128,2,512]{2,1,0:T(2,128)(2,1)S(1)}, u32[]{:S(2)}, u32[]{:S(2)}) %all-to-all-start.2) | async-done | bytes 262176 | tf_op jit(solution)/shard_map/all_to_all | solution.py:171
  79.5 0.8 gather_fusion.3
  80.3 0.7 constant_dynamic-update-slice_fusion.1
  81.0 0.7 fusion.75
  81.7 0.8 pad_maximum_fusion
  82.5 2.4 collective-permute-start.2
  84.9 1.8 convolution_bitcast_fusion
  86.8 4.3 %collective-permute-start.1 = (bf16[400,512]{1,0:T(8,128)(2,1)}, bf16[400,512]{1,0:T(8,128)(2,1)}, u32[]{:S(2)}, u32[]{:S(2)}) collective-permute-start(bf16[400,512]{1,0:T(8,128)(2,1)} %pad_maximum_fusion), channel_id=1, source_target_pairs={{0,2},{1,3},{2,0},{3,1},{4,6},{5,7},{6,4},{7,5},{8,10},{9,11},{10,... | collective-permute-start | bytes 1228808 | tf_op jit(solution)/shard_map/ppermute | solution.py:188
  91.3 3.7 %collective-permute-start = (bf16[400,512]{1,0:T(8,128)(2,1)}, bf16[400,512]{1,0:T(8,128)(2,1)S(1)}, u32[]{:S(2)}, u32[]{:S(2)}) collective-permute-start(bf16[400,512]{1,0:T(8,128)(2,1)} %pad_maximum_fusion), channel_id=1, source_target_pairs={{0,1},{1,2},{2,3},{3,0},{4,5},{5,6},{6,7},{7,4},{8,9},{9,10},{10,1... | collective-permute-start | bytes 1228808 | tf_op jit(solution)/shard_map/ppermute | solution.py:188
  95.0 1.1 collective-permute-done.2
  96.1 0.7 slice_bitcast_fusion.2
  96.9 9.0 %collective-permute-done.1 = bf16[400,512]{1,0:T(8,128)(2,1)} collective-permute-done((bf16[400,512]{1,0:T(8,128)(2,1)}, bf16[400,512]{1,0:T(8,128)(2,1)}, u32[]{:S(2)}, u32[]{:S(2)}) %collective-permute-start.1) | collective-permute-done | bytes 409632 | tf_op jit(solution)/shard_map/ppermute | solution.py:188
  105.8 0.7 slice_bitcast_fusion.3
  106.6 3.8 %collective-permute-done = bf16[400,512]{1,0:T(8,128)(2,1)S(1)} collective-permute-done((bf16[400,512]{1,0:T(8,128)(2,1)}, bf16[400,512]{1,0:T(8,128)(2,1)S(1)}, u32[]{:S(2)}, u32[]{:S(2)}) %collective-permute-start) | collective-permute-done | bytes 409632 | tf_op jit(solution)/shard_map/ppermute | solution.py:188
  110.9 0.8 slice_dynamic-update-slice_fusion.2
  111.7 1.8 slice_dynamic-update-slice_fusion.1
  113.5 1.8 slice_dynamic-update-slice_fusion
  115.3 2.5 fusion.6
  117.7 1.8 convolution_bitcast_fusion.1
  119.6 0.9 fusion.73
  120.5 15.8 %all_gather.3 = bf16[512,512]{1,0:T(8,128)(2,1)S(1)} all-gather(bf16[512,128]{1,0:T(8,128)(2,1)S(1)} %get-tuple-element.6), channel_id=1, replica_groups=mesh['nodes'=128,'rep'=4] {'rep'}, dimensions={1}, use_global_device_ids=true | all-gather | bytes 655360 | tf_op jit(solution)/shard_map/all_gather | solution.py:210
  136.3 4.0 %fusion.1 = bf16[4096,512]{1,0:T(8,128)(2,1)} fusion(bf16[512,512]{1,0:T(8,128)(2,1)S(1)} %all_gather.3, s32[4096]{0:T(1024)S(1)} %eq.116), kind=kOutput, calls=%fused_computation.11 | convolution fusion | flops 2151677952 | bytes 4734976 | tf_op jit(solution)/shard_map/dot_general | solution.py:42
  140.3 10.8 %all-to-all-start.3 = ((bf16[128,32,512]{2,1,0:T(8,128)(2,1)}), bf16[128,32,512]{2,1,0:T(8,128)(2,1)}, u32[]{:S(2)}, u32[]{:S(2)}) async-start(bf16[128,32,512]{2,1,0:T(8,128)(2,1)} %bitcast.123), calls=%async_computation.3 | async-start | bytes 8388608 | tf_op jit(solution)/shard_map/all_to_all | solution.py:212
  151.6 4.7 %cosine_convert_fusion.tenc_ref = bf16[2048,128]{1,0:T(8,128)(2,1)} fusion(f32[128]{0:T(128)S(1)} %copy-done.14, f32[128]{0:T(128)S(1)} %copy-done.15, f32[2048]{0:T(1024)S(1)} %mul.121), kind=kLoop, calls=%fused_computation.39 | loop fusion | flops 786432 | bytes 533504 | tf_op jit(solution)/shard_map/convert_element_type | solution.py:215
  156.3 0.8 gather_fusion.5
  157.1 0.9 convolution_convert_fusion.q_ref
  158.0 95.5 %all-to-all-done.3 = bf16[128,32,512]{2,1,0:T(8,128)(2,1)} async-done(((bf16[128,32,512]{2,1,0:T(8,128)(2,1)}), bf16[128,32,512]{2,1,0:T(8,128)(2,1)}, u32[]{:S(2)}, u32[]{:S(2)}) %all-to-all-start.3) | async-done | bytes 4194336 | tf_op jit(solution)/shard_map/all_to_all | solution.py:212
  253.6 12.0 %gather_fusion.4 = bf16[2048,512]{1,0:T(8,128)(2,1)} fusion(bf16[4096,512]{1,0:T(8,128)(2,1)} %bitcast.25, s32[2048]{0:T(1024)S(1)} %broadcast_clamp_fusion), kind=kCustom, calls=%fused_computation.5 | custom fusion | bytes 4202496 | tf_op jit(solution)/shard_map/gather | solution.py:213
  265.5 20.8 %shard_map.185 = bf16[128,512]{1,0:T(8,128)(2,1)} custom-call(bf16[2048,512]{1,0:T(8,128)(2,1)} %gather_fusion.4, bf16[2048,128]{1,0:T(8,128)(2,1)} %cosine_convert_fusion.tenc_ref, bf16[128,512]{1,0:T(8,128)(2,1)} %convolution_convert_fusion.q_ref, bf16[512,1024]{1,0:T(8,128)(2,1)} %wm_ref.1, bf16[128,1024]{1,0:T(8,128)(2,1)} %wt_ref.1), custom_call_target="tpu_custom_call" | custom-call | tf_op jit(solution)/shard_map/pallas_call | solution.py:79
  (116 shorter events, 5.0 us)
Async XLA Ops:
  0.6 55.1 %copy-start = (bf16[1152,512]{1,0:T(8,128)(2,1)S(1)}, bf16[1152,512]{1,0:T(8,128)(2,1)}, u32[]{:S(2)}) copy-start(bf16[1152,512]{1,0:T(8,128)(2,1)} %param.29) | copy-start | bytes 3538948
  2.3 0.7 copy-start.9
  3.2 3.0 %copy-start.12 = (s32[128,1]{0,1:T(1,128)S(1)}, s32[128,1]{0,1:T(1,128)}, u32[]{:S(2)}) copy-start(s32[128,1]{0,1:T(1,128)} %param.21) | copy-start | bytes 1540
  3.2 3.4 %copy-start.17 = (s32[128]{0:T(128)S(1)}, s32[128]{0:T(128)}, u32[]{:S(2)}) copy-start(s32[128]{0:T(128)} %param.20) | copy-start | bytes 1540
  3.2 3.5 %copy-start.1 = (s32[512]{0:T(512)S(1)}, s32[512]{0:T(512)}, u32[]{:S(2)}) copy-start(s32[512]{0:T(512)} %param.19) | copy-start | bytes 6148
  3.9 4.1 %copy-start.16 = (s32[128]{0:T(128)S(1)}, s32[128]{0:T(128)}, u32[]{:S(2)}) copy-start(s32[128]{0:T(128)} %param.22) | copy-start | bytes 1540
  3.9 4.1 %copy-start.19 = (s32[128]{0:T(128)S(1)}, s32[128]{0:T(128)}, u32[]{:S(2)}) copy-start(s32[128]{0:T(128)} %param.23) | copy-start | bytes 1540
  5.5 21.5 %copy-start.2 = (f32[512,512]{1,0:T(8,128)S(1)}, f32[512,512]{1,0:T(8,128)}, u32[]{:S(2)}) copy-start(f32[512,512]{1,0:T(8,128)} %param.18) | copy-start | bytes 3145732
  6.6 22.9 %copy-start.21 = (s32[128]{0:T(128)}, s32[128]{0:T(128)S(1)}, u32[]{:S(2)}) copy-start(s32[128]{0:T(128)S(1)} %fusion.70) | copy-start | bytes 1540
  9.9 24.4 %all-to-all-start = ((s32[128,1,38]{2,1,0:T(1,128)}), s32[128,1,38]{2,1,0:T(1,128)S(1)}, u32[]{:S(2)}, u32[]{:S(2)}) async-start(s32[128,1,38]{2,1,0:T(1,128)} %copy.56), calls=%async_computation | async-start | bytes 131072 | tf_op jit(solution)/shard_map/all_to_all | solution.py:144
  34.3 21.3 %all-to-all-start.1 = ((bf16[128,2,512]{2,1,0:T(2,128)(2,1)}), bf16[128,2,512]{2,1,0:T(2,128)(2,1)S(1)}, u32[]{:S(2)}, u32[]{:S(2)}) async-start(bf16[128,2,512]{2,1,0:T(2,128)(2,1)} %reshape.159), calls=%async_computation.1 | async-start | bytes 524288 | tf_op jit(solution)/shard_map/all_to_all | solution.py:145
  57.6 0.9 copy-start.5
  57.6 10.3 %copy-start.22 = (s32[128]{0:T(128)S(1)}, s32[128]{0:T(128)}, u32[]{:S(2)}) copy-start(s32[128]{0:T(128)} %copy-done.21) | copy-start | bytes 1540
  57.6 10.3 %copy-start.11 = (s32[256]{0:T(256)S(1)}, s32[256]{0:T(256)}, u32[]{:S(2)}) copy-start(s32[256]{0:T(256)} %get-tuple-element.2) | copy-start | bytes 3076
  57.6 10.3 %copy-start.18 = (s32[128]{0:T(128)S(1)}, s32[128]{0:T(128)}, u32[]{:S(2)}) copy-start(s32[128]{0:T(128)} %param.20) | copy-start | bytes 1540
  58.4 20.9 %all-to-all-start.2 = ((bf16[128,2,512]{2,1,0:T(2,128)(2,1)}), bf16[128,2,512]{2,1,0:T(2,128)(2,1)S(1)}, u32[]{:S(2)}, u32[]{:S(2)}) async-start(bf16[128,2,512]{2,1,0:T(2,128)(2,1)} %reshape.161), calls=%async_computation.2 | async-start | bytes 524288 | tf_op jit(solution)/shard_map/all_to_all | solution.py:171
  79.5 1.5 copy-start.6
  80.3 4.6 %copy-start.3 = (f32[3,512,128]{2,1,0:T(8,128)S(1)}, f32[3,512,128]{2,1,0:T(8,128)}, u32[]{:S(2)}) copy-start(f32[3,512,128]{2,1,0:T(8,128)} %param.31) | copy-start | bytes 2359300
  81.7 9.4 %copy-start.13 = (f32[4,128]{1,0:T(4,128)S(1)}, f32[4,128]{1,0:T(4,128)}, u32[]{:S(2)}) copy-start(f32[4,128]{1,0:T(4,128)} %param.32) | copy-start | bytes 6148
  82.5 13.6 %collective-permute-start.2 = (bf16[400,512]{1,0:T(8,128)(2,1)}, bf16[400,512]{1,0:T(8,128)(2,1)}, u32[]{:S(2)}, u32[]{:S(2)}) collective-permute-start(bf16[400,512]{1,0:T(8,128)(2,1)} %pad_maximum_fusion), channel_id=1, source_target_pairs={{0,3},{1,0},{2,1},{3,2},{4,7},{5,4},{6,5},{7,6},{8,11},{9,8},{10,9... | collective-permute-start | bytes 1228808 | tf_op jit(solution)/shard_map/ppermute | solution.py:188
  86.8 19.1 %collective-permute-start.1 = (bf16[400,512]{1,0:T(8,128)(2,1)}, bf16[400,512]{1,0:T(8,128)(2,1)}, u32[]{:S(2)}, u32[]{:S(2)}) collective-permute-start(bf16[400,512]{1,0:T(8,128)(2,1)} %pad_maximum_fusion), channel_id=1, source_target_pairs={{0,2},{1,3},{2,0},{3,1},{4,6},{5,7},{6,4},{7,5},{8,10},{9,11},{10,... | collective-permute-start | bytes 1228808 | tf_op jit(solution)/shard_map/ppermute | solution.py:188
  91.3 19.1 %collective-permute-start = (bf16[400,512]{1,0:T(8,128)(2,1)}, bf16[400,512]{1,0:T(8,128)(2,1)S(1)}, u32[]{:S(2)}, u32[]{:S(2)}) collective-permute-start(bf16[400,512]{1,0:T(8,128)(2,1)} %pad_maximum_fusion), channel_id=1, source_target_pairs={{0,1},{1,2},{2,3},{3,0},{4,5},{5,6},{6,7},{7,4},{8,9},{9,10},{10,1... | collective-permute-start | bytes 1228808 | tf_op jit(solution)/shard_map/ppermute | solution.py:188
  115.2 2.5 copy-start.4
  140.3 10.8 %copy-start.20 = (s32[128]{0:T(128)S(1)}, s32[128]{0:T(128)}, u32[]{:S(2)}) copy-start(s32[128]{0:T(128)} %param.23) | copy-start | bytes 1540
  140.3 10.9 %copy-start.8 = (s32[128,16,1]{0,2,1:T(1,128)S(1)}, s32[128,16,1]{0,2,1:T(1,128)}, u32[]{:S(2)}) copy-start(s32[128,16,1]{0,2,1:T(1,128)} %param.24) | copy-start | bytes 24580
  140.3 11.1 %copy-start.10 = (s32[128,16]{0,1:T(8,128)S(1)}, s32[128,16]{0,1:T(8,128)}, u32[]{:S(2)}) copy-start(s32[128,16]{0,1:T(8,128)} %param.26) | copy-start | bytes 24580
  140.3 11.3 %copy-start.14 = (f32[128]{0:T(128)S(1)}, f32[128]{0:T(128)}, u32[]{:S(2)}) copy-start(f32[128]{0:T(128)} %param.28) | copy-start | bytes 1540
  140.3 11.3 %copy-start.15 = (f32[128]{0:T(128)S(1)}, f32[128]{0:T(128)}, u32[]{:S(2)}) copy-start(f32[128]{0:T(128)} %param.27) | copy-start | bytes 1540
  140.3 113.3 %all-to-all-start.3 = ((bf16[128,32,512]{2,1,0:T(8,128)(2,1)}), bf16[128,32,512]{2,1,0:T(8,128)(2,1)}, u32[]{:S(2)}, u32[]{:S(2)}) async-start(bf16[128,32,512]{2,1,0:T(8,128)(2,1)} %bitcast.123), calls=%async_computation.3 | async-start | bytes 8388608 | tf_op jit(solution)/shard_map/all_to_all | solution.py:212
  151.1 6.0 %copy-start.7 = (bf16[512,512]{1,0:T(8,128)(2,1)S(1)}, bf16[512,512]{1,0:T(8,128)(2,1)}, u32[]{:S(2)}) copy-start(bf16[512,512]{1,0:T(8,128)(2,1)} %param.33) | copy-start | bytes 1572868

commit v4 on v3

--- a/solution.py
+++ b/solution.py
@@ -173,23 +173,28 @@
     )
     msg_src = back.reshape(-1, back.shape[2])[dst_slot]
 
-    local_msgs = jnp.concatenate([msg_src, msg_dst], axis=0)
-    local_ids = jnp.concatenate([src_local, got_dst], axis=0)
+    def spread(value):
+        parts = [value]
+        for shift in range(1, reps):
+            pairs = [(i, (i + shift) % reps) for i in range(reps)]
+            parts.append(lax.ppermute(value, "rep", pairs))
+        return parts
+
+    local_ids = jnp.concatenate([got_dst, src_local], axis=0)
     id_hi, id_lo = split_pairs(local_ids + 1)
     id_rows = -(-2 * local_ids.shape[0] // width_m)
     id_rows = -(-id_rows // 16) * 16
     id_block = jnp.concatenate(
         [id_hi, id_lo, jnp.zeros((id_rows * width_m - 2 * local_ids.shape[0],), jnp.bfloat16)]
     ).reshape(id_rows, width_m)
-    payload = jnp.concatenate([local_msgs, id_block], axis=0)
-    parts = [payload]
-    for shift in range(1, reps):
-        pairs = [(i, (i + shift) % reps) for i in range(reps)]
-        parts.append(lax.ppermute(payload, "rep", pairs))
-    count = local_msgs.shape[0]
-    all_msgs = jnp.concatenate([p[:count] for p in parts], axis=0)
-    coded = jnp.stack([p[count:].reshape(-1)[: 2 * count] for p in parts]).astype(jnp.int32)
-    all_ids = (coded[:, :count] * 32 + coded[:, count:] - 1).reshape(-1)
+    early = spread(jnp.concatenate([msg_dst, id_block], axis=0))
+    late = spread(msg_src)
+    count = msg_dst.shape[0]
+    total = local_ids.shape[0]
+    all_msgs = jnp.concatenate([p[:count] for p in early] + late, axis=0)
+    coded = jnp.stack([p[count:].reshape(-1)[: 2 * total] for p in early]).astype(jnp.int32)
+    ids = coded[:, :total] * 32 + coded[:, total:] - 1
+    all_ids = jnp.concatenate([ids[:, :count].reshape(-1), ids[:, count:].reshape(-1)])
     row_ids = jnp.arange(rows_here, dtype=jnp.int32)[:, None]
     hits = row_ids == all_ids[None, :]
     sums = jnp.dot(hits.astype(jnp.bfloat16), all_msgs, preferred_element_type=jnp.float32)

time: 287 us -> 293 us (1.021)
  waiting for transfers between devices: 131 us -> 102 us
  starting transfers between devices: 57.6 us -> 76.2 us
  local copies, waits for them, and re-layouts: 33.6 us -> 44.8 us
  other arithmetic: 12.9 us -> 17.7 us
    ppermute x3 -> x6, waiting for transfers between devices: 13.9 us -> 1.87 us  [spread(): parts.append(lax.ppermute(value, 'rep', pairs))]
    ppermute x3 -> x6, starting transfers between devices: 10.5 us -> 20.2 us  [spread(): parts.append(lax.ppermute(value, 'rep', pairs))]
    all_to_all x1, waiting for transfers between devices: 11.3 us -> 3.97 us  [on_device(): lax.all_to_all(msg_src_slots.reshape(groups, dst_cap, -1), 'nodes', split...]
    all_to_all x1, waiting for transfers between devices: 5.33 us -> 0.29 us  [on_device(): lax.all_to_all(req_rows, 'nodes', split_axis=0, concat_axis=0, tiled=True)]
    all_to_all x1, waiting for transfers between devices: 4.77 us -> 0.2 us  [on_device(): lax.all_to_all(ints_out, 'nodes', split_axis=0, concat_axis=0, tiled=True)]
    all_to_all x1, starting transfers between devices: 9.83 us -> 14 us  [on_device(): lax.all_to_all(req_rows, 'nodes', split_axis=0, concat_axis=0, tiled=True)]
    all_to_all x1, starting transfers between devices: 9.45 us -> 13.4 us  [on_device(): lax.all_to_all(msg_src_slots.reshape(groups, dst_cap, -1), 'nodes', split...]
    unnamed x56 -> x79, local copies, waits for them, and re-layouts: 6.03 us -> 9.38 us
  transfers between devices with their start and end apart: 7 -> 10, of which waited for: 7 -> 5; matrix products, arithmetic and copies ran while one was open for 7% -> 14% of each run, Pallas kernels for 0% -> 0%
where the time goes in v4:
time: 293 us; the launch traced here: 292 us
  waiting for transfers between devices  102 us (35%)
  starting transfers between devices  76.2 us (26%)
  local copies, waits for them, and re-layouts  44.8 us (15%)
  Pallas kernels  20.8 us (7%)
  other arithmetic  17.7 us (6%)
  matrix products  14.8 us (5%)
  blocking collectives  13.9 us (5%)
    all_to_all x1, waiting for transfers between devices, on_device(): lax.all_to_all(served, 'nodes', split_axis=0, concat_axis=0, tiled=True)  95.4 us
    pallas_call x1, Pallas kernels, attend(): pl.pallas_call(attend_kernel, grid=(events // block,), in_specs=[pl.Block...  20.8 us
    ppermute x6, starting transfers between devices, spread(): parts.append(lax.ppermute(value, 'rep', pairs))  20.2 us
    all_to_all x1, starting transfers between devices, on_device(): lax.all_to_all(ints_out, 'nodes', split_axis=0, concat_axis=0, tiled=True)  17.5 us
    all_to_all x1, starting transfers between devices, on_device(): lax.all_to_all(req_rows, 'nodes', split_axis=0, concat_axis=0, tiled=True)  14 us
    all_gather x1, blocking collectives, on_device(): lax.all_gather(new_part.astype(jnp.bfloat16), 'rep', axis=1, tiled=True)  13.9 us
    all_to_all x1, starting transfers between devices, on_device(): lax.all_to_all(msg_src_slots.reshape(groups, dst_cap, -1), 'nodes', split...  13.4 us
    gather x1, local copies, waits for them, and re-layouts, on_device(): fetched = returned.reshape(-1, updated.shape[1])[nbr_slot]  11.9 us
  transfers between devices with their start and end apart: 10, of which 5 were waited for; matrix products, arithmetic and copies ran while one was open for 14% of the time, Pallas kernels for 0%

profile of v4, /device:TPU:34, one launch (start us, length us, event | category | flops | bytes accessed | tf_op | source)
XLA Modules:
  0.0 291.5 jit_solution(2827477520615423805)
XLA Ops:
  0.6 0.9 copy.50
  3.9 1.6 fusion.23
  6.7 1.3 gather_fusion
  8.1 0.9 scatter_custom_fusion
  9.2 0.8 copy.56
  10.0 17.5 %all-to-all-start = ((s32[128,1,38]{2,1,0:T(1,128)}), s32[128,1,38]{2,1,0:T(1,128)}, u32[]{:S(2)}, u32[]{:S(2)}) async-start(s32[128,1,38]{2,1,0:T(1,128)} %copy.56), calls=%async_computation | async-start | bytes 131072 | tf_op jit(solution)/shard_map/all_to_all | solution.py:144
  27.5 3.0 %convolution_bitcast_fusion = f32[3,512,128]{2,1,0:T(8,128)S(1)} fusion(f32[3,512,128]{2,1,0:T(8,128)} %param.31, f32[512,512]{1,0:T(8,128)S(1)} %copy-done.2), kind=kOutput, calls=%fused_computation.17 | convolution fusion | flops 1207959552 | bytes 2621440 | tf_op jit(solution)/shard_map/rk,gku->gru/dot_general | solution.py:209
  30.5 2.3 scatter_custom_fusion.1
  32.8 1.7 reshape.165
  34.8 14.0 %all-to-all-start.1 = ((bf16[128,2,512]{2,1,0:T(2,128)(2,1)}), bf16[128,2,512]{2,1,0:T(2,128)(2,1)}, u32[]{:S(2)}, u32[]{:S(2)}) async-start(bf16[128,2,512]{2,1,0:T(2,128)(2,1)} %reshape.165), calls=%async_computation.1 | async-start | bytes 524288 | tf_op jit(solution)/shard_map/all_to_all | solution.py:145
  48.8 1.6 reshape.164
  50.4 1.0 slice_reduce_fusion
  51.4 1.9 gather_fusion.2
  53.4 1.9 gather_fusion.1
  56.7 1.2 fusion.54
  57.9 1.6 cosine_convert_fusion.2
  59.8 1.1 reshape.166
  60.9 2.0 multiply_convert_fusion
  62.9 0.7 fusion.75
  64.4 2.4 collective-permute-start.2
  67.4 1.2 pad_clamp_fusion
  68.6 4.3 %collective-permute-start.1 = (bf16[272,512]{1,0:T(8,128)(2,1)}, bf16[272,512]{1,0:T(8,128)(2,1)}, u32[]{:S(2)}, u32[]{:S(2)}) collective-permute-start(bf16[272,512]{1,0:T(8,128)(2,1)} %pad_maximum_fusion), channel_id=1, source_target_pairs={{0,2},{1,3},{2,0},{3,1},{4,6},{5,7},{6,4},{7,5},{8,10},{9,11},{10,... | collective-permute-start | bytes 835592 | tf_op jit(solution)/shard_map/ppermute | solution.py:180
  73.6 1.6 slice.181
  75.7 1.5 eq.113
  77.2 3.7 %collective-permute-start = (bf16[272,512]{1,0:T(8,128)(2,1)}, bf16[272,512]{1,0:T(8,128)(2,1)}, u32[]{:S(2)}, u32[]{:S(2)}) collective-permute-start(bf16[272,512]{1,0:T(8,128)(2,1)} %pad_maximum_fusion), channel_id=1, source_target_pairs={{0,1},{1,2},{2,3},{3,0},{4,5},{5,6},{6,7},{7,4},{8,9},{9,10},{10,1... | collective-permute-start | bytes 835592 | tf_op jit(solution)/shard_map/ppermute | solution.py:180
  80.9 0.8 reshape.173
  81.7 13.4 %all-to-all-start.2 = ((bf16[128,2,512]{2,1,0:T(2,128)(2,1)}), bf16[128,2,512]{2,1,0:T(2,128)(2,1)S(1)}, u32[]{:S(2)}, u32[]{:S(2)}) async-start(bf16[128,2,512]{2,1,0:T(2,128)(2,1)} %reshape.173), calls=%async_computation.2 | async-start | bytes 524288 | tf_op jit(solution)/shard_map/all_to_all | solution.py:171
  95.3 0.7 slice_bitcast_fusion.3
  98.0 1.7 slice_dynamic-update-slice_fusion.2
  100.2 1.7 slice_dynamic-update-slice_fusion.1
  102.6 4.0 %all-to-all-done.2 = bf16[128,2,512]{2,1,0:T(2,128)(2,1)S(1)} async-done(((bf16[128,2,512]{2,1,0:T(2,128)(2,1)}), bf16[128,2,512]{2,1,0:T(2,128)(2,1)S(1)}, u32[]{:S(2)}, u32[]{:S(2)}) %all-to-all-start.2) | async-done | bytes 262176 | tf_op jit(solution)/shard_map/all_to_all | solution.py:171
  106.7 1.0 gather_fusion.3
  107.6 1.9 collective-permute-start.3
  109.6 4.2 %collective-permute-start.4 = (bf16[128,512]{1,0:T(8,128)(2,1)S(1)}, bf16[128,512]{1,0:T(8,128)(2,1)S(1)}, u32[]{:S(2)}, u32[]{:S(2)}) collective-permute-start(bf16[128,512]{1,0:T(8,128)(2,1)S(1)} %gather_fusion.3), channel_id=1, source_target_pairs={{0,2},{1,3},{2,0},{3,1},{4,6},{5,7},{6,4},{7,5},{8,10},{9,11},{10,... | collective-permute-start | bytes 393224 | tf_op jit(solution)/shard_map/ppermute | solution.py:180
  113.8 3.6 %collective-permute-start.5 = (bf16[128,512]{1,0:T(8,128)(2,1)S(1)}, bf16[128,512]{1,0:T(8,128)(2,1)S(1)}, u32[]{:S(2)}, u32[]{:S(2)}) collective-permute-start(bf16[128,512]{1,0:T(8,128)(2,1)S(1)} %gather_fusion.3), channel_id=1, source_target_pairs={{0,3},{1,0},{2,1},{3,2},{4,7},{5,4},{6,5},{7,6},{8,11},{9,8},{10,9... | collective-permute-start | bytes 393224 | tf_op jit(solution)/shard_map/ppermute | solution.py:180
  119.4 1.9 collective-permute-done.5
  121.9 2.5 fusion.6
  124.5 1.8 convolution_bitcast_fusion.1
  126.3 0.9 fusion.73
  127.3 13.9 %all_gather.3 = bf16[512,512]{1,0:T(8,128)(2,1)S(1)} all-gather(bf16[512,128]{1,0:T(8,128)(2,1)S(1)} %get-tuple-element.6), channel_id=1, replica_groups=mesh['nodes'=128,'rep'=4] {'rep'}, dimensions={1}, use_global_device_ids=true | all-gather | bytes 655360 | tf_op jit(solution)/shard_map/all_gather | solution.py:215
  141.2 4.0 %fusion.1 = bf16[4096,512]{1,0:T(8,128)(2,1)} fusion(bf16[512,512]{1,0:T(8,128)(2,1)S(1)} %all_gather.3, s32[4096]{0:T(1024)S(1)} %copy-done.12), kind=kOutput, calls=%fused_computation.11 | convolution fusion | flops 2151677952 | bytes 4734976 | tf_op jit(solution)/shard_map/dot_general | solution.py:42
  145.2 11.1 %all-to-all-start.3 = ((bf16[128,32,512]{2,1,0:T(8,128)(2,1)}), bf16[128,32,512]{2,1,0:T(8,128)(2,1)}, u32[]{:S(2)}, u32[]{:S(2)}) async-start(bf16[128,32,512]{2,1,0:T(8,128)(2,1)} %bitcast.128), calls=%async_computation.3 | async-start | bytes 8388608 | tf_op jit(solution)/shard_map/all_to_all | solution.py:217
  156.8 4.7 %cosine_convert_fusion.tenc_ref = bf16[2048,128]{1,0:T(8,128)(2,1)} fusion(f32[128]{0:T(128)S(1)} %copy-done.25, f32[128]{0:T(128)S(1)} %copy-done.26, f32[2048]{0:T(1024)S(1)} %mul.121), kind=kLoop, calls=%fused_computation.39 | loop fusion | flops 786432 | bytes 533504 | tf_op jit(solution)/shard_map/convert_element_type | solution.py:220
  161.5 1.0 gather_fusion.5
  162.5 0.9 convolution_convert_fusion.q_ref
  163.4 95.4 %all-to-all-done.3 = bf16[128,32,512]{2,1,0:T(8,128)(2,1)} async-done(((bf16[128,32,512]{2,1,0:T(8,128)(2,1)}), bf16[128,32,512]{2,1,0:T(8,128)(2,1)}, u32[]{:S(2)}, u32[]{:S(2)}) %all-to-all-start.3) | async-done | bytes 4194336 | tf_op jit(solution)/shard_map/all_to_all | solution.py:217
  258.7 11.9 %gather_fusion.4 = bf16[2048,512]{1,0:T(8,128)(2,1)} fusion(bf16[4096,512]{1,0:T(8,128)(2,1)} %bitcast.26, s32[2048]{0:T(1024)S(1)} %broadcast_clamp_fusion), kind=kCustom, calls=%fused_computation.5 | custom fusion | bytes 4202496 | tf_op jit(solution)/shard_map/gather | solution.py:218
  270.7 20.8 %shard_map.185 = bf16[128,512]{1,0:T(8,128)(2,1)} custom-call(bf16[2048,512]{1,0:T(8,128)(2,1)} %gather_fusion.4, bf16[2048,128]{1,0:T(8,128)(2,1)} %cosine_convert_fusion.tenc_ref, bf16[128,512]{1,0:T(8,128)(2,1)} %convolution_convert_fusion.q_ref, bf16[512,1024]{1,0:T(8,128)(2,1)} %wm_ref.1, bf16[128,1024]{1,0:T(8,128)(2,1)} %wt_ref.1), custom_call_target="tpu_custom_call" | custom-call | tf_op jit(solution)/shard_map/pallas_call | solution.py:79
  (145 shorter events, 14.5 us)
Async XLA Ops:
  0.6 60.2 %copy-start = (bf16[1152,512]{1,0:T(8,128)(2,1)S(1)}, bf16[1152,512]{1,0:T(8,128)(2,1)}, u32[]{:S(2)}) copy-start(bf16[1152,512]{1,0:T(8,128)(2,1)} %param.29) | copy-start | bytes 3538948
  2.3 0.7 copy-start.15
  3.2 3.0 %copy-start.18 = (s32[128,1]{0,1:T(1,128)S(1)}, s32[128,1]{0,1:T(1,128)}, u32[]{:S(2)}) copy-start(s32[128,1]{0,1:T(1,128)} %param.21) | copy-start | bytes 1540
  3.2 3.4 %copy-start.28 = (s32[128]{0:T(128)S(1)}, s32[128]{0:T(128)}, u32[]{:S(2)}) copy-start(s32[128]{0:T(128)} %param.20) | copy-start | bytes 1540
  3.2 3.5 %copy-start.1 = (s32[512]{0:T(512)S(1)}, s32[512]{0:T(512)}, u32[]{:S(2)}) copy-start(s32[512]{0:T(512)} %param.19) | copy-start | bytes 6148
  3.9 5.2 %copy-start.5 = (s32[2048]{0:T(1024)}, s32[2048]{0:T(1024)S(1)}, u32[]{:S(2)}) copy-start(s32[2048]{0:T(1024)S(1)} %fusion.20) | copy-start | bytes 24580
  3.9 4.1 %copy-start.27 = (s32[128]{0:T(128)S(1)}, s32[128]{0:T(128)}, u32[]{:S(2)}) copy-start(s32[128]{0:T(128)} %param.22) | copy-start | bytes 1540
  3.9 4.1 %copy-start.29 = (s32[128]{0:T(128)S(1)}, s32[128]{0:T(128)}, u32[]{:S(2)}) copy-start(s32[128]{0:T(128)} %param.23) | copy-start | bytes 1540
  5.5 21.9 %copy-start.2 = (f32[512,512]{1,0:T(8,128)S(1)}, f32[512,512]{1,0:T(8,128)}, u32[]{:S(2)}) copy-start(f32[512,512]{1,0:T(8,128)} %param.18) | copy-start | bytes 3145732
  6.7 23.9 %copy-start.31 = (s32[128]{0:T(128)}, s32[128]{0:T(128)S(1)}, u32[]{:S(2)}) copy-start(s32[128]{0:T(128)S(1)} %fusion.70) | copy-start | bytes 1540
  6.7 23.8 %copy-start.17 = (s32[1024]{0:T(1024)}, s32[1024]{0:T(1024)S(1)}, u32[]{:S(2)}) copy-start(s32[1024]{0:T(1024)S(1)} %pad_clamp_fusion.2) | copy-start | bytes 12292
  10.0 24.8 %all-to-all-start = ((s32[128,1,38]{2,1,0:T(1,128)}), s32[128,1,38]{2,1,0:T(1,128)}, u32[]{:S(2)}, u32[]{:S(2)}) async-start(s32[128,1,38]{2,1,0:T(1,128)} %copy.56), calls=%async_computation | async-start | bytes 131072 | tf_op jit(solution)/shard_map/all_to_all | solution.py:144
  34.8 25.0 %all-to-all-start.1 = ((bf16[128,2,512]{2,1,0:T(2,128)(2,1)}), bf16[128,2,512]{2,1,0:T(2,128)(2,1)}, u32[]{:S(2)}, u32[]{:S(2)}) async-start(bf16[128,2,512]{2,1,0:T(2,128)(2,1)} %reshape.165), calls=%async_computation.1 | async-start | bytes 524288 | tf_op jit(solution)/shard_map/all_to_all | solution.py:145
  56.1 0.5 copy-start.13
  56.1 0.5 copy-start.14
  62.9 3.9 %copy-start.23 = (f32[4,128]{1,0:T(4,128)S(1)}, f32[4,128]{1,0:T(4,128)}, u32[]{:S(2)}) copy-start(f32[4,128]{1,0:T(4,128)} %param.32) | copy-start | bytes 6148
  64.4 30.8 %collective-permute-start.2 = (bf16[272,512]{1,0:T(8,128)(2,1)}, bf16[272,512]{1,0:T(8,128)(2,1)S(1)}, u32[]{:S(2)}, u32[]{:S(2)}) collective-permute-start(bf16[272,512]{1,0:T(8,128)(2,1)} %pad_maximum_fusion), channel_id=1, source_target_pairs={{0,3},{1,0},{2,1},{3,2},{4,7},{5,4},{6,5},{7,6},{8,11},{9,8},{10,9... | collective-permute-start | bytes 835592 | tf_op jit(solution)/shard_map/ppermute | solution.py:180
  68.6 26.6 %collective-permute-start.1 = (bf16[272,512]{1,0:T(8,128)(2,1)}, bf16[272,512]{1,0:T(8,128)(2,1)}, u32[]{:S(2)}, u32[]{:S(2)}) collective-permute-start(bf16[272,512]{1,0:T(8,128)(2,1)} %pad_maximum_fusion), channel_id=1, source_target_pairs={{0,2},{1,3},{2,0},{3,1},{4,6},{5,7},{6,4},{7,5},{8,10},{9,11},{10,... | collective-permute-start | bytes 835592 | tf_op jit(solution)/shard_map/ppermute | solution.py:180
  77.2 18.8 %collective-permute-start = (bf16[272,512]{1,0:T(8,128)(2,1)}, bf16[272,512]{1,0:T(8,128)(2,1)}, u32[]{:S(2)}, u32[]{:S(2)}) collective-permute-start(bf16[272,512]{1,0:T(8,128)(2,1)} %pad_maximum_fusion), channel_id=1, source_target_pairs={{0,1},{1,2},{2,3},{3,0},{4,5},{5,6},{6,7},{7,4},{8,9},{9,10},{10,1... | collective-permute-start | bytes 835592 | tf_op jit(solution)/shard_map/ppermute | solution.py:180
  81.7 24.8 %all-to-all-start.2 = ((bf16[128,2,512]{2,1,0:T(2,128)(2,1)}), bf16[128,2,512]{2,1,0:T(2,128)(2,1)S(1)}, u32[]{:S(2)}, u32[]{:S(2)}) async-start(bf16[128,2,512]{2,1,0:T(2,128)(2,1)} %reshape.173), calls=%async_computation.2 | async-start | bytes 524288 | tf_op jit(solution)/shard_map/all_to_all | solution.py:171
  97.5 4.3 %copy-start.8 = (s32[1536]{0:T(1024)}, s32[1536]{0:T(1024)S(1)}, u32[]{:S(2)}) copy-start(s32[1536]{0:T(1024)S(1)} %pad_add_fusion) | copy-start | bytes 18436
  98.0 3.9 %copy-start.10 = (f32[512]{0:T(512)}, f32[512]{0:T(512)S(1)}, u32[]{:S(2)}) copy-start(f32[512]{0:T(512)S(1)} %convert_reduce_fusion) | copy-start | bytes 6148
  102.6 7.0 %copy-start.11 = (f32[512]{0:T(512)S(1)}, f32[512]{0:T(512)}, u32[]{:S(2)}) copy-start(f32[512]{0:T(512)} %copy-done.10) | copy-start | bytes 6148
  102.6 19.3 %copy-start.9 = (s32[1536]{0:T(1024)S(1)}, s32[1536]{0:T(1024)}, u32[]{:S(2)}) copy-start(s32[1536]{0:T(1024)} %copy-done.8) | copy-start | bytes 18436
  102.6 19.3 %copy-start.24 = (f32[512]{0:T(512)S(1)}, f32[512]{0:T(512)}, u32[]{:S(2)}) copy-start(f32[512]{0:T(512)} %broadcast_maximum_fusion) | copy-start | bytes 6148
  107.6 10.5 %collective-permute-start.3 = (bf16[128,512]{1,0:T(8,128)(2,1)S(1)}, bf16[128,512]{1,0:T(8,128)(2,1)S(1)}, u32[]{:S(2)}, u32[]{:S(2)}) collective-permute-start(bf16[128,512]{1,0:T(8,128)(2,1)S(1)} %gather_fusion.3), channel_id=1, source_target_pairs={{0,1},{1,2},{2,3},{3,0},{4,5},{5,6},{6,7},{7,4},{8,9},{9,10},{10,1... | collective-permute-start | bytes 393224 | tf_op jit(solution)/shard_map/ppermute | solution.py:180
  109.6 9.2 %collective-permute-start.4 = (bf16[128,512]{1,0:T(8,128)(2,1)S(1)}, bf16[128,512]{1,0:T(8,128)(2,1)S(1)}, u32[]{:S(2)}, u32[]{:S(2)}) collective-permute-start(bf16[128,512]{1,0:T(8,128)(2,1)S(1)} %gather_fusion.3), channel_id=1, source_target_pairs={{0,2},{1,3},{2,0},{3,1},{4,6},{5,7},{6,4},{7,5},{8,10},{9,11},{10,... | collective-permute-start | bytes 393224 | tf_op jit(solution)/shard_map/ppermute | solution.py:180
  113.8 7.5 %collective-permute-start.5 = (bf16[128,512]{1,0:T(8,128)(2,1)S(1)}, bf16[128,512]{1,0:T(8,128)(2,1)S(1)}, u32[]{:S(2)}, u32[]{:S(2)}) collective-permute-start(bf16[128,512]{1,0:T(8,128)(2,1)S(1)} %gather_fusion.3), channel_id=1, source_target_pairs={{0,3},{1,0},{2,1},{3,2},{4,7},{5,4},{6,5},{7,6},{8,11},{9,8},{10,9... | collective-permute-start | bytes 393224 | tf_op jit(solution)/shard_map/ppermute | solution.py:180
  121.9 2.5 copy-start.3
  124.4 1.9 copy-start.19
  124.4 1.9 copy-start.20
  124.4 1.9 copy-start.21
  124.5 1.9 copy-start.22
  126.3 14.9 %copy-start.12 = (s32[4096]{0:T(1024)S(1)}, s32[4096]{0:T(1024)}, u32[]{:S(2)}) copy-start(s32[4096]{0:T(1024)} %eq.113) | copy-start | bytes 49156
  145.2 11.1 %copy-start.30 = (s32[128]{0:T(128)S(1)}, s32[128]{0:T(128)}, u32[]{:S(2)}) copy-start(s32[128]{0:T(128)} %param.23) | copy-start | bytes 1540
  145.2 11.1 %copy-start.7 = (s32[128,16,1]{0,2,1:T(1,128)S(1)}, s32[128,16,1]{0,2,1:T(1,128)}, u32[]{:S(2)}) copy-start(s32[128,16,1]{0,2,1:T(1,128)} %param.24) | copy-start | bytes 24580
  145.2 11.4 %copy-start.16 = (s32[128,16]{0,1:T(8,128)S(1)}, s32[128,16]{0,1:T(8,128)}, u32[]{:S(2)}) copy-start(s32[128,16]{0,1:T(8,128)} %param.26) | copy-start | bytes 24580
  145.2 11.6 %copy-start.6 = (s32[2048]{0:T(1024)S(1)}, s32[2048]{0:T(1024)}, u32[]{:S(2)}) copy-start(s32[2048]{0:T(1024)} %copy-done.5) | copy-start | bytes 24580
  145.2 11.6 %copy-start.25 = (f32[128]{0:T(128)S(1)}, f32[128]{0:T(128)}, u32[]{:S(2)}) copy-start(f32[128]{0:T(128)} %param.28) | copy-start | bytes 1540
  145.2 11.6 %copy-start.26 = (f32[128]{0:T(128)S(1)}, f32[128]{0:T(128)}, u32[]{:S(2)}) copy-start(f32[128]{0:T(128)} %param.27) | copy-start | bytes 1540
  145.2 113.5 %all-to-all-start.3 = ((bf16[128,32,512]{2,1,0:T(8,128)(2,1)}), bf16[128,32,512]{2,1,0:T(8,128)(2,1)}, u32[]{:S(2)}, u32[]{:S(2)}) async-start(bf16[128,32,512]{2,1,0:T(8,128)(2,1)} %bitcast.128), calls=%async_computation.3 | async-start | bytes 8388608 | tf_op jit(solution)/shard_map/all_to_all | solution.py:217
  156.3 6.2 %copy-start.4 = (bf16[512,512]{1,0:T(8,128)(2,1)S(1)}, bf16[512,512]{1,0:T(8,128)(2,1)}, u32[]{:S(2)}) copy-start(bf16[512,512]{1,0:T(8,128)(2,1)} %param.33) | copy-start | bytes 1572868

commit v5 on v4

--- a/solution.py
+++ b/solution.py
@@ -4,10 +4,9 @@
 import jax.numpy as jnp
 from jax import lax
 from jax.experimental import pallas as pl
-from jax.experimental.pallas import tpu as pltpu
 from jax.sharding import PartitionSpec as P
 
-HEADS = 8
+
 HEAD_DIM = 64
 
 
@@ -91,7 +90,7 @@
     )(fetched, time_enc, query, w_keyval_mem, w_keyval_time)
 
 
-def on_device(
+def on_device_body(
     memory,
     last_tick,
     src_local,
@@ -247,7 +246,7 @@
         P(),
     )
     return jax.shard_map(
-        on_device,
+        on_device_body,
         mesh=mesh,
         in_specs=placed,
         out_specs=(P("nodes", "rep"), P(("nodes", "rep"), None)),

time: 293 us -> 293 us (level)
  no operation moved by 1% of the time
where the time goes in v5:
time: 293 us; the launch traced here: 291 us
  waiting for transfers between devices  102 us (35%)
  starting transfers between devices  76.2 us (26%)
  local copies, waits for them, and re-layouts  44.8 us (15%)
  Pallas kernels  20.8 us (7%)
  other arithmetic  17.7 us (6%)
  matrix products  14.8 us (5%)
  blocking collectives  13.9 us (5%)
    all_to_all x1, waiting for transfers between devices, on_device_body(): lax.all_to_all(served, 'nodes', split_axis=0, concat_axis=0, tiled=True)  95.4 us
    pallas_call x1, Pallas kernels, attend(): pl.pallas_call(attend_kernel, grid=(events // block,), in_specs=[pl.Block...  20.8 us
    ppermute x6, starting transfers between devices, spread(): parts.append(lax.ppermute(value, 'rep', pairs))  20.2 us
    all_to_all x1, starting transfers between devices, on_device_body(): lax.all_to_all(ints_out, 'nodes', split_axis=0, concat_axis=0, tiled=True)  17.5 us
    all_to_all x1, starting transfers between devices, on_device_body(): lax.all_to_all(req_rows, 'nodes', split_axis=0, concat_axis=0, tiled=True)  14 us
    all_gather x1, blocking collectives, on_device_body(): lax.all_gather(new_part.astype(jnp.bfloat16), 'rep', axis=1, tiled=True)  13.9 us
    all_to_all x1, starting transfers between devices, on_device_body(): lax.all_to_all(msg_src_slots.reshape(groups, dst_cap, -1), 'nodes', split...  13.4 us
    gather x1, local copies, waits for them, and re-layouts, on_device_body(): fetched = returned.reshape(-1, updated.shape[1])[nbr_slot]  11.9 us
  transfers between devices with their start and end apart: 10, of which 5 were waited for; matrix products, arithmetic and copies ran while one was open for 14% of the time, Pallas kernels for 0%

profile of v5, /device:TPU:34, one launch (start us, length us, event | category | flops | bytes accessed | tf_op | source)
XLA Modules:
  0.0 291.5 jit_solution(2827477520615423805)
XLA Ops:
  0.6 0.9 copy.50
  3.9 1.6 fusion.23
  6.7 1.3 gather_fusion
  8.1 0.9 scatter_custom_fusion
  9.2 0.8 copy.56
  10.0 17.5 %all-to-all-start = ((s32[128,1,38]{2,1,0:T(1,128)}), s32[128,1,38]{2,1,0:T(1,128)}, u32[]{:S(2)}, u32[]{:S(2)}) async-start(s32[128,1,38]{2,1,0:T(1,128)} %copy.56), calls=%async_computation | async-start | bytes 131072 | tf_op jit(solution)/shard_map/all_to_all | solution.py:143
  27.5 3.0 %convolution_bitcast_fusion = f32[3,512,128]{2,1,0:T(8,128)S(1)} fusion(f32[3,512,128]{2,1,0:T(8,128)} %param.31, f32[512,512]{1,0:T(8,128)S(1)} %copy-done.2), kind=kOutput, calls=%fused_computation.17 | convolution fusion | flops 1207959552 | bytes 2621440 | tf_op jit(solution)/shard_map/rk,gku->gru/dot_general | solution.py:208
  30.5 2.3 scatter_custom_fusion.1
  32.8 1.7 reshape.165
  34.8 14.0 %all-to-all-start.1 = ((bf16[128,2,512]{2,1,0:T(2,128)(2,1)}), bf16[128,2,512]{2,1,0:T(2,128)(2,1)}, u32[]{:S(2)}, u32[]{:S(2)}) async-start(bf16[128,2,512]{2,1,0:T(2,128)(2,1)} %reshape.165), calls=%async_computation.1 | async-start | bytes 524288 | tf_op jit(solution)/shard_map/all_to_all | solution.py:144
  48.8 1.6 reshape.164
  50.4 1.0 slice_reduce_fusion
  51.4 1.9 gather_fusion.2
  53.4 1.9 gather_fusion.1
  56.7 1.2 fusion.54
  57.9 1.6 cosine_convert_fusion.2
  59.8 1.1 reshape.166
  60.9 2.0 multiply_convert_fusion
  62.9 0.7 fusion.75
  64.4 2.4 collective-permute-start.2
  67.4 1.2 pad_clamp_fusion
  68.6 4.3 %collective-permute-start.1 = (bf16[272,512]{1,0:T(8,128)(2,1)}, bf16[272,512]{1,0:T(8,128)(2,1)}, u32[]{:S(2)}, u32[]{:S(2)}) collective-permute-start(bf16[272,512]{1,0:T(8,128)(2,1)} %pad_maximum_fusion), channel_id=1, source_target_pairs={{0,2},{1,3},{2,0},{3,1},{4,6},{5,7},{6,4},{7,5},{8,10},{9,11},{10,... | collective-permute-start | bytes 835592 | tf_op jit(solution)/shard_map/ppermute | solution.py:179
  73.6 1.6 slice.181
  75.7 1.5 eq.113
  77.2 3.7 %collective-permute-start = (bf16[272,512]{1,0:T(8,128)(2,1)}, bf16[272,512]{1,0:T(8,128)(2,1)}, u32[]{:S(2)}, u32[]{:S(2)}) collective-permute-start(bf16[272,512]{1,0:T(8,128)(2,1)} %pad_maximum_fusion), channel_id=1, source_target_pairs={{0,1},{1,2},{2,3},{3,0},{4,5},{5,6},{6,7},{7,4},{8,9},{9,10},{10,1... | collective-permute-start | bytes 835592 | tf_op jit(solution)/shard_map/ppermute | solution.py:179
  80.9 0.8 reshape.173
  81.7 13.4 %all-to-all-start.2 = ((bf16[128,2,512]{2,1,0:T(2,128)(2,1)}), bf16[128,2,512]{2,1,0:T(2,128)(2,1)S(1)}, u32[]{:S(2)}, u32[]{:S(2)}) async-start(bf16[128,2,512]{2,1,0:T(2,128)(2,1)} %reshape.173), calls=%async_computation.2 | async-start | bytes 524288 | tf_op jit(solution)/shard_map/all_to_all | solution.py:170
  95.3 0.7 slice_bitcast_fusion.3
  98.0 1.7 slice_dynamic-update-slice_fusion.2
  100.2 1.7 slice_dynamic-update-slice_fusion.1
  102.6 4.0 %all-to-all-done.2 = bf16[128,2,512]{2,1,0:T(2,128)(2,1)S(1)} async-done(((bf16[128,2,512]{2,1,0:T(2,128)(2,1)}), bf16[128,2,512]{2,1,0:T(2,128)(2,1)S(1)}, u32[]{:S(2)}, u32[]{:S(2)}) %all-to-all-start.2) | async-done | bytes 262176 | tf_op jit(solution)/shard_map/all_to_all | solution.py:170
  106.7 1.0 gather_fusion.3
  107.6 1.9 collective-permute-start.3
  109.6 4.2 %collective-permute-start.4 = (bf16[128,512]{1,0:T(8,128)(2,1)S(1)}, bf16[128,512]{1,0:T(8,128)(2,1)S(1)}, u32[]{:S(2)}, u32[]{:S(2)}) collective-permute-start(bf16[128,512]{1,0:T(8,128)(2,1)S(1)} %gather_fusion.3), channel_id=1, source_target_pairs={{0,2},{1,3},{2,0},{3,1},{4,6},{5,7},{6,4},{7,5},{8,10},{9,11},{10,... | collective-permute-start | bytes 393224 | tf_op jit(solution)/shard_map/ppermute | solution.py:179
  113.8 3.6 %collective-permute-start.5 = (bf16[128,512]{1,0:T(8,128)(2,1)S(1)}, bf16[128,512]{1,0:T(8,128)(2,1)S(1)}, u32[]{:S(2)}, u32[]{:S(2)}) collective-permute-start(bf16[128,512]{1,0:T(8,128)(2,1)S(1)} %gather_fusion.3), channel_id=1, source_target_pairs={{0,3},{1,0},{2,1},{3,2},{4,7},{5,4},{6,5},{7,6},{8,11},{9,8},{10,9... | collective-permute-start | bytes 393224 | tf_op jit(solution)/shard_map/ppermute | solution.py:179
  119.4 1.9 collective-permute-done.5
  121.9 2.5 fusion.6
  124.5 1.8 convolution_bitcast_fusion.1
  126.3 0.9 fusion.73
  127.3 13.9 %all_gather.3 = bf16[512,512]{1,0:T(8,128)(2,1)S(1)} all-gather(bf16[512,128]{1,0:T(8,128)(2,1)S(1)} %get-tuple-element.6), channel_id=1, replica_groups=mesh['nodes'=128,'rep'=4] {'rep'}, dimensions={1}, use_global_device_ids=true | all-gather | bytes 655360 | tf_op jit(solution)/shard_map/all_gather | solution.py:214
  141.2 4.0 %fusion.1 = bf16[4096,512]{1,0:T(8,128)(2,1)} fusion(bf16[512,512]{1,0:T(8,128)(2,1)S(1)} %all_gather.3, s32[4096]{0:T(1024)S(1)} %copy-done.12), kind=kOutput, calls=%fused_computation.11 | convolution fusion | flops 2151677952 | bytes 4734976 | tf_op jit(solution)/shard_map/dot_general | solution.py:41
  145.2 11.1 %all-to-all-start.3 = ((bf16[128,32,512]{2,1,0:T(8,128)(2,1)}), bf16[128,32,512]{2,1,0:T(8,128)(2,1)}, u32[]{:S(2)}, u32[]{:S(2)}) async-start(bf16[128,32,512]{2,1,0:T(8,128)(2,1)} %bitcast.128), calls=%async_computation.3 | async-start | bytes 8388608 | tf_op jit(solution)/shard_map/all_to_all | solution.py:216
  156.8 4.7 %cosine_convert_fusion.tenc_ref = bf16[2048,128]{1,0:T(8,128)(2,1)} fusion(f32[128]{0:T(128)S(1)} %copy-done.25, f32[128]{0:T(128)S(1)} %copy-done.26, f32[2048]{0:T(1024)S(1)} %mul.121), kind=kLoop, calls=%fused_computation.39 | loop fusion | flops 786432 | bytes 533504 | tf_op jit(solution)/shard_map/convert_element_type | solution.py:219
  161.5 1.0 gather_fusion.5
  162.5 0.9 convolution_convert_fusion.q_ref
  163.4 95.4 %all-to-all-done.3 = bf16[128,32,512]{2,1,0:T(8,128)(2,1)} async-done(((bf16[128,32,512]{2,1,0:T(8,128)(2,1)}), bf16[128,32,512]{2,1,0:T(8,128)(2,1)}, u32[]{:S(2)}, u32[]{:S(2)}) %all-to-all-start.3) | async-done | bytes 4194336 | tf_op jit(solution)/shard_map/all_to_all | solution.py:216
  258.7 11.9 %gather_fusion.4 = bf16[2048,512]{1,0:T(8,128)(2,1)} fusion(bf16[4096,512]{1,0:T(8,128)(2,1)} %bitcast.26, s32[2048]{0:T(1024)S(1)} %broadcast_clamp_fusion), kind=kCustom, calls=%fused_computation.5 | custom fusion | bytes 4202496 | tf_op jit(solution)/shard_map/gather | solution.py:217
  270.7 20.8 %shard_map.185 = bf16[128,512]{1,0:T(8,128)(2,1)} custom-call(bf16[2048,512]{1,0:T(8,128)(2,1)} %gather_fusion.4, bf16[2048,128]{1,0:T(8,128)(2,1)} %cosine_convert_fusion.tenc_ref, bf16[128,512]{1,0:T(8,128)(2,1)} %convolution_convert_fusion.q_ref, bf16[512,1024]{1,0:T(8,128)(2,1)} %wm_ref.1, bf16[128,1024]{1,0:T(8,128)(2,1)} %wt_ref.1), custom_call_target="tpu_custom_call" | custom-call | tf_op jit(solution)/shard_map/pallas_call | solution.py:78
  (145 shorter events, 14.5 us)
Async XLA Ops:
  0.6 60.2 %copy-start = (bf16[1152,512]{1,0:T(8,128)(2,1)S(1)}, bf16[1152,512]{1,0:T(8,128)(2,1)}, u32[]{:S(2)}) copy-start(bf16[1152,512]{1,0:T(8,128)(2,1)} %param.29) | copy-start | bytes 3538948
  2.3 0.7 copy-start.15
  3.2 3.0 %copy-start.18 = (s32[128,1]{0,1:T(1,128)S(1)}, s32[128,1]{0,1:T(1,128)}, u32[]{:S(2)}) copy-start(s32[128,1]{0,1:T(1,128)} %param.21) | copy-start | bytes 1540
  3.2 3.4 %copy-start.28 = (s32[128]{0:T(128)S(1)}, s32[128]{0:T(128)}, u32[]{:S(2)}) copy-start(s32[128]{0:T(128)} %param.20) | copy-start | bytes 1540
  3.2 3.5 %copy-start.1 = (s32[512]{0:T(512)S(1)}, s32[512]{0:T(512)}, u32[]{:S(2)}) copy-start(s32[512]{0:T(512)} %param.19) | copy-start | bytes 6148
  3.9 5.2 %copy-start.5 = (s32[2048]{0:T(1024)}, s32[2048]{0:T(1024)S(1)}, u32[]{:S(2)}) copy-start(s32[2048]{0:T(1024)S(1)} %fusion.20) | copy-start | bytes 24580
  3.9 4.1 %copy-start.27 = (s32[128]{0:T(128)S(1)}, s32[128]{0:T(128)}, u32[]{:S(2)}) copy-start(s32[128]{0:T(128)} %param.22) | copy-start | bytes 1540
  3.9 4.1 %copy-start.29 = (s32[128]{0:T(128)S(1)}, s32[128]{0:T(128)}, u32[]{:S(2)}) copy-start(s32[128]{0:T(128)} %param.23) | copy-start | bytes 1540
  5.5 21.9 %copy-start.2 = (f32[512,512]{1,0:T(8,128)S(1)}, f32[512,512]{1,0:T(8,128)}, u32[]{:S(2)}) copy-start(f32[512,512]{1,0:T(8,128)} %param.18) | copy-start | bytes 3145732
  6.7 23.9 %copy-start.31 = (s32[128]{0:T(128)}, s32[128]{0:T(128)S(1)}, u32[]{:S(2)}) copy-start(s32[128]{0:T(128)S(1)} %fusion.70) | copy-start | bytes 1540
  6.7 23.8 %copy-start.17 = (s32[1024]{0:T(1024)}, s32[1024]{0:T(1024)S(1)}, u32[]{:S(2)}) copy-start(s32[1024]{0:T(1024)S(1)} %pad_clamp_fusion.2) | copy-start | bytes 12292
  10.0 24.8 %all-to-all-start = ((s32[128,1,38]{2,1,0:T(1,128)}), s32[128,1,38]{2,1,0:T(1,128)}, u32[]{:S(2)}, u32[]{:S(2)}) async-start(s32[128,1,38]{2,1,0:T(1,128)} %copy.56), calls=%async_computation | async-start | bytes 131072 | tf_op jit(solution)/shard_map/all_to_all | solution.py:143
  34.8 25.0 %all-to-all-start.1 = ((bf16[128,2,512]{2,1,0:T(2,128)(2,1)}), bf16[128,2,512]{2,1,0:T(2,128)(2,1)}, u32[]{:S(2)}, u32[]{:S(2)}) async-start(bf16[128,2,512]{2,1,0:T(2,128)(2,1)} %reshape.165), calls=%async_computation.1 | async-start | bytes 524288 | tf_op jit(solution)/shard_map/all_to_all | solution.py:144
  56.1 0.5 copy-start.13
  56.1 0.5 copy-start.14
  62.9 3.9 %copy-start.23 = (f32[4,128]{1,0:T(4,128)S(1)}, f32[4,128]{1,0:T(4,128)}, u32[]{:S(2)}) copy-start(f32[4,128]{1,0:T(4,128)} %param.32) | copy-start | bytes 6148
  64.4 30.8 %collective-permute-start.2 = (bf16[272,512]{1,0:T(8,128)(2,1)}, bf16[272,512]{1,0:T(8,128)(2,1)S(1)}, u32[]{:S(2)}, u32[]{:S(2)}) collective-permute-start(bf16[272,512]{1,0:T(8,128)(2,1)} %pad_maximum_fusion), channel_id=1, source_target_pairs={{0,3},{1,0},{2,1},{3,2},{4,7},{5,4},{6,5},{7,6},{8,11},{9,8},{10,9... | collective-permute-start | bytes 835592 | tf_op jit(solution)/shard_map/ppermute | solution.py:179
  68.6 26.6 %collective-permute-start.1 = (bf16[272,512]{1,0:T(8,128)(2,1)}, bf16[272,512]{1,0:T(8,128)(2,1)}, u32[]{:S(2)}, u32[]{:S(2)}) collective-permute-start(bf16[272,512]{1,0:T(8,128)(2,1)} %pad_maximum_fusion), channel_id=1, source_target_pairs={{0,2},{1,3},{2,0},{3,1},{4,6},{5,7},{6,4},{7,5},{8,10},{9,11},{10,... | collective-permute-start | bytes 835592 | tf_op jit(solution)/shard_map/ppermute | solution.py:179
  77.2 18.8 %collective-permute-start = (bf16[272,512]{1,0:T(8,128)(2,1)}, bf16[272,512]{1,0:T(8,128)(2,1)}, u32[]{:S(2)}, u32[]{:S(2)}) collective-permute-start(bf16[272,512]{1,0:T(8,128)(2,1)} %pad_maximum_fusion), channel_id=1, source_target_pairs={{0,1},{1,2},{2,3},{3,0},{4,5},{5,6},{6,7},{7,4},{8,9},{9,10},{10,1... | collective-permute-start | bytes 835592 | tf_op jit(solution)/shard_map/ppermute | solution.py:179
  81.7 24.8 %all-to-all-start.2 = ((bf16[128,2,512]{2,1,0:T(2,128)(2,1)}), bf16[128,2,512]{2,1,0:T(2,128)(2,1)S(1)}, u32[]{:S(2)}, u32[]{:S(2)}) async-start(bf16[128,2,512]{2,1,0:T(2,128)(2,1)} %reshape.173), calls=%async_computation.2 | async-start | bytes 524288 | tf_op jit(solution)/shard_map/all_to_all | solution.py:170
  97.5 4.3 %copy-start.8 = (s32[1536]{0:T(1024)}, s32[1536]{0:T(1024)S(1)}, u32[]{:S(2)}) copy-start(s32[1536]{0:T(1024)S(1)} %pad_add_fusion) | copy-start | bytes 18436
  98.0 3.9 %copy-start.10 = (f32[512]{0:T(512)}, f32[512]{0:T(512)S(1)}, u32[]{:S(2)}) copy-start(f32[512]{0:T(512)S(1)} %convert_reduce_fusion) | copy-start | bytes 6148
  102.6 7.0 %copy-start.11 = (f32[512]{0:T(512)S(1)}, f32[512]{0:T(512)}, u32[]{:S(2)}) copy-start(f32[512]{0:T(512)} %copy-done.10) | copy-start | bytes 6148
  102.6 19.3 %copy-start.9 = (s32[1536]{0:T(1024)S(1)}, s32[1536]{0:T(1024)}, u32[]{:S(2)}) copy-start(s32[1536]{0:T(1024)} %copy-done.8) | copy-start | bytes 18436
  102.6 19.3 %copy-start.24 = (f32[512]{0:T(512)S(1)}, f32[512]{0:T(512)}, u32[]{:S(2)}) copy-start(f32[512]{0:T(512)} %broadcast_maximum_fusion) | copy-start | bytes 6148
  107.6 10.5 %collective-permute-start.3 = (bf16[128,512]{1,0:T(8,128)(2,1)S(1)}, bf16[128,512]{1,0:T(8,128)(2,1)S(1)}, u32[]{:S(2)}, u32[]{:S(2)}) collective-permute-start(bf16[128,512]{1,0:T(8,128)(2,1)S(1)} %gather_fusion.3), channel_id=1, source_target_pairs={{0,1},{1,2},{2,3},{3,0},{4,5},{5,6},{6,7},{7,4},{8,9},{9,10},{10,1... | collective-permute-start | bytes 393224 | tf_op jit(solution)/shard_map/ppermute | solution.py:179
  109.6 9.2 %collective-permute-start.4 = (bf16[128,512]{1,0:T(8,128)(2,1)S(1)}, bf16[128,512]{1,0:T(8,128)(2,1)S(1)}, u32[]{:S(2)}, u32[]{:S(2)}) collective-permute-start(bf16[128,512]{1,0:T(8,128)(2,1)S(1)} %gather_fusion.3), channel_id=1, source_target_pairs={{0,2},{1,3},{2,0},{3,1},{4,6},{5,7},{6,4},{7,5},{8,10},{9,11},{10,... | collective-permute-start | bytes 393224 | tf_op jit(solution)/shard_map/ppermute | solution.py:179
  113.8 7.5 %collective-permute-start.5 = (bf16[128,512]{1,0:T(8,128)(2,1)S(1)}, bf16[128,512]{1,0:T(8,128)(2,1)S(1)}, u32[]{:S(2)}, u32[]{:S(2)}) collective-permute-start(bf16[128,512]{1,0:T(8,128)(2,1)S(1)} %gather_fusion.3), channel_id=1, source_target_pairs={{0,3},{1,0},{2,1},{3,2},{4,7},{5,4},{6,5},{7,6},{8,11},{9,8},{10,9... | collective-permute-start | bytes 393224 | tf_op jit(solution)/shard_map/ppermute | solution.py:179
  121.9 2.5 copy-start.3
  124.4 1.9 copy-start.19
  124.4 1.9 copy-start.20
  124.4 1.9 copy-start.21
  124.5 1.9 copy-start.22
  126.3 14.9 %copy-start.12 = (s32[4096]{0:T(1024)S(1)}, s32[4096]{0:T(1024)}, u32[]{:S(2)}) copy-start(s32[4096]{0:T(1024)} %eq.113) | copy-start | bytes 49156
  145.2 11.1 %copy-start.30 = (s32[128]{0:T(128)S(1)}, s32[128]{0:T(128)}, u32[]{:S(2)}) copy-start(s32[128]{0:T(128)} %param.23) | copy-start | bytes 1540
  145.2 11.1 %copy-start.7 = (s32[128,16,1]{0,2,1:T(1,128)S(1)}, s32[128,16,1]{0,2,1:T(1,128)}, u32[]{:S(2)}) copy-start(s32[128,16,1]{0,2,1:T(1,128)} %param.24) | copy-start | bytes 24580
  145.2 11.3 %copy-start.16 = (s32[128,16]{0,1:T(8,128)S(1)}, s32[128,16]{0,1:T(8,128)}, u32[]{:S(2)}) copy-start(s32[128,16]{0,1:T(8,128)} %param.26) | copy-start | bytes 24580
  145.2 11.6 %copy-start.6 = (s32[2048]{0:T(1024)S(1)}, s32[2048]{0:T(1024)}, u32[]{:S(2)}) copy-start(s32[2048]{0:T(1024)} %copy-done.5) | copy-start | bytes 24580
  145.2 11.6 %copy-start.25 = (f32[128]{0:T(128)S(1)}, f32[128]{0:T(128)}, u32[]{:S(2)}) copy-start(f32[128]{0:T(128)} %param.28) | copy-start | bytes 1540
  145.2 11.6 %copy-start.26 = (f32[128]{0:T(128)S(1)}, f32[128]{0:T(128)}, u32[]{:S(2)}) copy-start(f32[128]{0:T(128)} %param.27) | copy-start | bytes 1540
  145.2 113.5 %all-to-all-start.3 = ((bf16[128,32,512]{2,1,0:T(8,128)(2,1)}), bf16[128,32,512]{2,1,0:T(8,128)(2,1)}, u32[]{:S(2)}, u32[]{:S(2)}) async-start(bf16[128,32,512]{2,1,0:T(8,128)(2,1)} %bitcast.128), calls=%async_computation.3 | async-start | bytes 8388608 | tf_op jit(solution)/shard_map/all_to_all | solution.py:216
  156.3 6.2 %copy-start.4 = (bf16[512,512]{1,0:T(8,128)(2,1)S(1)}, bf16[512,512]{1,0:T(8,128)(2,1)}, u32[]{:S(2)}) copy-start(bf16[512,512]{1,0:T(8,128)(2,1)} %param.33) | copy-start | bytes 1572868

commit v6 on v3

--- a/solution.py
+++ b/solution.py
@@ -182,10 +182,8 @@
         [id_hi, id_lo, jnp.zeros((id_rows * width_m - 2 * local_ids.shape[0],), jnp.bfloat16)]
     ).reshape(id_rows, width_m)
     payload = jnp.concatenate([local_msgs, id_block], axis=0)
-    parts = [payload]
-    for shift in range(1, reps):
-        pairs = [(i, (i + shift) % reps) for i in range(reps)]
-        parts.append(lax.ppermute(payload, "rep", pairs))
+    gathered = lax.all_gather(payload, "rep", axis=0, tiled=True).reshape(reps, *payload.shape)
+    parts = [gathered[r] for r in range(reps)]
     count = local_msgs.shape[0]
     all_msgs = jnp.concatenate([p[:count] for p in parts], axis=0)
     coded = jnp.stack([p[count:].reshape(-1)[: 2 * count] for p in parts]).astype(jnp.int32)

time: 287 us -> 299 us (1.042)
  the two profiles are of different devices: /device:TPU:34 before, /device:TPU:43 now
where the time goes in v6:
time: 299 us; the launch traced here: 298 us
  waiting for transfers between devices  145 us (48%)
  starting transfers between devices  53.2 us (18%)
  local copies, waits for them, and re-layouts  28.7 us (10%)
  Pallas kernels  20.8 us (7%)
  between operations  14.7 us (5%)
  matrix products  12.3 us (4%)
  blocking collectives  11.7 us (4%)
  other arithmetic  11.5 us (4%)
    all_to_all x1, waiting for transfers between devices, on_device(): lax.all_to_all(served, 'nodes', split_axis=0, concat_axis=0, tiled=True)  96.8 us
    all_gather x1, waiting for transfers between devices, on_device(): lax.all_gather(payload, 'rep', axis=0, tiled=True)  23.4 us
    pallas_call x1, Pallas kernels, attend(): pl.pallas_call(attend_kernel, grid=(events // block,), in_specs=[pl.Block...  20.8 us
    all_to_all x1, starting transfers between devices, on_device(): lax.all_to_all(served, 'nodes', split_axis=0, concat_axis=0, tiled=True)  18.1 us
    all_to_all x1, starting transfers between devices, on_device(): lax.all_to_all(ints_out, 'nodes', split_axis=0, concat_axis=0, tiled=True)  17.2 us
    all_to_all x1, waiting for transfers between devices, on_device(): lax.all_to_all(msg_src_slots.reshape(groups, dst_cap, -1), 'nodes', split...  12 us
    gather x1, local copies, waits for them, and re-layouts, on_device(): fetched = returned.reshape(-1, updated.shape[1])[nbr_slot]  12 us
    all_gather x1, blocking collectives, on_device(): lax.all_gather(new_part.astype(jnp.bfloat16), 'rep', axis=1, tiled=True)  11.7 us
  transfers between devices with their start and end apart: 5, of which 5 were waited for; matrix products, arithmetic and copies ran while one was open for 6% of the time, Pallas kernels for 0%

profile of v6, /device:TPU:43, one launch (start us, length us, event | category | flops | bytes accessed | tf_op | source)
XLA Modules:
  0.0 298.0 jit_solution(17092869439442330008)
XLA Ops:
  7.2 0.9 copy.50
  8.3 0.3 fusion.31
  8.8 0.3 copy.53
  9.2 0.2 copy-done.5
  9.6 0.6 fusion.25
  10.3 1.6 fusion.30
  11.9 0.6 convolution_convert_fusion.1
  12.6 0.2 reduce_window_sum.26
  12.8 0.2 select_reduce_fusion
  13.1 1.3 gather_fusion
  14.5 0.9 scatter_custom_fusion.1
  15.5 0.8 copy.56
  16.3 17.2 %all-to-all-start.1 = ((s32[128,1,38]{2,1,0:T(1,128)}), s32[128,1,38]{2,1,0:T(1,128)S(1)}, u32[]{:S(2)}, u32[]{:S(2)}) async-start(s32[128,1,38]{2,1,0:T(1,128)} %copy.56), calls=%async_computation.1 | async-start | bytes 131072 | tf_op jit(solution)/shard_map/all_to_all | solution.py:144
  33.6 1.7 scatter_custom_fusion
  35.3 0.8 reshape.176
  36.1 5.4 %all-to-all-done.1 = s32[128,1,38]{2,1,0:T(1,128)S(1)} async-done(((s32[128,1,38]{2,1,0:T(1,128)}), s32[128,1,38]{2,1,0:T(1,128)S(1)}, u32[]{:S(2)}, u32[]{:S(2)}) %all-to-all-start.1) | async-done | bytes 19488 | tf_op jit(solution)/shard_map/all_to_all | solution.py:144
  41.6 9.2 %all-to-all-start = ((bf16[128,2,512]{2,1,0:T(2,128)(2,1)}), bf16[128,2,512]{2,1,0:T(2,128)(2,1)S(1)}, u32[]{:S(2)}, u32[]{:S(2)}) async-start(bf16[128,2,512]{2,1,0:T(2,128)(2,1)} %reshape.176), calls=%async_computation | async-start | bytes 524288 | tf_op jit(solution)/shard_map/all_to_all | solution.py:145
  50.8 0.1 maximum_reduce_fusion
  51.0 1.9 gather_fusion.2
  52.9 1.2 gather_fusion.1
  54.1 0.1 copy.57
  54.2 0.3 fusion.62
  54.5 0.9 cosine_convert_fusion.2
  55.4 7.5 %all-to-all-done = bf16[128,2,512]{2,1,0:T(2,128)(2,1)S(1)} async-done(((bf16[128,2,512]{2,1,0:T(2,128)(2,1)}), bf16[128,2,512]{2,1,0:T(2,128)(2,1)S(1)}, u32[]{:S(2)}, u32[]{:S(2)}) %all-to-all-start) | async-done | bytes 262176 | tf_op jit(solution)/shard_map/all_to_all | solution.py:145
  63.0 1.0 multiply_convert_fusion
  64.1 0.8 reshape.181
  64.9 8.7 %all-to-all-start.2 = ((bf16[128,2,512]{2,1,0:T(2,128)(2,1)}), bf16[128,2,512]{2,1,0:T(2,128)(2,1)S(1)}, u32[]{:S(2)}, u32[]{:S(2)}) async-start(bf16[128,2,512]{2,1,0:T(2,128)(2,1)} %reshape.181), calls=%async_computation.2 | async-start | bytes 524288 | tf_op jit(solution)/shard_map/all_to_all | solution.py:171
  73.8 12.0 %all-to-all-done.2 = bf16[128,2,512]{2,1,0:T(2,128)(2,1)S(1)} async-done(((bf16[128,2,512]{2,1,0:T(2,128)(2,1)}), bf16[128,2,512]{2,1,0:T(2,128)(2,1)S(1)}, u32[]{:S(2)}, u32[]{:S(2)}) %all-to-all-start.2) | async-done | bytes 262176 | tf_op jit(solution)/shard_map/all_to_all | solution.py:171
  85.9 0.8 gather_fusion.3
  86.7 0.8 pad_maximum_fusion
  87.6 3.0 convolution_bitcast_fusion
  90.7 23.4 %all-gather.2.cloned.1.call-done = bf16[1600,512]{1,0:T(8,128)(2,1)} async-done(((bf16[400,512]{1,0:T(8,128)(2,1)}), bf16[1600,512]{1,0:T(8,128)(2,1)}) %all-gather.2.cloned.1.call-update) | async-done | bytes 1638416 | tf_op jit(solution)/shard_map/all_gather | solution.py:185
  114.1 0.8 slice_bitcast_fusion.5
  115.1 0.4 convert_reduce_fusion
  115.5 1.5 fusion.84
  116.9 1.0 fusion.3
  117.9 0.1 copy-done.14
  118.1 1.9 convolution_bitcast_fusion.1
  119.9 0.9 fusion.82
  120.9 11.7 %all_gather.7 = bf16[512,512]{1,0:T(8,128)(2,1)S(1)} all-gather(bf16[512,128]{1,0:T(8,128)(2,1)S(1)} %get-tuple-element.6), channel_id=1, replica_groups=mesh['nodes'=128,'rep'=4] {'rep'}, dimensions={1}, use_global_device_ids=true | all-gather | bytes 655360 | tf_op jit(solution)/shard_map/all_gather | solution.py:208
  132.6 3.9 %fusion.1 = bf16[4096,512]{1,0:T(8,128)(2,1)} fusion(bf16[512,512]{1,0:T(8,128)(2,1)S(1)} %all_gather.7, s32[4096]{0:T(1024)S(1)} %eq.116), kind=kOutput, calls=%fused_computation.11 | convolution fusion | flops 2151677952 | bytes 4734976 | tf_op jit(solution)/shard_map/dot_general | solution.py:42
  136.5 18.1 %all-to-all-start.3 = ((bf16[128,32,512]{2,1,0:T(8,128)(2,1)}), bf16[128,32,512]{2,1,0:T(8,128)(2,1)}, u32[]{:S(2)}, u32[]{:S(2)}) async-start(bf16[128,32,512]{2,1,0:T(8,128)(2,1)} %bitcast.125), calls=%async_computation.3 | async-start | bytes 8388608 | tf_op jit(solution)/shard_map/all_to_all | solution.py:210
  155.1 4.7 %cosine_convert_fusion.tenc_ref = bf16[2048,128]{1,0:T(8,128)(2,1)} fusion(f32[128]{0:T(128)S(1)} %copy-done.9, f32[128]{0:T(128)S(1)} %copy-done.10, f32[2048]{0:T(1024)S(1)} %mul.121), kind=kLoop, calls=%fused_computation.45 | loop fusion | flops 786432 | bytes 533504 | tf_op jit(solution)/shard_map/convert_element_type | solution.py:213
  159.8 0.8 gather_fusion.5
  160.7 0.9 convolution_convert_fusion.q_ref
  161.6 96.8 %all-to-all-done.3 = bf16[128,32,512]{2,1,0:T(8,128)(2,1)} async-done(((bf16[128,32,512]{2,1,0:T(8,128)(2,1)}), bf16[128,32,512]{2,1,0:T(8,128)(2,1)}, u32[]{:S(2)}, u32[]{:S(2)}) %all-to-all-start.3) | async-done | bytes 4194336 | tf_op jit(solution)/shard_map/all_to_all | solution.py:210
  258.4 12.0 %gather_fusion.4 = bf16[2048,512]{1,0:T(8,128)(2,1)} fusion(bf16[4096,512]{1,0:T(8,128)(2,1)} %bitcast.25, s32[2048]{0:T(1024)S(1)} %broadcast_clamp_fusion), kind=kCustom, calls=%fused_computation.5 | custom fusion | bytes 4202496 | tf_op jit(solution)/shard_map/gather | solution.py:211
  270.3 20.8 %shard_map.185 = bf16[128,512]{1,0:T(8,128)(2,1)} custom-call(bf16[2048,512]{1,0:T(8,128)(2,1)} %gather_fusion.4, bf16[2048,128]{1,0:T(8,128)(2,1)} %cosine_convert_fusion.tenc_ref, bf16[128,512]{1,0:T(8,128)(2,1)} %convolution_convert_fusion.q_ref, bf16[512,1024]{1,0:T(8,128)(2,1)} %wm_ref.1, bf16[128,1024]{1,0:T(8,128)(2,1)} %wt_ref.1), custom_call_target="tpu_custom_call" | custom-call | tf_op jit(solution)/shard_map/pallas_call | solution.py:79
  (92 shorter events, 2.2 us)
Async XLA Ops:
  7.2 55.8 %copy-start = (bf16[1152,512]{1,0:T(8,128)(2,1)S(1)}, bf16[1152,512]{1,0:T(8,128)(2,1)}, u32[]{:S(2)}) copy-start(bf16[1152,512]{1,0:T(8,128)(2,1)} %param.29) | copy-start | bytes 3538948
  8.7 0.7 copy-start.5
  8.8 3.7 %copy-start.7 = (s32[128,1]{0,1:T(1,128)S(1)}, s32[128,1]{0,1:T(1,128)}, u32[]{:S(2)}) copy-start(s32[128,1]{0,1:T(1,128)} %param.21) | copy-start | bytes 1540
  9.4 3.6 %copy-start.12 = (s32[128]{0:T(128)S(1)}, s32[128]{0:T(128)}, u32[]{:S(2)}) copy-start(s32[128]{0:T(128)} %param.20) | copy-start | bytes 1540
  9.4 3.7 %copy-start.1 = (s32[512]{0:T(512)S(1)}, s32[512]{0:T(512)}, u32[]{:S(2)}) copy-start(s32[512]{0:T(512)} %param.19) | copy-start | bytes 6148
  9.4 4.9 %copy-start.11 = (s32[128]{0:T(128)S(1)}, s32[128]{0:T(128)}, u32[]{:S(2)}) copy-start(s32[128]{0:T(128)} %param.22) | copy-start | bytes 1540
  9.4 4.9 %copy-start.13 = (s32[128]{0:T(128)S(1)}, s32[128]{0:T(128)}, u32[]{:S(2)}) copy-start(s32[128]{0:T(128)} %param.23) | copy-start | bytes 1540
  9.6 23.9 %copy-start.2 = (f32[512,512]{1,0:T(8,128)S(1)}, f32[512,512]{1,0:T(8,128)}, u32[]{:S(2)}) copy-start(f32[512,512]{1,0:T(8,128)} %param.18) | copy-start | bytes 3145732
  16.3 25.2 %all-to-all-start.1 = ((s32[128,1,38]{2,1,0:T(1,128)}), s32[128,1,38]{2,1,0:T(1,128)S(1)}, u32[]{:S(2)}, u32[]{:S(2)}) async-start(s32[128,1,38]{2,1,0:T(1,128)} %copy.56), calls=%async_computation.1 | async-start | bytes 131072 | tf_op jit(solution)/shard_map/all_to_all | solution.py:144
  36.1 18.4 %copy-start.9 = (f32[128]{0:T(128)S(1)}, f32[128]{0:T(128)}, u32[]{:S(2)}) copy-start(f32[128]{0:T(128)} %param.28) | copy-start | bytes 1540
  36.1 18.4 %copy-start.10 = (f32[128]{0:T(128)S(1)}, f32[128]{0:T(128)}, u32[]{:S(2)}) copy-start(f32[128]{0:T(128)} %param.27) | copy-start | bytes 1540
  41.6 21.4 %all-to-all-start = ((bf16[128,2,512]{2,1,0:T(2,128)(2,1)}), bf16[128,2,512]{2,1,0:T(2,128)(2,1)S(1)}, u32[]{:S(2)}, u32[]{:S(2)}) async-start(bf16[128,2,512]{2,1,0:T(2,128)(2,1)} %reshape.176), calls=%async_computation | async-start | bytes 524288 | tf_op jit(solution)/shard_map/all_to_all | solution.py:145
  64.0 23.5 %copy-start.8 = (f32[4,128]{1,0:T(4,128)S(1)}, f32[4,128]{1,0:T(4,128)}, u32[]{:S(2)}) copy-start(f32[4,128]{1,0:T(4,128)} %param.32) | copy-start | bytes 6148
  64.9 20.9 %all-to-all-start.2 = ((bf16[128,2,512]{2,1,0:T(2,128)(2,1)}), bf16[128,2,512]{2,1,0:T(2,128)(2,1)S(1)}, u32[]{:S(2)}, u32[]{:S(2)}) async-start(bf16[128,2,512]{2,1,0:T(2,128)(2,1)} %reshape.181), calls=%async_computation.2 | async-start | bytes 524288 | tf_op jit(solution)/shard_map/all_to_all | solution.py:171
  73.6 40.5 %all-gather.2.cloned.1.call-start = ((), (), s32[]{:S(2)}) async-start(), calls=%async_computation.4 | async-start | bytes 2048000 | tf_op jit(solution)/shard_map/all_gather | solution.py:185
  116.9 1.1 copy-start.14
  136.5 18.1 %copy-start.4 = (s32[128,16,1]{0,2,1:T(1,128)S(1)}, s32[128,16,1]{0,2,1:T(1,128)}, u32[]{:S(2)}) copy-start(s32[128,16,1]{0,2,1:T(1,128)} %param.24) | copy-start | bytes 24580
  136.5 18.4 %copy-start.6 = (s32[128,16]{0,1:T(8,128)S(1)}, s32[128,16]{0,1:T(8,128)}, u32[]{:S(2)}) copy-start(s32[128,16]{0,1:T(8,128)} %param.26) | copy-start | bytes 24580
  136.5 24.1 %copy-start.3 = (bf16[512,512]{1,0:T(8,128)(2,1)S(1)}, bf16[512,512]{1,0:T(8,128)(2,1)}, u32[]{:S(2)}) copy-start(bf16[512,512]{1,0:T(8,128)(2,1)} %param.33) | copy-start | bytes 1572868
  136.5 121.8 %all-to-all-start.3 = ((bf16[128,32,512]{2,1,0:T(8,128)(2,1)}), bf16[128,32,512]{2,1,0:T(8,128)(2,1)}, u32[]{:S(2)}, u32[]{:S(2)}) async-start(bf16[128,32,512]{2,1,0:T(8,128)(2,1)} %bitcast.125), calls=%async_computation.3 | async-start | bytes 8388608 | tf_op jit(solution)/shard_map/all_to_all | solution.py:210
Sparse Core Ops, SparseCore 0:
  87.7 26.3 all-gather.1

commit v7 on v3

--- a/solution.py
+++ b/solution.py
@@ -57,22 +57,29 @@
     prod = (keys.reshape(block, nbrs, width) * query[:, None, :]).reshape(rows, width)
     lane = lax.broadcasted_iota(jnp.int32, (width, 128), 0)
     col = lax.broadcasted_iota(jnp.int32, (width, 128), 1)
-    head_of = (lane // HEAD_DIM == col).astype(f32)
-    highest = lax.Precision.HIGHEST
-    scores = jnp.dot(prod, head_of, preferred_element_type=f32, precision=highest)
+    head_of = (lane // HEAD_DIM == col).astype(bf16)
+    hi = prod.astype(bf16)
+    lo = (prod - hi.astype(f32)).astype(bf16)
+    scores = jnp.dot(hi, head_of, preferred_element_type=f32) + jnp.dot(
+        lo, head_of, preferred_element_type=f32
+    )
     scores = (scores / math.sqrt(HEAD_DIM)).reshape(block, nbrs, 128)
     top = jnp.max(scores, axis=1, keepdims=True)
     ex = jnp.exp(scores - top)
     weights = (ex / jnp.sum(ex, axis=1, keepdims=True)).reshape(rows, 128)
     row = lax.broadcasted_iota(jnp.int32, (128, width), 0)
     lane2 = lax.broadcasted_iota(jnp.int32, (128, width), 1)
-    head_to = (lane2 // HEAD_DIM == row).astype(f32)
-    spread = jnp.dot(weights, head_to, preferred_element_type=f32, precision=highest)
+    head_to = (lane2 // HEAD_DIM == row).astype(bf16)
+    w_hi = weights.astype(bf16)
+    w_lo = (weights - w_hi.astype(f32)).astype(bf16)
+    spread = jnp.dot(w_hi, head_to, preferred_element_type=f32) + jnp.dot(
+        w_lo, head_to, preferred_element_type=f32
+    )
     mixed = jnp.sum((spread * values).reshape(block, nbrs, width), axis=1)
     out_ref[...] = mixed.astype(out_ref.dtype)
 
 
-def attend(fetched, time_enc, query, w_keyval_mem, w_keyval_time, block=16):
+def attend(fetched, time_enc, query, w_keyval_mem, w_keyval_time, block=32):
     events, width = query.shape
     nbrs = fetched.shape[0] // events
     rows = block * nbrs

time: 287 us -> 277 us (0.965)
  Pallas kernels: 20.8 us -> 11 us
    pallas_call x1, Pallas kernels: 20.8 us -> 11 us  [attend(): pl.pallas_call(attend_kernel, grid=(events // block,), in_specs=[pl.Block...]
where the time goes in v7:
time: 277 us
  waiting for transfers between devices  131 us (47%)
  starting transfers between devices  57.6 us (21%)
  local copies, waits for them, and re-layouts  33.6 us (12%)
  blocking collectives  15.8 us (6%)
  matrix products  13.4 us (5%)
  other arithmetic  12.9 us (5%)
  Pallas kernels  11 us (4%)
    all_to_all x1, waiting for transfers between devices, on_device(): lax.all_to_all(served, 'nodes', split_axis=0, concat_axis=0, tiled=True)  95.5 us
    all_to_all x1, starting transfers between devices, on_device(): lax.all_to_all(ints_out, 'nodes', split_axis=0, concat_axis=0, tiled=True)  17 us
    all_gather x1, blocking collectives, on_device(): lax.all_gather(new_part.astype(jnp.bfloat16), 'rep', axis=1, tiled=True)  15.8 us
    ppermute x3, waiting for transfers between devices, on_device(): parts.append(lax.ppermute(payload, 'rep', pairs))  13.9 us
    gather x1, local copies, waits for them, and re-layouts, on_device(): fetched = returned.reshape(-1, updated.shape[1])[nbr_slot]  12 us
    all_to_all x1, waiting for transfers between devices, on_device(): lax.all_to_all(msg_src_slots.reshape(groups, dst_cap, -1), 'nodes', split...  11.3 us
    pallas_call x1, Pallas kernels, attend(): pl.pallas_call(attend_kernel, grid=(events // block,), in_specs=[pl.Block...  11 us
    all_to_all x1, starting transfers between devices, on_device(): lax.all_to_all(served, 'nodes', split_axis=0, concat_axis=0, tiled=True)  10.8 us
  transfers between devices with their start and end apart: 7, of which 7 were waited for; matrix products, arithmetic and copies ran while one was open for 7% of the time, Pallas kernels for 0%

profile of v7, /device:TPU:34, one launch (start us, length us, event | category | flops | bytes accessed | tf_op | source)
XLA Modules:
  0.0 276.5 jit_solution(9336680118451794311)
XLA Ops:
  0.6 0.9 copy.50
  3.2 0.6 fusion.20
  3.9 1.6 fusion.23
  6.7 1.3 gather_fusion
  8.1 0.9 scatter_custom_fusion
  9.2 0.8 copy.56
  9.9 17.0 %all-to-all-start = ((s32[128,1,38]{2,1,0:T(1,128)}), s32[128,1,38]{2,1,0:T(1,128)S(1)}, u32[]{:S(2)}, u32[]{:S(2)}) async-start(s32[128,1,38]{2,1,0:T(1,128)} %copy.56), calls=%async_computation | async-start | bytes 131072 | tf_op jit(solution)/shard_map/all_to_all | solution.py:151
  27.1 1.7 scatter_custom_fusion.1
  28.8 0.8 reshape.159
  29.6 4.8 %all-to-all-done = s32[128,1,38]{2,1,0:T(1,128)S(1)} async-done(((s32[128,1,38]{2,1,0:T(1,128)}), s32[128,1,38]{2,1,0:T(1,128)S(1)}, u32[]{:S(2)}, u32[]{:S(2)}) %all-to-all-start) | async-done | bytes 19488 | tf_op jit(solution)/shard_map/all_to_all | solution.py:151
  34.3 9.8 %all-to-all-start.1 = ((bf16[128,2,512]{2,1,0:T(2,128)(2,1)}), bf16[128,2,512]{2,1,0:T(2,128)(2,1)S(1)}, u32[]{:S(2)}, u32[]{:S(2)}) async-start(bf16[128,2,512]{2,1,0:T(2,128)(2,1)} %reshape.159), calls=%async_computation.1 | async-start | bytes 524288 | tf_op jit(solution)/shard_map/all_to_all | solution.py:152
  44.3 0.7 slice_reduce_fusion
  45.0 1.9 gather_fusion.2
  46.9 1.2 gather_fusion.1
  48.5 1.8 cosine_convert_fusion.2
  50.3 5.3 %all-to-all-done.1 = bf16[128,2,512]{2,1,0:T(2,128)(2,1)S(1)} async-done(((bf16[128,2,512]{2,1,0:T(2,128)(2,1)}), bf16[128,2,512]{2,1,0:T(2,128)(2,1)S(1)}, u32[]{:S(2)}, u32[]{:S(2)}) %all-to-all-start.1) | async-done | bytes 262176 | tf_op jit(solution)/shard_map/all_to_all | solution.py:152
  55.7 1.8 multiply_convert_fusion
  57.6 0.8 reshape.161
  58.4 9.5 %all-to-all-start.2 = ((bf16[128,2,512]{2,1,0:T(2,128)(2,1)}), bf16[128,2,512]{2,1,0:T(2,128)(2,1)S(1)}, u32[]{:S(2)}, u32[]{:S(2)}) async-start(bf16[128,2,512]{2,1,0:T(2,128)(2,1)} %reshape.161), calls=%async_computation.2 | async-start | bytes 524288 | tf_op jit(solution)/shard_map/all_to_all | solution.py:178
  68.0 11.3 %all-to-all-done.2 = bf16[128,2,512]{2,1,0:T(2,128)(2,1)S(1)} async-done(((bf16[128,2,512]{2,1,0:T(2,128)(2,1)}), bf16[128,2,512]{2,1,0:T(2,128)(2,1)S(1)}, u32[]{:S(2)}, u32[]{:S(2)}) %all-to-all-start.2) | async-done | bytes 262176 | tf_op jit(solution)/shard_map/all_to_all | solution.py:178
  79.5 0.8 gather_fusion.3
  80.3 0.7 constant_dynamic-update-slice_fusion.1
  81.0 0.7 fusion.75
  81.7 0.8 pad_maximum_fusion
  82.5 2.4 collective-permute-start.2
  84.9 1.8 convolution_bitcast_fusion
  86.8 4.3 %collective-permute-start.1 = (bf16[400,512]{1,0:T(8,128)(2,1)}, bf16[400,512]{1,0:T(8,128)(2,1)}, u32[]{:S(2)}, u32[]{:S(2)}) collective-permute-start(bf16[400,512]{1,0:T(8,128)(2,1)} %pad_maximum_fusion), channel_id=1, source_target_pairs={{0,2},{1,3},{2,0},{3,1},{4,6},{5,7},{6,4},{7,5},{8,10},{9,11},{10,... | collective-permute-start | bytes 1228808 | tf_op jit(solution)/shard_map/ppermute | solution.py:195
  91.3 3.7 %collective-permute-start = (bf16[400,512]{1,0:T(8,128)(2,1)}, bf16[400,512]{1,0:T(8,128)(2,1)S(1)}, u32[]{:S(2)}, u32[]{:S(2)}) collective-permute-start(bf16[400,512]{1,0:T(8,128)(2,1)} %pad_maximum_fusion), channel_id=1, source_target_pairs={{0,1},{1,2},{2,3},{3,0},{4,5},{5,6},{6,7},{7,4},{8,9},{9,10},{10,1... | collective-permute-start | bytes 1228808 | tf_op jit(solution)/shard_map/ppermute | solution.py:195
  95.0 1.1 collective-permute-done.2
  96.1 0.7 slice_bitcast_fusion.2
  96.9 9.0 %collective-permute-done.1 = bf16[400,512]{1,0:T(8,128)(2,1)} collective-permute-done((bf16[400,512]{1,0:T(8,128)(2,1)}, bf16[400,512]{1,0:T(8,128)(2,1)}, u32[]{:S(2)}, u32[]{:S(2)}) %collective-permute-start.1) | collective-permute-done | bytes 409632 | tf_op jit(solution)/shard_map/ppermute | solution.py:195
  105.8 0.7 slice_bitcast_fusion.3
  106.6 3.8 %collective-permute-done = bf16[400,512]{1,0:T(8,128)(2,1)S(1)} collective-permute-done((bf16[400,512]{1,0:T(8,128)(2,1)}, bf16[400,512]{1,0:T(8,128)(2,1)S(1)}, u32[]{:S(2)}, u32[]{:S(2)}) %collective-permute-start) | collective-permute-done | bytes 409632 | tf_op jit(solution)/shard_map/ppermute | solution.py:195
  110.9 0.8 slice_dynamic-update-slice_fusion.2
  111.7 1.8 slice_dynamic-update-slice_fusion.1
  113.5 1.8 slice_dynamic-update-slice_fusion
  115.3 2.5 fusion.6
  117.7 1.8 convolution_bitcast_fusion.1
  119.6 0.9 fusion.73
  120.5 15.8 %all_gather.3 = bf16[512,512]{1,0:T(8,128)(2,1)S(1)} all-gather(bf16[512,128]{1,0:T(8,128)(2,1)S(1)} %get-tuple-element.6), channel_id=1, replica_groups=mesh['nodes'=128,'rep'=4] {'rep'}, dimensions={1}, use_global_device_ids=true | all-gather | bytes 655360 | tf_op jit(solution)/shard_map/all_gather | solution.py:217
  136.3 4.0 %fusion.1 = bf16[4096,512]{1,0:T(8,128)(2,1)} fusion(bf16[512,512]{1,0:T(8,128)(2,1)S(1)} %all_gather.3, s32[4096]{0:T(1024)S(1)} %eq.116), kind=kOutput, calls=%fused_computation.11 | convolution fusion | flops 2151677952 | bytes 4734976 | tf_op jit(solution)/shard_map/dot_general | solution.py:42
  140.3 10.8 %all-to-all-start.3 = ((bf16[128,32,512]{2,1,0:T(8,128)(2,1)}), bf16[128,32,512]{2,1,0:T(8,128)(2,1)}, u32[]{:S(2)}, u32[]{:S(2)}) async-start(bf16[128,32,512]{2,1,0:T(8,128)(2,1)} %bitcast.123), calls=%async_computation.3 | async-start | bytes 8388608 | tf_op jit(solution)/shard_map/all_to_all | solution.py:219
  151.6 4.7 %cosine_convert_fusion.tenc_ref = bf16[2048,128]{1,0:T(8,128)(2,1)} fusion(f32[128]{0:T(128)S(1)} %copy-done.14, f32[128]{0:T(128)S(1)} %copy-done.15, f32[2048]{0:T(1024)S(1)} %mul.121), kind=kLoop, calls=%fused_computation.39 | loop fusion | flops 786432 | bytes 533504 | tf_op jit(solution)/shard_map/convert_element_type | solution.py:222
  156.3 0.8 gather_fusion.5
  157.1 0.9 convolution_convert_fusion.q_ref
  158.0 95.5 %all-to-all-done.3 = bf16[128,32,512]{2,1,0:T(8,128)(2,1)} async-done(((bf16[128,32,512]{2,1,0:T(8,128)(2,1)}), bf16[128,32,512]{2,1,0:T(8,128)(2,1)}, u32[]{:S(2)}, u32[]{:S(2)}) %all-to-all-start.3) | async-done | bytes 4194336 | tf_op jit(solution)/shard_map/all_to_all | solution.py:219
  253.6 12.0 %gather_fusion.4 = bf16[2048,512]{1,0:T(8,128)(2,1)} fusion(bf16[4096,512]{1,0:T(8,128)(2,1)} %bitcast.25, s32[2048]{0:T(1024)S(1)} %broadcast_clamp_fusion), kind=kCustom, calls=%fused_computation.5 | custom fusion | bytes 4202496 | tf_op jit(solution)/shard_map/gather | solution.py:220
  265.5 11.0 %shard_map.185 = bf16[128,512]{1,0:T(8,128)(2,1)} custom-call(bf16[2048,512]{1,0:T(8,128)(2,1)} %gather_fusion.4, bf16[2048,128]{1,0:T(8,128)(2,1)} %cosine_convert_fusion.tenc_ref, bf16[128,512]{1,0:T(8,128)(2,1)} %convolution_convert_fusion.q_ref, bf16[512,1024]{1,0:T(8,128)(2,1)} %wm_ref.1, bf16[128,1024]{1,0:T(8,128)(2,1)} %wt_ref.1), custom_call_target="tpu_custom_call" | custom-call | tf_op jit(solution)/shard_map/pallas_call | solution.py:86
  (116 shorter events, 5.0 us)
Async XLA Ops:
  0.6 55.1 %copy-start = (bf16[1152,512]{1,0:T(8,128)(2,1)S(1)}, bf16[1152,512]{1,0:T(8,128)(2,1)}, u32[]{:S(2)}) copy-start(bf16[1152,512]{1,0:T(8,128)(2,1)} %param.29) | copy-start | bytes 3538948
  2.3 0.7 copy-start.9
  3.2 3.0 %copy-start.12 = (s32[128,1]{0,1:T(1,128)S(1)}, s32[128,1]{0,1:T(1,128)}, u32[]{:S(2)}) copy-start(s32[128,1]{0,1:T(1,128)} %param.21) | copy-start | bytes 1540
  3.2 3.4 %copy-start.17 = (s32[128]{0:T(128)S(1)}, s32[128]{0:T(128)}, u32[]{:S(2)}) copy-start(s32[128]{0:T(128)} %param.20) | copy-start | bytes 1540
  3.2 3.5 %copy-start.1 = (s32[512]{0:T(512)S(1)}, s32[512]{0:T(512)}, u32[]{:S(2)}) copy-start(s32[512]{0:T(512)} %param.19) | copy-start | bytes 6148
  3.9 4.1 %copy-start.16 = (s32[128]{0:T(128)S(1)}, s32[128]{0:T(128)}, u32[]{:S(2)}) copy-start(s32[128]{0:T(128)} %param.22) | copy-start | bytes 1540
  3.9 4.1 %copy-start.19 = (s32[128]{0:T(128)S(1)}, s32[128]{0:T(128)}, u32[]{:S(2)}) copy-start(s32[128]{0:T(128)} %param.23) | copy-start | bytes 1540
  5.5 21.5 %copy-start.2 = (f32[512,512]{1,0:T(8,128)S(1)}, f32[512,512]{1,0:T(8,128)}, u32[]{:S(2)}) copy-start(f32[512,512]{1,0:T(8,128)} %param.18) | copy-start | bytes 3145732
  6.6 22.9 %copy-start.21 = (s32[128]{0:T(128)}, s32[128]{0:T(128)S(1)}, u32[]{:S(2)}) copy-start(s32[128]{0:T(128)S(1)} %fusion.70) | copy-start | bytes 1540
  9.9 24.4 %all-to-all-start = ((s32[128,1,38]{2,1,0:T(1,128)}), s32[128,1,38]{2,1,0:T(1,128)S(1)}, u32[]{:S(2)}, u32[]{:S(2)}) async-start(s32[128,1,38]{2,1,0:T(1,128)} %copy.56), calls=%async_computation | async-start | bytes 131072 | tf_op jit(solution)/shard_map/all_to_all | solution.py:151
  34.3 21.3 %all-to-all-start.1 = ((bf16[128,2,512]{2,1,0:T(2,128)(2,1)}), bf16[128,2,512]{2,1,0:T(2,128)(2,1)S(1)}, u32[]{:S(2)}, u32[]{:S(2)}) async-start(bf16[128,2,512]{2,1,0:T(2,128)(2,1)} %reshape.159), calls=%async_computation.1 | async-start | bytes 524288 | tf_op jit(solution)/shard_map/all_to_all | solution.py:152
  57.6 0.9 copy-start.5
  57.6 10.3 %copy-start.22 = (s32[128]{0:T(128)S(1)}, s32[128]{0:T(128)}, u32[]{:S(2)}) copy-start(s32[128]{0:T(128)} %copy-done.21) | copy-start | bytes 1540
  57.6 10.3 %copy-start.11 = (s32[256]{0:T(256)S(1)}, s32[256]{0:T(256)}, u32[]{:S(2)}) copy-start(s32[256]{0:T(256)} %get-tuple-element.2) | copy-start | bytes 3076
  57.6 10.3 %copy-start.18 = (s32[128]{0:T(128)S(1)}, s32[128]{0:T(128)}, u32[]{:S(2)}) copy-start(s32[128]{0:T(128)} %param.20) | copy-start | bytes 1540
  58.4 20.9 %all-to-all-start.2 = ((bf16[128,2,512]{2,1,0:T(2,128)(2,1)}), bf16[128,2,512]{2,1,0:T(2,128)(2,1)S(1)}, u32[]{:S(2)}, u32[]{:S(2)}) async-start(bf16[128,2,512]{2,1,0:T(2,128)(2,1)} %reshape.161), calls=%async_computation.2 | async-start | bytes 524288 | tf_op jit(solution)/shard_map/all_to_all | solution.py:178
  79.5 1.5 copy-start.6
  80.3 4.6 %copy-start.3 = (f32[3,512,128]{2,1,0:T(8,128)S(1)}, f32[3,512,128]{2,1,0:T(8,128)}, u32[]{:S(2)}) copy-start(f32[3,512,128]{2,1,0:T(8,128)} %param.31) | copy-start | bytes 2359300
  81.7 9.4 %copy-start.13 = (f32[4,128]{1,0:T(4,128)S(1)}, f32[4,128]{1,0:T(4,128)}, u32[]{:S(2)}) copy-start(f32[4,128]{1,0:T(4,128)} %param.32) | copy-start | bytes 6148
  82.5 13.6 %collective-permute-start.2 = (bf16[400,512]{1,0:T(8,128)(2,1)}, bf16[400,512]{1,0:T(8,128)(2,1)}, u32[]{:S(2)}, u32[]{:S(2)}) collective-permute-start(bf16[400,512]{1,0:T(8,128)(2,1)} %pad_maximum_fusion), channel_id=1, source_target_pairs={{0,3},{1,0},{2,1},{3,2},{4,7},{5,4},{6,5},{7,6},{8,11},{9,8},{10,9... | collective-permute-start | bytes 1228808 | tf_op jit(solution)/shard_map/ppermute | solution.py:195
  86.8 19.1 %collective-permute-start.1 = (bf16[400,512]{1,0:T(8,128)(2,1)}, bf16[400,512]{1,0:T(8,128)(2,1)}, u32[]{:S(2)}, u32[]{:S(2)}) collective-permute-start(bf16[400,512]{1,0:T(8,128)(2,1)} %pad_maximum_fusion), channel_id=1, source_target_pairs={{0,2},{1,3},{2,0},{3,1},{4,6},{5,7},{6,4},{7,5},{8,10},{9,11},{10,... | collective-permute-start | bytes 1228808 | tf_op jit(solution)/shard_map/ppermute | solution.py:195
  91.3 19.1 %collective-permute-start = (bf16[400,512]{1,0:T(8,128)(2,1)}, bf16[400,512]{1,0:T(8,128)(2,1)S(1)}, u32[]{:S(2)}, u32[]{:S(2)}) collective-permute-start(bf16[400,512]{1,0:T(8,128)(2,1)} %pad_maximum_fusion), channel_id=1, source_target_pairs={{0,1},{1,2},{2,3},{3,0},{4,5},{5,6},{6,7},{7,4},{8,9},{9,10},{10,1... | collective-permute-start | bytes 1228808 | tf_op jit(solution)/shard_map/ppermute | solution.py:195
  115.2 2.5 copy-start.4
  140.3 10.8 %copy-start.20 = (s32[128]{0:T(128)S(1)}, s32[128]{0:T(128)}, u32[]{:S(2)}) copy-start(s32[128]{0:T(128)} %param.23) | copy-start | bytes 1540
  140.3 10.9 %copy-start.8 = (s32[128,16,1]{0,2,1:T(1,128)S(1)}, s32[128,16,1]{0,2,1:T(1,128)}, u32[]{:S(2)}) copy-start(s32[128,16,1]{0,2,1:T(1,128)} %param.24) | copy-start | bytes 24580
  140.3 11.1 %copy-start.10 = (s32[128,16]{0,1:T(8,128)S(1)}, s32[128,16]{0,1:T(8,128)}, u32[]{:S(2)}) copy-start(s32[128,16]{0,1:T(8,128)} %param.26) | copy-start | bytes 24580
  140.3 11.3 %copy-start.14 = (f32[128]{0:T(128)S(1)}, f32[128]{0:T(128)}, u32[]{:S(2)}) copy-start(f32[128]{0:T(128)} %param.28) | copy-start | bytes 1540
  140.3 11.3 %copy-start.15 = (f32[128]{0:T(128)S(1)}, f32[128]{0:T(128)}, u32[]{:S(2)}) copy-start(f32[128]{0:T(128)} %param.27) | copy-start | bytes 1540
  140.3 113.3 %all-to-all-start.3 = ((bf16[128,32,512]{2,1,0:T(8,128)(2,1)}), bf16[128,32,512]{2,1,0:T(8,128)(2,1)}, u32[]{:S(2)}, u32[]{:S(2)}) async-start(bf16[128,32,512]{2,1,0:T(8,128)(2,1)} %bitcast.123), calls=%async_computation.3 | async-start | bytes 8388608 | tf_op jit(solution)/shard_map/all_to_all | solution.py:219
  151.1 6.0 %copy-start.7 = (bf16[512,512]{1,0:T(8,128)(2,1)S(1)}, bf16[512,512]{1,0:T(8,128)(2,1)}, u32[]{:S(2)}) copy-start(bf16[512,512]{1,0:T(8,128)(2,1)} %param.33) | copy-start | bytes 1572868

commit v8 on v7

--- a/solution.py
+++ b/solution.py
@@ -217,7 +217,7 @@
     updated = lax.all_gather(new_part.astype(jnp.bfloat16), "rep", axis=1, tiled=True)
     served = select_rows(got_nbr.reshape(-1), updated).reshape(groups, nbr_cap, -1)
     returned = lax.all_to_all(served, "nodes", split_axis=0, concat_axis=0, tiled=True)
-    fetched = returned.reshape(-1, updated.shape[1])[nbr_slot]
+    fetched = select_rows(nbr_slot, returned.reshape(-1, updated.shape[1]))
     gaps = ticks[:, None] - nbr_tick.astype(jnp.float32)
     time_enc = encode(gaps, freq, phase).reshape(-1, freq.shape[0]).astype(jnp.bfloat16)
     query = jnp.dot(updated[src_local], w_query, preferred_element_type=jnp.float32).astype(

time: 277 us -> 279 us (level)
  matrix products: 13.4 us -> 25.9 us
  local copies, waits for them, and re-layouts: 33.6 us -> 22.7 us
    dot_general x1 -> x2, matrix products: 3.95 us -> 16.2 us  [select_rows(): jnp.dot(hits, table, preferred_element_type=jnp.float32).astype(table.dtype)]
    gather x1 -> x0, local copies, waits for them, and re-layouts: 12 us -> none  [on_device(): fetched = returned.reshape(-1, updated.shape[1])[nbr_slot]]
    unnamed x56 -> x68, local copies, waits for them, and re-layouts: 6.03 us -> 7.54 us
  transfers between devices with their start and end apart: 7 -> 7, of which waited for: 7 -> 6; matrix products, arithmetic and copies ran while one was open for 7% -> 7% of each run, Pallas kernels for 0% -> 0%
where the time goes in v8:
time: 279 us; the launch traced here: 278 us
  waiting for transfers between devices  131 us (47%)
  starting transfers between devices  57.6 us (21%)
  matrix products  25.9 us (9%)
  local copies, waits for them, and re-layouts  22.7 us (8%)
  blocking collectives  15.8 us (6%)
  other arithmetic  12.2 us (4%)
  Pallas kernels  11 us (4%)
    all_to_all x1, waiting for transfers between devices, on_device(): lax.all_to_all(served, 'nodes', split_axis=0, concat_axis=0, tiled=True)  95.6 us
    all_to_all x1, starting transfers between devices, on_device(): lax.all_to_all(ints_out, 'nodes', split_axis=0, concat_axis=0, tiled=True)  17 us
    dot_general x2, matrix products, select_rows(): jnp.dot(hits, table, preferred_element_type=jnp.float32).astype(table.dtype)  16.2 us
    all_gather x1, blocking collectives, on_device(): lax.all_gather(new_part.astype(jnp.bfloat16), 'rep', axis=1, tiled=True)  15.8 us
    ppermute x3, waiting for transfers between devices, on_device(): parts.append(lax.ppermute(payload, 'rep', pairs))  13.3 us
    pallas_call x1, Pallas kernels, attend(): pl.pallas_call(attend_kernel, grid=(events // block,), in_specs=[pl.Block...  11 us
    all_to_all x1, starting transfers between devices, on_device(): lax.all_to_all(served, 'nodes', split_axis=0, concat_axis=0, tiled=True)  10.8 us
    all_to_all x1, waiting for transfers between devices, on_device(): lax.all_to_all(msg_src_slots.reshape(groups, dst_cap, -1), 'nodes', split...  10.8 us
  transfers between devices with their start and end apart: 7, of which 6 were waited for; matrix products, arithmetic and copies ran while one was open for 7% of the time, Pallas kernels for 0%

profile of v8, /device:TPU:34, one launch (start us, length us, event | category | flops | bytes accessed | tf_op | source)
XLA Modules:
  0.0 277.8 jit_solution(7441904386626976535)
XLA Ops:
  0.6 0.9 copy.48
  3.1 0.6 fusion.23
  3.8 1.6 fusion.26
  5.4 0.6 convolution_convert_fusion.1
  6.6 1.3 gather_fusion
  8.0 0.9 scatter_custom_fusion
  9.1 0.8 copy.54
  9.9 17.0 %all-to-all-start = ((s32[128,1,38]{2,1,0:T(1,128)}), s32[128,1,38]{2,1,0:T(1,128)S(1)}, u32[]{:S(2)}, u32[]{:S(2)}) async-start(s32[128,1,38]{2,1,0:T(1,128)} %copy.54), calls=%async_computation | async-start | bytes 131072 | tf_op jit(solution)/shard_map/all_to_all | solution.py:151
  27.0 1.7 scatter_custom_fusion.1
  28.7 0.8 reshape.139
  29.5 4.8 %all-to-all-done = s32[128,1,38]{2,1,0:T(1,128)S(1)} async-done(((s32[128,1,38]{2,1,0:T(1,128)}), s32[128,1,38]{2,1,0:T(1,128)S(1)}, u32[]{:S(2)}, u32[]{:S(2)}) %all-to-all-start) | async-done | bytes 19488 | tf_op jit(solution)/shard_map/all_to_all | solution.py:151
  34.3 9.8 %all-to-all-start.1 = ((bf16[128,2,512]{2,1,0:T(2,128)(2,1)}), bf16[128,2,512]{2,1,0:T(2,128)(2,1)S(1)}, u32[]{:S(2)}, u32[]{:S(2)}) async-start(bf16[128,2,512]{2,1,0:T(2,128)(2,1)} %reshape.139), calls=%async_computation.1 | async-start | bytes 524288 | tf_op jit(solution)/shard_map/all_to_all | solution.py:152
  44.4 1.9 gather_fusion.2
  46.3 1.2 gather_fusion.1
  47.9 0.9 cosine_convert_fusion.2
  48.8 6.7 %all-to-all-done.1 = bf16[128,2,512]{2,1,0:T(2,128)(2,1)S(1)} async-done(((bf16[128,2,512]{2,1,0:T(2,128)(2,1)}), bf16[128,2,512]{2,1,0:T(2,128)(2,1)S(1)}, u32[]{:S(2)}, u32[]{:S(2)}) %all-to-all-start.1) | async-done | bytes 262176 | tf_op jit(solution)/shard_map/all_to_all | solution.py:152
  55.6 1.0 multiply_convert_fusion
  56.7 0.8 reshape.141
  57.5 9.5 %all-to-all-start.2 = ((bf16[128,2,512]{2,1,0:T(2,128)(2,1)}), bf16[128,2,512]{2,1,0:T(2,128)(2,1)S(1)}, u32[]{:S(2)}, u32[]{:S(2)}) async-start(bf16[128,2,512]{2,1,0:T(2,128)(2,1)} %reshape.141), calls=%async_computation.2 | async-start | bytes 524288 | tf_op jit(solution)/shard_map/all_to_all | solution.py:178
  67.6 10.8 %all-to-all-done.2 = bf16[128,2,512]{2,1,0:T(2,128)(2,1)S(1)} async-done(((bf16[128,2,512]{2,1,0:T(2,128)(2,1)}), bf16[128,2,512]{2,1,0:T(2,128)(2,1)S(1)}, u32[]{:S(2)}, u32[]{:S(2)}) %all-to-all-start.2) | async-done | bytes 262176 | tf_op jit(solution)/shard_map/all_to_all | solution.py:178
  78.5 0.8 gather_fusion.3
  79.3 0.7 constant_dynamic-update-slice_fusion.1
  80.0 0.7 fusion.78
  80.7 0.8 pad_maximum_fusion
  81.5 2.4 collective-permute-start.2
  84.0 3.0 %convolution_bitcast_fusion = f32[3,512,128]{2,1,0:T(8,128)S(1)} fusion(f32[3,512,128]{2,1,0:T(8,128)} %param.31, f32[512,512]{1,0:T(8,128)S(1)} %copy-done.2), kind=kOutput, calls=%fused_computation.20 | convolution fusion | flops 1207959552 | bytes 2621440 | tf_op jit(solution)/shard_map/rk,gku->gru/dot_general | solution.py:211
  86.9 4.3 %collective-permute-start.1 = (bf16[400,512]{1,0:T(8,128)(2,1)}, bf16[400,512]{1,0:T(8,128)(2,1)}, u32[]{:S(2)}, u32[]{:S(2)}) collective-permute-start(bf16[400,512]{1,0:T(8,128)(2,1)} %pad_maximum_fusion), channel_id=1, source_target_pairs={{0,2},{1,3},{2,0},{3,1},{4,6},{5,7},{6,4},{7,5},{8,10},{9,11},{10,... | collective-permute-start | bytes 1228808 | tf_op jit(solution)/shard_map/ppermute | solution.py:195
  91.9 0.7 pad_maximum_fusion.2
  92.7 3.7 %collective-permute-start = (bf16[400,512]{1,0:T(8,128)(2,1)}, bf16[400,512]{1,0:T(8,128)(2,1)S(1)}, u32[]{:S(2)}, u32[]{:S(2)}) collective-permute-start(bf16[400,512]{1,0:T(8,128)(2,1)} %pad_maximum_fusion), channel_id=1, source_target_pairs={{0,1},{1,2},{2,3},{3,0},{4,5},{5,6},{6,7},{7,4},{8,9},{9,10},{10,1... | collective-permute-start | bytes 1228808 | tf_op jit(solution)/shard_map/ppermute | solution.py:195
  96.5 8.4 %collective-permute-done.1 = bf16[400,512]{1,0:T(8,128)(2,1)} collective-permute-done((bf16[400,512]{1,0:T(8,128)(2,1)}, bf16[400,512]{1,0:T(8,128)(2,1)}, u32[]{:S(2)}, u32[]{:S(2)}) %collective-permute-start.1) | collective-permute-done | bytes 409632 | tf_op jit(solution)/shard_map/ppermute | solution.py:195
  104.9 0.7 slice_bitcast_fusion.3
  105.6 4.9 %collective-permute-done = bf16[400,512]{1,0:T(8,128)(2,1)S(1)} collective-permute-done((bf16[400,512]{1,0:T(8,128)(2,1)}, bf16[400,512]{1,0:T(8,128)(2,1)S(1)}, u32[]{:S(2)}, u32[]{:S(2)}) %collective-permute-start) | collective-permute-done | bytes 409632 | tf_op jit(solution)/shard_map/ppermute | solution.py:195
  110.6 0.8 copy-done.5
  111.8 1.8 slice_dynamic-update-slice_fusion.2
  113.6 1.8 slice_dynamic-update-slice_fusion.1
  115.4 0.8 slice_dynamic-update-slice_fusion
  116.2 2.5 fusion.9
  118.7 1.8 convolution_bitcast_fusion.1
  120.5 0.9 fusion.76
  121.5 15.8 %all_gather.3 = bf16[512,512]{1,0:T(8,128)(2,1)S(1)} all-gather(bf16[512,128]{1,0:T(8,128)(2,1)S(1)} %get-tuple-element.6), channel_id=1, replica_groups=mesh['nodes'=128,'rep'=4] {'rep'}, dimensions={1}, use_global_device_ids=true | all-gather | bytes 655360 | tf_op jit(solution)/shard_map/all_gather | solution.py:217
  137.3 3.9 %fusion.3 = bf16[4096,512]{1,0:T(8,128)(2,1)} fusion(bf16[512,512]{1,0:T(8,128)(2,1)S(1)} %all_gather.3, s32[4096]{0:T(1024)S(1)} %eq.132), kind=kOutput, calls=%fused_computation.13 | convolution fusion | flops 2151677952 | bytes 4734976 | tf_op jit(solution)/shard_map/dot_general | solution.py:42
  141.3 10.8 %all-to-all-start.3 = ((bf16[128,32,512]{2,1,0:T(8,128)(2,1)}), bf16[128,32,512]{2,1,0:T(8,128)(2,1)}, u32[]{:S(2)}, u32[]{:S(2)}) async-start(bf16[128,32,512]{2,1,0:T(8,128)(2,1)} %bitcast.120), calls=%async_computation.3 | async-start | bytes 8388608 | tf_op jit(solution)/shard_map/all_to_all | solution.py:219
  152.4 4.7 %cosine_convert_fusion.tenc_ref = bf16[2048,128]{1,0:T(8,128)(2,1)} fusion(f32[128]{0:T(128)S(1)} %copy-done.22, f32[128]{0:T(128)S(1)} %copy-done.24, f32[2048]{0:T(1024)S(1)} %mul.114), kind=kLoop, calls=%fused_computation.42 | loop fusion | flops 786432 | bytes 533504 | tf_op jit(solution)/shard_map/convert_element_type | solution.py:222
  157.0 1.0 gather_fusion.4
  158.0 0.9 convolution_convert_fusion.q_ref
  158.9 95.6 %all-to-all-done.3 = bf16[128,32,512]{2,1,0:T(8,128)(2,1)} async-done(((bf16[128,32,512]{2,1,0:T(8,128)(2,1)}), bf16[128,32,512]{2,1,0:T(8,128)(2,1)}, u32[]{:S(2)}, u32[]{:S(2)}) %all-to-all-start.3) | async-done | bytes 4194336 | tf_op jit(solution)/shard_map/all_to_all | solution.py:219
  254.5 12.3 %fusion.6.fetched_ref = bf16[2048,512]{1,0:T(8,128)(2,1)} fusion(bf16[4096,512]{1,0:T(8,128)(2,1)} %bitcast.25, s32[2048]{0:T(1024)S(1)} %multiply_add_fusion), kind=kOutput, calls=%fused_computation.18 | convolution fusion | flops 8599371776 | bytes 6299648 | tf_op jit(solution)/shard_map/dot_general | solution.py:42
  266.8 11.0 %shard_map.185 = bf16[128,512]{1,0:T(8,128)(2,1)} custom-call(bf16[2048,512]{1,0:T(8,128)(2,1)} %fusion.6.fetched_ref, bf16[2048,128]{1,0:T(8,128)(2,1)} %cosine_convert_fusion.tenc_ref, bf16[128,512]{1,0:T(8,128)(2,1)} %convolution_convert_fusion.q_ref, bf16[512,1024]{1,0:T(8,128)(2,1)} %wm_ref.1, bf16[128,1024]{1,0:T(8,128)(2,1)} %wt_ref.1), custom_call_target="tpu_custom_call" | custom-call | tf_op jit(solution)/shard_map/pallas_call | solution.py:86
  (124 shorter events, 5.3 us)
Async XLA Ops:
  0.6 55.0 %copy-start = (bf16[1152,512]{1,0:T(8,128)(2,1)S(1)}, bf16[1152,512]{1,0:T(8,128)(2,1)}, u32[]{:S(2)}) copy-start(bf16[1152,512]{1,0:T(8,128)(2,1)} %param.29) | copy-start | bytes 3538948
  1.7 3.7 %copy-start.8 = (s32[2048]{0:T(1024)}, s32[2048]{0:T(1024)S(1)}, u32[]{:S(2)}) copy-start(s32[2048]{0:T(1024)S(1)} %eq.112) | copy-start | bytes 24580
  2.2 0.7 copy-start.12
  2.9 3.2 %copy-start.15 = (s32[128,1]{0,1:T(1,128)S(1)}, s32[128,1]{0,1:T(1,128)}, u32[]{:S(2)}) copy-start(s32[128,1]{0,1:T(1,128)} %param.21) | copy-start | bytes 1540
  2.9 3.6 %copy-start.26 = (s32[128]{0:T(128)S(1)}, s32[128]{0:T(128)}, u32[]{:S(2)}) copy-start(s32[128]{0:T(128)} %param.20) | copy-start | bytes 1540
  2.9 3.7 %copy-start.1 = (s32[512]{0:T(512)S(1)}, s32[512]{0:T(512)}, u32[]{:S(2)}) copy-start(s32[512]{0:T(512)} %param.19) | copy-start | bytes 6148
  3.0 4.9 %copy-start.25 = (s32[128]{0:T(128)S(1)}, s32[128]{0:T(128)}, u32[]{:S(2)}) copy-start(s32[128]{0:T(128)} %param.22) | copy-start | bytes 1540
  3.0 4.9 %copy-start.27 = (s32[128]{0:T(128)S(1)}, s32[128]{0:T(128)}, u32[]{:S(2)}) copy-start(s32[128]{0:T(128)} %param.23) | copy-start | bytes 1540
  3.8 2.3 copy-start.6
  3.8 23.1 %copy-start.2 = (f32[512,512]{1,0:T(8,128)S(1)}, f32[512,512]{1,0:T(8,128)}, u32[]{:S(2)}) copy-start(f32[512,512]{1,0:T(8,128)} %param.18) | copy-start | bytes 3145732
  6.6 37.5 %copy-start.14 = (s32[1024]{0:T(1024)}, s32[1024]{0:T(1024)S(1)}, u32[]{:S(2)}) copy-start(s32[1024]{0:T(1024)S(1)} %pad_clamp_fusion.2) | copy-start | bytes 12292
  9.9 24.4 %all-to-all-start = ((s32[128,1,38]{2,1,0:T(1,128)}), s32[128,1,38]{2,1,0:T(1,128)S(1)}, u32[]{:S(2)}, u32[]{:S(2)}) async-start(s32[128,1,38]{2,1,0:T(1,128)} %copy.54), calls=%async_computation | async-start | bytes 131072 | tf_op jit(solution)/shard_map/all_to_all | solution.py:151
  34.3 21.3 %all-to-all-start.1 = ((bf16[128,2,512]{2,1,0:T(2,128)(2,1)}), bf16[128,2,512]{2,1,0:T(2,128)(2,1)S(1)}, u32[]{:S(2)}, u32[]{:S(2)}) async-start(bf16[128,2,512]{2,1,0:T(2,128)(2,1)} %reshape.139), calls=%async_computation.1 | async-start | bytes 524288 | tf_op jit(solution)/shard_map/all_to_all | solution.py:152
  44.1 3.8 %copy-start.21 = (f32[128]{0:T(128)S(1)}, f32[128]{0:T(128)}, u32[]{:S(2)}) copy-start(f32[128]{0:T(128)} %param.28) | copy-start | bytes 1540
  44.1 3.8 %copy-start.23 = (f32[128]{0:T(128)S(1)}, f32[128]{0:T(128)}, u32[]{:S(2)}) copy-start(f32[128]{0:T(128)} %param.27) | copy-start | bytes 1540
  57.5 20.9 %all-to-all-start.2 = ((bf16[128,2,512]{2,1,0:T(2,128)(2,1)}), bf16[128,2,512]{2,1,0:T(2,128)(2,1)S(1)}, u32[]{:S(2)}, u32[]{:S(2)}) async-start(bf16[128,2,512]{2,1,0:T(2,128)(2,1)} %reshape.141), calls=%async_computation.2 | async-start | bytes 524288 | tf_op jit(solution)/shard_map/all_to_all | solution.py:178
  67.0 0.5 copy-start.10
  67.0 0.6 copy-start.11
  80.0 11.3 %copy-start.20 = (f32[4,128]{1,0:T(4,128)S(1)}, f32[4,128]{1,0:T(4,128)}, u32[]{:S(2)}) copy-start(f32[4,128]{1,0:T(4,128)} %param.32) | copy-start | bytes 6148
  81.5 14.9 %collective-permute-start.2 = (bf16[400,512]{1,0:T(8,128)(2,1)}, bf16[400,512]{1,0:T(8,128)(2,1)S(1)}, u32[]{:S(2)}, u32[]{:S(2)}) collective-permute-start(bf16[400,512]{1,0:T(8,128)(2,1)} %pad_maximum_fusion), channel_id=1, source_target_pairs={{0,3},{1,0},{2,1},{3,2},{4,7},{5,4},{6,5},{7,6},{8,11},{9,8},{10,9... | collective-permute-start | bytes 1228808 | tf_op jit(solution)/shard_map/ppermute | solution.py:195
  86.9 17.9 %collective-permute-start.1 = (bf16[400,512]{1,0:T(8,128)(2,1)}, bf16[400,512]{1,0:T(8,128)(2,1)}, u32[]{:S(2)}, u32[]{:S(2)}) collective-permute-start(bf16[400,512]{1,0:T(8,128)(2,1)} %pad_maximum_fusion), channel_id=1, source_target_pairs={{0,2},{1,3},{2,0},{3,1},{4,6},{5,7},{6,4},{7,5},{8,10},{9,11},{10,... | collective-permute-start | bytes 1228808 | tf_op jit(solution)/shard_map/ppermute | solution.py:195
  92.7 17.8 %collective-permute-start = (bf16[400,512]{1,0:T(8,128)(2,1)}, bf16[400,512]{1,0:T(8,128)(2,1)S(1)}, u32[]{:S(2)}, u32[]{:S(2)}) collective-permute-start(bf16[400,512]{1,0:T(8,128)(2,1)} %pad_maximum_fusion), channel_id=1, source_target_pairs={{0,1},{1,2},{2,3},{3,0},{4,5},{5,6},{6,7},{7,4},{8,9},{9,10},{10,1... | collective-permute-start | bytes 1228808 | tf_op jit(solution)/shard_map/ppermute | solution.py:195
  110.6 0.8 copy-start.5
  116.2 2.5 copy-start.3
  118.6 1.9 copy-start.16
  118.7 1.9 copy-start.17
  118.7 1.9 copy-start.18
  118.7 1.9 copy-start.19
  141.2 10.9 %copy-start.28 = (s32[128]{0:T(128)S(1)}, s32[128]{0:T(128)}, u32[]{:S(2)}) copy-start(s32[128]{0:T(128)} %param.23) | copy-start | bytes 1540
  141.2 10.9 %copy-start.13 = (s32[128,16]{0,1:T(8,128)S(1)}, s32[128,16]{0,1:T(8,128)}, u32[]{:S(2)}) copy-start(s32[128,16]{0,1:T(8,128)} %param.26) | copy-start | bytes 24580
  141.2 11.1 %copy-start.7 = (s32[2048]{0:T(1024)S(1)}, s32[2048]{0:T(1024)}, u32[]{:S(2)}) copy-start(s32[2048]{0:T(1024)} %copy-done.6) | copy-start | bytes 24580
  141.2 11.1 %copy-start.9 = (s32[2048]{0:T(1024)S(1)}, s32[2048]{0:T(1024)}, u32[]{:S(2)}) copy-start(s32[2048]{0:T(1024)} %copy-done.8) | copy-start | bytes 24580
  141.2 11.1 %copy-start.22 = (f32[128]{0:T(128)S(1)}, f32[128]{0:T(128)}, u32[]{:S(2)}) copy-start(f32[128]{0:T(128)} %param.28) | copy-start | bytes 1540
  141.3 11.1 %copy-start.24 = (f32[128]{0:T(128)S(1)}, f32[128]{0:T(128)}, u32[]{:S(2)}) copy-start(f32[128]{0:T(128)} %param.27) | copy-start | bytes 1540
  141.3 16.8 %copy-start.4 = (bf16[512,512]{1,0:T(8,128)(2,1)S(1)}, bf16[512,512]{1,0:T(8,128)(2,1)}, u32[]{:S(2)}) copy-start(bf16[512,512]{1,0:T(8,128)(2,1)} %param.33) | copy-start | bytes 1572868
  141.3 113.3 %all-to-all-start.3 = ((bf16[128,32,512]{2,1,0:T(8,128)(2,1)}), bf16[128,32,512]{2,1,0:T(8,128)(2,1)}, u32[]{:S(2)}, u32[]{:S(2)}) async-start(bf16[128,32,512]{2,1,0:T(8,128)(2,1)} %bitcast.120), calls=%async_computation.3 | async-start | bytes 8388608 | tf_op jit(solution)/shard_map/all_to_all | solution.py:219

commit v9 on v7

--- a/solution.py
+++ b/solution.py
@@ -79,7 +79,7 @@
     out_ref[...] = mixed.astype(out_ref.dtype)
 
 
-def attend(fetched, time_enc, query, w_keyval_mem, w_keyval_time, block=32):
+def attend(fetched, time_enc, query, w_keyval_mem, w_keyval_time, block=64):
     events, width = query.shape
     nbrs = fetched.shape[0] // events
     rows = block * nbrs

time: 277 us -> 277 us (level)
  no operation moved by 1% of the time
where the time goes in v9:
time: 277 us; the launch traced here: 276 us
  waiting for transfers between devices  131 us (47%)
  starting transfers between devices  57.6 us (21%)
  local copies, waits for them, and re-layouts  33.6 us (12%)
  blocking collectives  15.8 us (6%)
  matrix products  13.4 us (5%)
  other arithmetic  12.9 us (5%)
  Pallas kernels  10.8 us (4%)
    all_to_all x1, waiting for transfers between devices, on_device(): lax.all_to_all(served, 'nodes', split_axis=0, concat_axis=0, tiled=True)  95.5 us
    all_to_all x1, starting transfers between devices, on_device(): lax.all_to_all(ints_out, 'nodes', split_axis=0, concat_axis=0, tiled=True)  17 us
    all_gather x1, blocking collectives, on_device(): lax.all_gather(new_part.astype(jnp.bfloat16), 'rep', axis=1, tiled=True)  15.8 us
    ppermute x3, waiting for transfers between devices, on_device(): parts.append(lax.ppermute(payload, 'rep', pairs))  13.9 us
    gather x1, local copies, waits for them, and re-layouts, on_device(): fetched = returned.reshape(-1, updated.shape[1])[nbr_slot]  12 us
    all_to_all x1, waiting for transfers between devices, on_device(): lax.all_to_all(msg_src_slots.reshape(groups, dst_cap, -1), 'nodes', split...  11.3 us
    all_to_all x1, starting transfers between devices, on_device(): lax.all_to_all(served, 'nodes', split_axis=0, concat_axis=0, tiled=True)  10.8 us
    pallas_call x1, Pallas kernels, attend(): pl.pallas_call(attend_kernel, grid=(events // block,), in_specs=[pl.Block...  10.8 us
  transfers between devices with their start and end apart: 7, of which 7 were waited for; matrix products, arithmetic and copies ran while one was open for 7% of the time, Pallas kernels for 0%

profile of v9, /device:TPU:34, one launch (start us, length us, event | category | flops | bytes accessed | tf_op | source)
XLA Modules:
  0.0 276.3 jit_solution(10466867749720908370)
XLA Ops:
  0.6 0.9 copy.50
  3.2 0.6 fusion.20
  3.9 1.6 fusion.23
  6.7 1.3 gather_fusion
  8.1 0.9 scatter_custom_fusion
  9.2 0.8 copy.56
  9.9 17.0 %all-to-all-start = ((s32[128,1,38]{2,1,0:T(1,128)}), s32[128,1,38]{2,1,0:T(1,128)S(1)}, u32[]{:S(2)}, u32[]{:S(2)}) async-start(s32[128,1,38]{2,1,0:T(1,128)} %copy.56), calls=%async_computation | async-start | bytes 131072 | tf_op jit(solution)/shard_map/all_to_all | solution.py:151
  27.1 1.7 scatter_custom_fusion.1
  28.8 0.8 reshape.159
  29.6 4.8 %all-to-all-done = s32[128,1,38]{2,1,0:T(1,128)S(1)} async-done(((s32[128,1,38]{2,1,0:T(1,128)}), s32[128,1,38]{2,1,0:T(1,128)S(1)}, u32[]{:S(2)}, u32[]{:S(2)}) %all-to-all-start) | async-done | bytes 19488 | tf_op jit(solution)/shard_map/all_to_all | solution.py:151
  34.3 9.8 %all-to-all-start.1 = ((bf16[128,2,512]{2,1,0:T(2,128)(2,1)}), bf16[128,2,512]{2,1,0:T(2,128)(2,1)S(1)}, u32[]{:S(2)}, u32[]{:S(2)}) async-start(bf16[128,2,512]{2,1,0:T(2,128)(2,1)} %reshape.159), calls=%async_computation.1 | async-start | bytes 524288 | tf_op jit(solution)/shard_map/all_to_all | solution.py:152
  44.3 0.7 slice_reduce_fusion
  45.0 1.9 gather_fusion.2
  46.9 1.2 gather_fusion.1
  48.5 1.8 cosine_convert_fusion.2
  50.3 5.3 %all-to-all-done.1 = bf16[128,2,512]{2,1,0:T(2,128)(2,1)S(1)} async-done(((bf16[128,2,512]{2,1,0:T(2,128)(2,1)}), bf16[128,2,512]{2,1,0:T(2,128)(2,1)S(1)}, u32[]{:S(2)}, u32[]{:S(2)}) %all-to-all-start.1) | async-done | bytes 262176 | tf_op jit(solution)/shard_map/all_to_all | solution.py:152
  55.7 1.8 multiply_convert_fusion
  57.6 0.8 reshape.161
  58.4 9.5 %all-to-all-start.2 = ((bf16[128,2,512]{2,1,0:T(2,128)(2,1)}), bf16[128,2,512]{2,1,0:T(2,128)(2,1)S(1)}, u32[]{:S(2)}, u32[]{:S(2)}) async-start(bf16[128,2,512]{2,1,0:T(2,128)(2,1)} %reshape.161), calls=%async_computation.2 | async-start | bytes 524288 | tf_op jit(solution)/shard_map/all_to_all | solution.py:178
  68.0 11.3 %all-to-all-done.2 = bf16[128,2,512]{2,1,0:T(2,128)(2,1)S(1)} async-done(((bf16[128,2,512]{2,1,0:T(2,128)(2,1)}), bf16[128,2,512]{2,1,0:T(2,128)(2,1)S(1)}, u32[]{:S(2)}, u32[]{:S(2)}) %all-to-all-start.2) | async-done | bytes 262176 | tf_op jit(solution)/shard_map/all_to_all | solution.py:178
  79.5 0.8 gather_fusion.3
  80.3 0.7 constant_dynamic-update-slice_fusion.1
  81.0 0.7 fusion.75
  81.7 0.8 pad_maximum_fusion
  82.5 2.4 collective-permute-start.2
  84.9 1.8 convolution_bitcast_fusion
  86.8 4.3 %collective-permute-start.1 = (bf16[400,512]{1,0:T(8,128)(2,1)}, bf16[400,512]{1,0:T(8,128)(2,1)}, u32[]{:S(2)}, u32[]{:S(2)}) collective-permute-start(bf16[400,512]{1,0:T(8,128)(2,1)} %pad_maximum_fusion), channel_id=1, source_target_pairs={{0,2},{1,3},{2,0},{3,1},{4,6},{5,7},{6,4},{7,5},{8,10},{9,11},{10,... | collective-permute-start | bytes 1228808 | tf_op jit(solution)/shard_map/ppermute | solution.py:195
  91.3 3.7 %collective-permute-start = (bf16[400,512]{1,0:T(8,128)(2,1)}, bf16[400,512]{1,0:T(8,128)(2,1)S(1)}, u32[]{:S(2)}, u32[]{:S(2)}) collective-permute-start(bf16[400,512]{1,0:T(8,128)(2,1)} %pad_maximum_fusion), channel_id=1, source_target_pairs={{0,1},{1,2},{2,3},{3,0},{4,5},{5,6},{6,7},{7,4},{8,9},{9,10},{10,1... | collective-permute-start | bytes 1228808 | tf_op jit(solution)/shard_map/ppermute | solution.py:195
  95.0 1.1 collective-permute-done.2
  96.1 0.7 slice_bitcast_fusion.2
  96.9 9.0 %collective-permute-done.1 = bf16[400,512]{1,0:T(8,128)(2,1)} collective-permute-done((bf16[400,512]{1,0:T(8,128)(2,1)}, bf16[400,512]{1,0:T(8,128)(2,1)}, u32[]{:S(2)}, u32[]{:S(2)}) %collective-permute-start.1) | collective-permute-done | bytes 409632 | tf_op jit(solution)/shard_map/ppermute | solution.py:195
  105.8 0.7 slice_bitcast_fusion.3
  106.6 3.8 %collective-permute-done = bf16[400,512]{1,0:T(8,128)(2,1)S(1)} collective-permute-done((bf16[400,512]{1,0:T(8,128)(2,1)}, bf16[400,512]{1,0:T(8,128)(2,1)S(1)}, u32[]{:S(2)}, u32[]{:S(2)}) %collective-permute-start) | collective-permute-done | bytes 409632 | tf_op jit(solution)/shard_map/ppermute | solution.py:195
  110.9 0.8 slice_dynamic-update-slice_fusion.2
  111.7 1.8 slice_dynamic-update-slice_fusion.1
  113.5 1.8 slice_dynamic-update-slice_fusion
  115.3 2.5 fusion.6
  117.7 1.8 convolution_bitcast_fusion.1
  119.6 0.9 fusion.73
  120.5 15.8 %all_gather.3 = bf16[512,512]{1,0:T(8,128)(2,1)S(1)} all-gather(bf16[512,128]{1,0:T(8,128)(2,1)S(1)} %get-tuple-element.6), channel_id=1, replica_groups=mesh['nodes'=128,'rep'=4] {'rep'}, dimensions={1}, use_global_device_ids=true | all-gather | bytes 655360 | tf_op jit(solution)/shard_map/all_gather | solution.py:217
  136.3 4.0 %fusion.1 = bf16[4096,512]{1,0:T(8,128)(2,1)} fusion(bf16[512,512]{1,0:T(8,128)(2,1)S(1)} %all_gather.3, s32[4096]{0:T(1024)S(1)} %eq.116), kind=kOutput, calls=%fused_computation.11 | convolution fusion | flops 2151677952 | bytes 4734976 | tf_op jit(solution)/shard_map/dot_general | solution.py:42
  140.3 10.8 %all-to-all-start.3 = ((bf16[128,32,512]{2,1,0:T(8,128)(2,1)}), bf16[128,32,512]{2,1,0:T(8,128)(2,1)}, u32[]{:S(2)}, u32[]{:S(2)}) async-start(bf16[128,32,512]{2,1,0:T(8,128)(2,1)} %bitcast.123), calls=%async_computation.3 | async-start | bytes 8388608 | tf_op jit(solution)/shard_map/all_to_all | solution.py:219
  151.6 4.7 %cosine_convert_fusion.tenc_ref = bf16[2048,128]{1,0:T(8,128)(2,1)} fusion(f32[128]{0:T(128)S(1)} %copy-done.14, f32[128]{0:T(128)S(1)} %copy-done.15, f32[2048]{0:T(1024)S(1)} %mul.121), kind=kLoop, calls=%fused_computation.39 | loop fusion | flops 786432 | bytes 533504 | tf_op jit(solution)/shard_map/convert_element_type | solution.py:222
  156.3 0.8 gather_fusion.5
  157.1 0.9 convolution_convert_fusion.q_ref
  158.0 95.5 %all-to-all-done.3 = bf16[128,32,512]{2,1,0:T(8,128)(2,1)} async-done(((bf16[128,32,512]{2,1,0:T(8,128)(2,1)}), bf16[128,32,512]{2,1,0:T(8,128)(2,1)}, u32[]{:S(2)}, u32[]{:S(2)}) %all-to-all-start.3) | async-done | bytes 4194336 | tf_op jit(solution)/shard_map/all_to_all | solution.py:219
  253.6 12.0 %gather_fusion.4 = bf16[2048,512]{1,0:T(8,128)(2,1)} fusion(bf16[4096,512]{1,0:T(8,128)(2,1)} %bitcast.25, s32[2048]{0:T(1024)S(1)} %broadcast_clamp_fusion), kind=kCustom, calls=%fused_computation.5 | custom fusion | bytes 4202496 | tf_op jit(solution)/shard_map/gather | solution.py:220
  265.5 10.8 %shard_map.185 = bf16[128,512]{1,0:T(8,128)(2,1)} custom-call(bf16[2048,512]{1,0:T(8,128)(2,1)} %gather_fusion.4, bf16[2048,128]{1,0:T(8,128)(2,1)} %cosine_convert_fusion.tenc_ref, bf16[128,512]{1,0:T(8,128)(2,1)} %convolution_convert_fusion.q_ref, bf16[512,1024]{1,0:T(8,128)(2,1)} %wm_ref.1, bf16[128,1024]{1,0:T(8,128)(2,1)} %wt_ref.1), custom_call_target="tpu_custom_call" | custom-call | tf_op jit(solution)/shard_map/pallas_call | solution.py:86
  (116 shorter events, 5.0 us)
Async XLA Ops:
  0.6 55.1 %copy-start = (bf16[1152,512]{1,0:T(8,128)(2,1)S(1)}, bf16[1152,512]{1,0:T(8,128)(2,1)}, u32[]{:S(2)}) copy-start(bf16[1152,512]{1,0:T(8,128)(2,1)} %param.29) | copy-start | bytes 3538948
  2.3 0.7 copy-start.9
  3.2 3.0 %copy-start.12 = (s32[128,1]{0,1:T(1,128)S(1)}, s32[128,1]{0,1:T(1,128)}, u32[]{:S(2)}) copy-start(s32[128,1]{0,1:T(1,128)} %param.21) | copy-start | bytes 1540
  3.2 3.4 %copy-start.17 = (s32[128]{0:T(128)S(1)}, s32[128]{0:T(128)}, u32[]{:S(2)}) copy-start(s32[128]{0:T(128)} %param.20) | copy-start | bytes 1540
  3.2 3.5 %copy-start.1 = (s32[512]{0:T(512)S(1)}, s32[512]{0:T(512)}, u32[]{:S(2)}) copy-start(s32[512]{0:T(512)} %param.19) | copy-start | bytes 6148
  3.9 4.1 %copy-start.16 = (s32[128]{0:T(128)S(1)}, s32[128]{0:T(128)}, u32[]{:S(2)}) copy-start(s32[128]{0:T(128)} %param.22) | copy-start | bytes 1540
  3.9 4.1 %copy-start.19 = (s32[128]{0:T(128)S(1)}, s32[128]{0:T(128)}, u32[]{:S(2)}) copy-start(s32[128]{0:T(128)} %param.23) | copy-start | bytes 1540
  5.5 21.5 %copy-start.2 = (f32[512,512]{1,0:T(8,128)S(1)}, f32[512,512]{1,0:T(8,128)}, u32[]{:S(2)}) copy-start(f32[512,512]{1,0:T(8,128)} %param.18) | copy-start | bytes 3145732
  6.6 22.9 %copy-start.21 = (s32[128]{0:T(128)}, s32[128]{0:T(128)S(1)}, u32[]{:S(2)}) copy-start(s32[128]{0:T(128)S(1)} %fusion.70) | copy-start | bytes 1540
  9.9 24.4 %all-to-all-start = ((s32[128,1,38]{2,1,0:T(1,128)}), s32[128,1,38]{2,1,0:T(1,128)S(1)}, u32[]{:S(2)}, u32[]{:S(2)}) async-start(s32[128,1,38]{2,1,0:T(1,128)} %copy.56), calls=%async_computation | async-start | bytes 131072 | tf_op jit(solution)/shard_map/all_to_all | solution.py:151
  34.3 21.3 %all-to-all-start.1 = ((bf16[128,2,512]{2,1,0:T(2,128)(2,1)}), bf16[128,2,512]{2,1,0:T(2,128)(2,1)S(1)}, u32[]{:S(2)}, u32[]{:S(2)}) async-start(bf16[128,2,512]{2,1,0:T(2,128)(2,1)} %reshape.159), calls=%async_computation.1 | async-start | bytes 524288 | tf_op jit(solution)/shard_map/all_to_all | solution.py:152
  57.6 0.9 copy-start.5
  57.6 10.3 %copy-start.22 = (s32[128]{0:T(128)S(1)}, s32[128]{0:T(128)}, u32[]{:S(2)}) copy-start(s32[128]{0:T(128)} %copy-done.21) | copy-start | bytes 1540
  57.6 10.3 %copy-start.11 = (s32[256]{0:T(256)S(1)}, s32[256]{0:T(256)}, u32[]{:S(2)}) copy-start(s32[256]{0:T(256)} %get-tuple-element.2) | copy-start | bytes 3076
  57.6 10.3 %copy-start.18 = (s32[128]{0:T(128)S(1)}, s32[128]{0:T(128)}, u32[]{:S(2)}) copy-start(s32[128]{0:T(128)} %param.20) | copy-start | bytes 1540
  58.4 20.9 %all-to-all-start.2 = ((bf16[128,2,512]{2,1,0:T(2,128)(2,1)}), bf16[128,2,512]{2,1,0:T(2,128)(2,1)S(1)}, u32[]{:S(2)}, u32[]{:S(2)}) async-start(bf16[128,2,512]{2,1,0:T(2,128)(2,1)} %reshape.161), calls=%async_computation.2 | async-start | bytes 524288 | tf_op jit(solution)/shard_map/all_to_all | solution.py:178
  79.5 1.5 copy-start.6
  80.3 4.6 %copy-start.3 = (f32[3,512,128]{2,1,0:T(8,128)S(1)}, f32[3,512,128]{2,1,0:T(8,128)}, u32[]{:S(2)}) copy-start(f32[3,512,128]{2,1,0:T(8,128)} %param.31) | copy-start | bytes 2359300
  81.7 9.4 %copy-start.13 = (f32[4,128]{1,0:T(4,128)S(1)}, f32[4,128]{1,0:T(4,128)}, u32[]{:S(2)}) copy-start(f32[4,128]{1,0:T(4,128)} %param.32) | copy-start | bytes 6148
  82.5 13.6 %collective-permute-start.2 = (bf16[400,512]{1,0:T(8,128)(2,1)}, bf16[400,512]{1,0:T(8,128)(2,1)}, u32[]{:S(2)}, u32[]{:S(2)}) collective-permute-start(bf16[400,512]{1,0:T(8,128)(2,1)} %pad_maximum_fusion), channel_id=1, source_target_pairs={{0,3},{1,0},{2,1},{3,2},{4,7},{5,4},{6,5},{7,6},{8,11},{9,8},{10,9... | collective-permute-start | bytes 1228808 | tf_op jit(solution)/shard_map/ppermute | solution.py:195
  86.8 19.1 %collective-permute-start.1 = (bf16[400,512]{1,0:T(8,128)(2,1)}, bf16[400,512]{1,0:T(8,128)(2,1)}, u32[]{:S(2)}, u32[]{:S(2)}) collective-permute-start(bf16[400,512]{1,0:T(8,128)(2,1)} %pad_maximum_fusion), channel_id=1, source_target_pairs={{0,2},{1,3},{2,0},{3,1},{4,6},{5,7},{6,4},{7,5},{8,10},{9,11},{10,... | collective-permute-start | bytes 1228808 | tf_op jit(solution)/shard_map/ppermute | solution.py:195
  91.3 19.1 %collective-permute-start = (bf16[400,512]{1,0:T(8,128)(2,1)}, bf16[400,512]{1,0:T(8,128)(2,1)S(1)}, u32[]{:S(2)}, u32[]{:S(2)}) collective-permute-start(bf16[400,512]{1,0:T(8,128)(2,1)} %pad_maximum_fusion), channel_id=1, source_target_pairs={{0,1},{1,2},{2,3},{3,0},{4,5},{5,6},{6,7},{7,4},{8,9},{9,10},{10,1... | collective-permute-start | bytes 1228808 | tf_op jit(solution)/shard_map/ppermute | solution.py:195
  115.2 2.5 copy-start.4
  140.3 10.8 %copy-start.20 = (s32[128]{0:T(128)S(1)}, s32[128]{0:T(128)}, u32[]{:S(2)}) copy-start(s32[128]{0:T(128)} %param.23) | copy-start | bytes 1540
  140.3 10.9 %copy-start.8 = (s32[128,16,1]{0,2,1:T(1,128)S(1)}, s32[128,16,1]{0,2,1:T(1,128)}, u32[]{:S(2)}) copy-start(s32[128,16,1]{0,2,1:T(1,128)} %param.24) | copy-start | bytes 24580
  140.3 11.1 %copy-start.10 = (s32[128,16]{0,1:T(8,128)S(1)}, s32[128,16]{0,1:T(8,128)}, u32[]{:S(2)}) copy-start(s32[128,16]{0,1:T(8,128)} %param.26) | copy-start | bytes 24580
  140.3 11.3 %copy-start.14 = (f32[128]{0:T(128)S(1)}, f32[128]{0:T(128)}, u32[]{:S(2)}) copy-start(f32[128]{0:T(128)} %param.28) | copy-start | bytes 1540
  140.3 11.3 %copy-start.15 = (f32[128]{0:T(128)S(1)}, f32[128]{0:T(128)}, u32[]{:S(2)}) copy-start(f32[128]{0:T(128)} %param.27) | copy-start | bytes 1540
  140.3 113.3 %all-to-all-start.3 = ((bf16[128,32,512]{2,1,0:T(8,128)(2,1)}), bf16[128,32,512]{2,1,0:T(8,128)(2,1)}, u32[]{:S(2)}, u32[]{:S(2)}) async-start(bf16[128,32,512]{2,1,0:T(8,128)(2,1)} %bitcast.123), calls=%async_computation.3 | async-start | bytes 8388608 | tf_op jit(solution)/shard_map/all_to_all | solution.py:219
  151.1 6.0 %copy-start.7 = (bf16[512,512]{1,0:T(8,128)(2,1)S(1)}, bf16[512,512]{1,0:T(8,128)(2,1)}, u32[]{:S(2)}) copy-start(bf16[512,512]{1,0:T(8,128)(2,1)} %param.33) | copy-start | bytes 1572868

commit v10 on v9

--- a/solution.py
+++ b/solution.py
@@ -141,12 +141,10 @@
         .reshape(groups, dst_cap * 3)
     )
     nbr_ids = scatter_ids(nbr_hot, nbr_rank, nbr_local.reshape(-1), nbr_cap)
-    req_rows = (
-        jnp.zeros((groups * dst_cap, width_m), jnp.bfloat16)
-        .at[dst_slot]
-        .set(near_rows)
-        .reshape(groups, dst_cap, width_m)
-    )
+    req_rows = select_rows(
+        jnp.full((groups * dst_cap,), -1, jnp.int32).at[dst_slot].set(jnp.arange(events, dtype=jnp.int32)),
+        near_rows,
+    ).reshape(groups, dst_cap, width_m)
     ints_out = jnp.concatenate([req_ints, nbr_ids], axis=1)
     ints_in = lax.all_to_all(ints_out, "nodes", split_axis=0, concat_axis=0, tiled=True)
     rows_in = lax.all_to_all(req_rows, "nodes", split_axis=0, concat_axis=0, tiled=True)

time: 277 us -> 279 us (level)
  the two profiles are of different devices: /device:TPU:34 before, /device:TPU:43 now
where the time goes in v10:
time: 279 us
  waiting for transfers between devices  134 us (48%)
  starting transfers between devices  57.7 us (21%)
  local copies, waits for them, and re-layouts  33.8 us (12%)
  blocking collectives  13.9 us (5%)
  matrix products  13.7 us (5%)
  other arithmetic  12.9 us (5%)
  Pallas kernels  10.8 us (4%)
    all_to_all x1, waiting for transfers between devices, on_device(): lax.all_to_all(served, 'nodes', split_axis=0, concat_axis=0, tiled=True)  97.7 us
    all_to_all x1, starting transfers between devices, on_device(): lax.all_to_all(ints_out, 'nodes', split_axis=0, concat_axis=0, tiled=True)  17.2 us
    all_gather x1, blocking collectives, on_device(): lax.all_gather(new_part.astype(jnp.bfloat16), 'rep', axis=1, tiled=True)  13.9 us
    ppermute x3, waiting for transfers between devices, on_device(): parts.append(lax.ppermute(payload, 'rep', pairs))  13.7 us
    all_to_all x1, starting transfers between devices, on_device(): lax.all_to_all(served, 'nodes', split_axis=0, concat_axis=0, tiled=True)  12.8 us
    all_to_all x1, waiting for transfers between devices, on_device(): lax.all_to_all(msg_src_slots.reshape(groups, dst_cap, -1), 'nodes', split...  12 us
    gather x1, local copies, waits for them, and re-layouts, on_device(): fetched = returned.reshape(-1, updated.shape[1])[nbr_slot]  12 us
    pallas_call x1, Pallas kernels, attend(): pl.pallas_call(attend_kernel, grid=(events // block,), in_specs=[pl.Block...  10.8 us
  transfers between devices with their start and end apart: 7, of which 7 were waited for; matrix products, arithmetic and copies ran while one was open for 7% of the time, Pallas kernels for 0%

profile of v10, /device:TPU:43, one launch (start us, length us, event | category | flops | bytes accessed | tf_op | source)
XLA Modules:
  0.0 278.6 jit_solution(7256549404436837340)
XLA Ops:
  0.6 0.9 copy.50
  3.9 1.6 fusion.23
  6.7 1.3 gather_fusion
  8.1 0.9 scatter_custom_fusion
  9.2 0.8 copy.56
  9.9 17.2 %all-to-all-start = ((s32[128,1,38]{2,1,0:T(1,128)}), s32[128,1,38]{2,1,0:T(1,128)S(1)}, u32[]{:S(2)}, u32[]{:S(2)}) async-start(s32[128,1,38]{2,1,0:T(1,128)} %copy.56), calls=%async_computation | async-start | bytes 131072 | tf_op jit(solution)/shard_map/all_to_all | solution.py:149
  27.2 0.8 gather_fusion.1
  28.1 1.0 scatter_custom_fusion.1
  29.4 0.8 reshape.160
  30.2 5.0 %all-to-all-done = s32[128,1,38]{2,1,0:T(1,128)S(1)} async-done(((s32[128,1,38]{2,1,0:T(1,128)}), s32[128,1,38]{2,1,0:T(1,128)S(1)}, u32[]{:S(2)}, u32[]{:S(2)}) %all-to-all-start) | async-done | bytes 19488 | tf_op jit(solution)/shard_map/all_to_all | solution.py:149
  35.2 9.2 %all-to-all-start.1 = ((bf16[128,2,512]{2,1,0:T(2,128)(2,1)}), bf16[128,2,512]{2,1,0:T(2,128)(2,1)S(1)}, u32[]{:S(2)}, u32[]{:S(2)}) async-start(bf16[128,2,512]{2,1,0:T(2,128)(2,1)} %reshape.160), calls=%async_computation.1 | async-start | bytes 524288 | tf_op jit(solution)/shard_map/all_to_all | solution.py:150
  44.5 0.7 slice_reduce_fusion
  45.1 1.9 gather_fusion.3
  47.1 1.2 gather_fusion.2
  48.6 1.8 cosine_convert_fusion.2
  50.5 6.1 %all-to-all-done.1 = bf16[128,2,512]{2,1,0:T(2,128)(2,1)S(1)} async-done(((bf16[128,2,512]{2,1,0:T(2,128)(2,1)}), bf16[128,2,512]{2,1,0:T(2,128)(2,1)S(1)}, u32[]{:S(2)}, u32[]{:S(2)}) %all-to-all-start.1) | async-done | bytes 262176 | tf_op jit(solution)/shard_map/all_to_all | solution.py:150
  56.7 1.8 multiply_convert_fusion
  58.6 0.8 reshape.162
  59.4 8.9 %all-to-all-start.2 = ((bf16[128,2,512]{2,1,0:T(2,128)(2,1)}), bf16[128,2,512]{2,1,0:T(2,128)(2,1)S(1)}, u32[]{:S(2)}, u32[]{:S(2)}) async-start(bf16[128,2,512]{2,1,0:T(2,128)(2,1)} %reshape.162), calls=%async_computation.2 | async-start | bytes 524288 | tf_op jit(solution)/shard_map/all_to_all | solution.py:176
  68.4 12.0 %all-to-all-done.2 = bf16[128,2,512]{2,1,0:T(2,128)(2,1)S(1)} async-done(((bf16[128,2,512]{2,1,0:T(2,128)(2,1)}), bf16[128,2,512]{2,1,0:T(2,128)(2,1)S(1)}, u32[]{:S(2)}, u32[]{:S(2)}) %all-to-all-start.2) | async-done | bytes 262176 | tf_op jit(solution)/shard_map/all_to_all | solution.py:176
  80.6 0.8 gather_fusion.4
  81.4 0.7 constant_dynamic-update-slice_fusion.1
  82.1 0.7 fusion.75
  82.8 0.8 pad_maximum_fusion
  83.6 2.2 collective-permute-start.2
  85.8 1.8 convolution_bitcast_fusion
  87.6 4.1 %collective-permute-start.1 = (bf16[400,512]{1,0:T(8,128)(2,1)}, bf16[400,512]{1,0:T(8,128)(2,1)}, u32[]{:S(2)}, u32[]{:S(2)}) collective-permute-start(bf16[400,512]{1,0:T(8,128)(2,1)} %pad_maximum_fusion), channel_id=1, source_target_pairs={{0,2},{1,3},{2,0},{3,1},{4,6},{5,7},{6,4},{7,5},{8,10},{9,11},{10,... | collective-permute-start | bytes 1228808 | tf_op jit(solution)/shard_map/ppermute | solution.py:193
  91.9 3.4 %collective-permute-start = (bf16[400,512]{1,0:T(8,128)(2,1)}, bf16[400,512]{1,0:T(8,128)(2,1)S(1)}, u32[]{:S(2)}, u32[]{:S(2)}) collective-permute-start(bf16[400,512]{1,0:T(8,128)(2,1)} %pad_maximum_fusion), channel_id=1, source_target_pairs={{0,1},{1,2},{2,3},{3,0},{4,5},{5,6},{6,7},{7,4},{8,9},{9,10},{10,1... | collective-permute-start | bytes 1228808 | tf_op jit(solution)/shard_map/ppermute | solution.py:193
  95.3 1.1 collective-permute-done.2
  96.4 0.7 slice_bitcast_fusion.2
  97.2 9.0 %collective-permute-done.1 = bf16[400,512]{1,0:T(8,128)(2,1)} collective-permute-done((bf16[400,512]{1,0:T(8,128)(2,1)}, bf16[400,512]{1,0:T(8,128)(2,1)}, u32[]{:S(2)}, u32[]{:S(2)}) %collective-permute-start.1) | collective-permute-done | bytes 409632 | tf_op jit(solution)/shard_map/ppermute | solution.py:193
  106.1 0.7 slice_bitcast_fusion.3
  106.9 3.6 %collective-permute-done = bf16[400,512]{1,0:T(8,128)(2,1)S(1)} collective-permute-done((bf16[400,512]{1,0:T(8,128)(2,1)}, bf16[400,512]{1,0:T(8,128)(2,1)S(1)}, u32[]{:S(2)}, u32[]{:S(2)}) %collective-permute-start) | collective-permute-done | bytes 409632 | tf_op jit(solution)/shard_map/ppermute | solution.py:193
  111.0 0.8 slice_dynamic-update-slice_fusion.2
  111.8 1.8 slice_dynamic-update-slice_fusion.1
  113.6 1.8 slice_dynamic-update-slice_fusion
  115.3 2.5 fusion.6
  117.8 1.8 convolution_bitcast_fusion.1
  119.6 0.9 fusion.73
  120.6 13.9 %all_gather.3 = bf16[512,512]{1,0:T(8,128)(2,1)S(1)} all-gather(bf16[512,128]{1,0:T(8,128)(2,1)S(1)} %get-tuple-element.6), channel_id=1, replica_groups=mesh['nodes'=128,'rep'=4] {'rep'}, dimensions={1}, use_global_device_ids=true | all-gather | bytes 655360 | tf_op jit(solution)/shard_map/all_gather | solution.py:215
  134.5 4.0 %fusion.1 = bf16[4096,512]{1,0:T(8,128)(2,1)} fusion(bf16[512,512]{1,0:T(8,128)(2,1)S(1)} %all_gather.3, s32[4096]{0:T(1024)S(1)} %eq.132), kind=kOutput, calls=%fused_computation.11 | convolution fusion | flops 2151677952 | bytes 4734976 | tf_op jit(solution)/shard_map/dot_general | solution.py:42
  138.5 12.8 %all-to-all-start.3 = ((bf16[128,32,512]{2,1,0:T(8,128)(2,1)}), bf16[128,32,512]{2,1,0:T(8,128)(2,1)}, u32[]{:S(2)}, u32[]{:S(2)}) async-start(bf16[128,32,512]{2,1,0:T(8,128)(2,1)} %bitcast.124), calls=%async_computation.3 | async-start | bytes 8388608 | tf_op jit(solution)/shard_map/all_to_all | solution.py:217
  151.8 4.7 %cosine_convert_fusion.tenc_ref = bf16[2048,128]{1,0:T(8,128)(2,1)} fusion(f32[128]{0:T(128)S(1)} %copy-done.14, f32[128]{0:T(128)S(1)} %copy-done.15, f32[2048]{0:T(1024)S(1)} %mul.121), kind=kLoop, calls=%fused_computation.40 | loop fusion | flops 786432 | bytes 533504 | tf_op jit(solution)/shard_map/convert_element_type | solution.py:220
  156.5 0.8 gather_fusion.6
  157.3 0.9 convolution_convert_fusion.1.q_ref
  158.2 97.7 %all-to-all-done.3 = bf16[128,32,512]{2,1,0:T(8,128)(2,1)} async-done(((bf16[128,32,512]{2,1,0:T(8,128)(2,1)}), bf16[128,32,512]{2,1,0:T(8,128)(2,1)}, u32[]{:S(2)}, u32[]{:S(2)}) %all-to-all-start.3) | async-done | bytes 4194336 | tf_op jit(solution)/shard_map/all_to_all | solution.py:217
  255.9 12.0 %gather_fusion.5 = bf16[2048,512]{1,0:T(8,128)(2,1)} fusion(bf16[4096,512]{1,0:T(8,128)(2,1)} %bitcast.25, s32[2048]{0:T(1024)S(1)} %broadcast_clamp_fusion), kind=kCustom, calls=%fused_computation.5 | custom fusion | bytes 4202496 | tf_op jit(solution)/shard_map/gather | solution.py:218
  267.8 10.8 %shard_map.185 = bf16[128,512]{1,0:T(8,128)(2,1)} custom-call(bf16[2048,512]{1,0:T(8,128)(2,1)} %gather_fusion.5, bf16[2048,128]{1,0:T(8,128)(2,1)} %cosine_convert_fusion.tenc_ref, bf16[128,512]{1,0:T(8,128)(2,1)} %convolution_convert_fusion.1.q_ref, bf16[512,1024]{1,0:T(8,128)(2,1)} %wm_ref.1, bf16[128,1024]{1,0:T(8,128)(2,1)} %wt_ref.1), custom_call_target="tpu_custom_call" | custom-call | tf_op jit(solution)/shard_map/pallas_call | solution.py:86
  (119 shorter events, 5.9 us)
Async XLA Ops:
  0.6 56.0 %copy-start = (bf16[1152,512]{1,0:T(8,128)(2,1)S(1)}, bf16[1152,512]{1,0:T(8,128)(2,1)}, u32[]{:S(2)}) copy-start(bf16[1152,512]{1,0:T(8,128)(2,1)} %param.29) | copy-start | bytes 3538948
  2.3 0.7 copy-start.9
  3.2 3.0 %copy-start.12 = (s32[128,1]{0,1:T(1,128)S(1)}, s32[128,1]{0,1:T(1,128)}, u32[]{:S(2)}) copy-start(s32[128,1]{0,1:T(1,128)} %param.21) | copy-start | bytes 1540
  3.2 3.4 %copy-start.17 = (s32[128]{0:T(128)S(1)}, s32[128]{0:T(128)}, u32[]{:S(2)}) copy-start(s32[128]{0:T(128)} %param.20) | copy-start | bytes 1540
  3.2 3.5 %copy-start.1 = (s32[512]{0:T(512)S(1)}, s32[512]{0:T(512)}, u32[]{:S(2)}) copy-start(s32[512]{0:T(512)} %param.19) | copy-start | bytes 6148
  3.9 4.1 %copy-start.16 = (s32[128]{0:T(128)S(1)}, s32[128]{0:T(128)}, u32[]{:S(2)}) copy-start(s32[128]{0:T(128)} %param.22) | copy-start | bytes 1540
  3.9 4.1 %copy-start.19 = (s32[128]{0:T(128)S(1)}, s32[128]{0:T(128)}, u32[]{:S(2)}) copy-start(s32[128]{0:T(128)} %param.23) | copy-start | bytes 1540
  5.5 21.6 %copy-start.2 = (f32[512,512]{1,0:T(8,128)S(1)}, f32[512,512]{1,0:T(8,128)}, u32[]{:S(2)}) copy-start(f32[512,512]{1,0:T(8,128)} %param.18) | copy-start | bytes 3145732
  6.6 21.4 %copy-start.21 = (s32[128]{0:T(128)}, s32[128]{0:T(128)S(1)}, u32[]{:S(2)}) copy-start(s32[128]{0:T(128)S(1)} %fusion.68) | copy-start | bytes 1540
  9.9 25.2 %all-to-all-start = ((s32[128,1,38]{2,1,0:T(1,128)}), s32[128,1,38]{2,1,0:T(1,128)S(1)}, u32[]{:S(2)}, u32[]{:S(2)}) async-start(s32[128,1,38]{2,1,0:T(1,128)} %copy.56), calls=%async_computation | async-start | bytes 131072 | tf_op jit(solution)/shard_map/all_to_all | solution.py:149
  35.2 21.4 %all-to-all-start.1 = ((bf16[128,2,512]{2,1,0:T(2,128)(2,1)}), bf16[128,2,512]{2,1,0:T(2,128)(2,1)S(1)}, u32[]{:S(2)}, u32[]{:S(2)}) async-start(bf16[128,2,512]{2,1,0:T(2,128)(2,1)} %reshape.160), calls=%async_computation.1 | async-start | bytes 524288 | tf_op jit(solution)/shard_map/all_to_all | solution.py:150
  58.5 0.9 copy-start.5
  58.5 9.8 %copy-start.22 = (s32[128]{0:T(128)S(1)}, s32[128]{0:T(128)}, u32[]{:S(2)}) copy-start(s32[128]{0:T(128)} %copy-done.21) | copy-start | bytes 1540
  58.5 9.8 %copy-start.11 = (s32[256]{0:T(256)S(1)}, s32[256]{0:T(256)}, u32[]{:S(2)}) copy-start(s32[256]{0:T(256)} %get-tuple-element.2) | copy-start | bytes 3076
  58.5 9.8 %copy-start.18 = (s32[128]{0:T(128)S(1)}, s32[128]{0:T(128)}, u32[]{:S(2)}) copy-start(s32[128]{0:T(128)} %param.20) | copy-start | bytes 1540
  59.4 21.1 %all-to-all-start.2 = ((bf16[128,2,512]{2,1,0:T(2,128)(2,1)}), bf16[128,2,512]{2,1,0:T(2,128)(2,1)S(1)}, u32[]{:S(2)}, u32[]{:S(2)}) async-start(bf16[128,2,512]{2,1,0:T(2,128)(2,1)} %reshape.162), calls=%async_computation.2 | async-start | bytes 524288 | tf_op jit(solution)/shard_map/all_to_all | solution.py:176
  80.6 1.5 copy-start.6
  81.4 4.3 %copy-start.3 = (f32[3,512,128]{2,1,0:T(8,128)S(1)}, f32[3,512,128]{2,1,0:T(8,128)}, u32[]{:S(2)}) copy-start(f32[3,512,128]{2,1,0:T(8,128)} %param.31) | copy-start | bytes 2359300
  82.8 8.8 %copy-start.13 = (f32[4,128]{1,0:T(4,128)S(1)}, f32[4,128]{1,0:T(4,128)}, u32[]{:S(2)}) copy-start(f32[4,128]{1,0:T(4,128)} %param.32) | copy-start | bytes 6148
  83.6 12.8 %collective-permute-start.2 = (bf16[400,512]{1,0:T(8,128)(2,1)}, bf16[400,512]{1,0:T(8,128)(2,1)}, u32[]{:S(2)}, u32[]{:S(2)}) collective-permute-start(bf16[400,512]{1,0:T(8,128)(2,1)} %pad_maximum_fusion), channel_id=1, source_target_pairs={{0,3},{1,0},{2,1},{3,2},{4,7},{5,4},{6,5},{7,6},{8,11},{9,8},{10,9... | collective-permute-start | bytes 1228808 | tf_op jit(solution)/shard_map/ppermute | solution.py:193
  87.6 18.5 %collective-permute-start.1 = (bf16[400,512]{1,0:T(8,128)(2,1)}, bf16[400,512]{1,0:T(8,128)(2,1)}, u32[]{:S(2)}, u32[]{:S(2)}) collective-permute-start(bf16[400,512]{1,0:T(8,128)(2,1)} %pad_maximum_fusion), channel_id=1, source_target_pairs={{0,2},{1,3},{2,0},{3,1},{4,6},{5,7},{6,4},{7,5},{8,10},{9,11},{10,... | collective-permute-start | bytes 1228808 | tf_op jit(solution)/shard_map/ppermute | solution.py:193
  91.9 18.6 %collective-permute-start = (bf16[400,512]{1,0:T(8,128)(2,1)}, bf16[400,512]{1,0:T(8,128)(2,1)S(1)}, u32[]{:S(2)}, u32[]{:S(2)}) collective-permute-start(bf16[400,512]{1,0:T(8,128)(2,1)} %pad_maximum_fusion), channel_id=1, source_target_pairs={{0,1},{1,2},{2,3},{3,0},{4,5},{5,6},{6,7},{7,4},{8,9},{9,10},{10,1... | collective-permute-start | bytes 1228808 | tf_op jit(solution)/shard_map/ppermute | solution.py:193
  115.3 2.5 copy-start.4
  138.4 12.8 %copy-start.20 = (s32[128]{0:T(128)S(1)}, s32[128]{0:T(128)}, u32[]{:S(2)}) copy-start(s32[128]{0:T(128)} %param.23) | copy-start | bytes 1540
  138.4 12.9 %copy-start.8 = (s32[128,16,1]{0,2,1:T(1,128)S(1)}, s32[128,16,1]{0,2,1:T(1,128)}, u32[]{:S(2)}) copy-start(s32[128,16,1]{0,2,1:T(1,128)} %param.24) | copy-start | bytes 24580
  138.4 13.1 %copy-start.10 = (s32[128,16]{0,1:T(8,128)S(1)}, s32[128,16]{0,1:T(8,128)}, u32[]{:S(2)}) copy-start(s32[128,16]{0,1:T(8,128)} %param.26) | copy-start | bytes 24580
  138.4 13.3 %copy-start.14 = (f32[128]{0:T(128)S(1)}, f32[128]{0:T(128)}, u32[]{:S(2)}) copy-start(f32[128]{0:T(128)} %param.28) | copy-start | bytes 1540
  138.4 13.3 %copy-start.15 = (f32[128]{0:T(128)S(1)}, f32[128]{0:T(128)}, u32[]{:S(2)}) copy-start(f32[128]{0:T(128)} %param.27) | copy-start | bytes 1540
  138.5 117.4 %all-to-all-start.3 = ((bf16[128,32,512]{2,1,0:T(8,128)(2,1)}), bf16[128,32,512]{2,1,0:T(8,128)(2,1)}, u32[]{:S(2)}, u32[]{:S(2)}) async-start(bf16[128,32,512]{2,1,0:T(8,128)(2,1)} %bitcast.124), calls=%async_computation.3 | async-start | bytes 8388608 | tf_op jit(solution)/shard_map/all_to_all | solution.py:217
  151.3 6.0 %copy-start.7 = (bf16[512,512]{1,0:T(8,128)(2,1)S(1)}, bf16[512,512]{1,0:T(8,128)(2,1)}, u32[]{:S(2)}) copy-start(bf16[512,512]{1,0:T(8,128)(2,1)} %param.33) | copy-start | bytes 1572868
